TPU v7x, 512 devices: a whole 4x4x16 slice. The times are simulated.
512 devices in a mesh: take: 4 (over y), outer: 16 (over z), inner: 8 (over x, core).
Axes of the slice: x: 4, y: 4, z: 16, core: 2. Of those that a mesh axis runs over, the one named last changes fastest.
Arguments:
- frames: bfloat16 [16, 65536, 256], P('take', ('outer', 'inner')), may hold values from -6 to 6
- conv_weight: bfloat16 [3, 3, 256, 256], replicated, may hold values from -0.21875 to 0.21875
- conv_bias: float32 [3, 256], replicated, may hold values from -1 to 1
- dilations: int32 [3], replicated, may hold values from 1 to 64, as said below
- head_weight: bfloat16 [256, 128], replicated, may hold values from -0.375 to 0.375
- present: int32 [16, 65536], P('take', ('outer', 'inner')), may hold values 0 or 1
- frame_keep: float32 [16, 65536], P('take', ('outer', 'inner')), may hold values from 0.5 to 1
- channel_params: float32 [3, 64], replicated, may hold values from 0 to 2
- head_cotangent: bfloat16 [16, 65536, 128], P('take', ('outer', 'inner')), may hold values from -6 to 6
Outputs:
- filtered_mean: float32 [16, 64, 65536], P('take', None, ('outer', 'inner'))
- head_grad: float32 [256, 128], replicated
Inputs may be any that keep to these rules, and one draw needn't show every extreme that they name: `dilations`: every dilation is 1 to 64; some layer has exactly 64 and another exactly 1.
All inputs are finite; a program needn't handle non-finite values. No bound on the sum of `present` on one device may be relied on, other than what follows from the above.
Results may differ from a plain program's by a relative error of at most 0.0048.
Values may be sent and summed in bfloat16 or wider, within the bound.
No kernel may reach another device: no remote copies, remote signals or barrier semaphores. Data moves between devices by JAX's collectives and lax.ppermute only.
A program may use at most 64 MiB of HBM per device.

v0:
```python
import jax
import jax.numpy as jnp
from jax import lax
from jax.sharding import PartitionSpec as P

STATE = 64
LAYERS = 3
DMAX = 64


def extended_2(block, sides, width):
    for axis, dim in sides:
        count = lax.axis_size(axis)
        forward = [(i, i + 1) for i in range(count - 1)]
        backward = [(target, source) for source, target in forward]
        low = lax.ppermute(
            lax.slice_in_dim(block, block.shape[dim] - width, None, axis=dim), axis, forward
        )
        high = lax.ppermute(lax.slice_in_dim(block, 0, width, axis=dim), axis, backward)
        block = jnp.concatenate([low, block, high], axis=dim)
    return block


def prefix_2(part, axis, combine, identity):
    place = lax.axis_index(axis)
    gathered = jax.tree.map(lambda a: lax.all_gather(a, axis), part)
    state = jax.tree.map(lambda a, e: jnp.zeros_like(a) + jnp.asarray(e, a.dtype), part, identity)

    def one(turn, state):
        return combine(
            state, jax.tree.map(lambda a: lax.dynamic_index_in_dim(a, turn, 0, False), gathered)
        )

    return lax.fori_loop(0, place, one, state)


def combine(early, late):
    a_one, b_one, c_one, e_one, j_one = early
    a_two, b_two, c_two, e_two, j_two = late
    denom = 1.0 + c_one * j_two
    new_a = a_two * a_one / denom
    new_b = a_two * (b_one + c_one * e_two) / denom + b_two
    new_c = a_two * a_two * c_one / denom + c_two
    new_e = a_one * (e_two - j_two * b_one) / denom + e_one
    new_j = a_one * a_one * j_two / denom + j_one
    return (new_a, new_b, new_c, new_e, new_j)


def doubling_prefix(elems, axis):
    length = elems[0].shape[axis]
    result = elems
    offset = 1
    while offset < length:
        moved = []
        for index, item in enumerate(result):
            fill_value = 1.0 if index == 0 else 0.0
            pad_shape = list(item.shape)
            pad_shape[axis] = offset
            fill = jnp.full(pad_shape, fill_value, item.dtype)
            kept = lax.slice_in_dim(item, 0, length - offset, axis=axis)
            moved.append(jnp.concatenate([fill, kept], axis=axis))
        result = combine(tuple(moved), result)
        offset = offset * 2
    return result


def elements(obs, logp, params, present, keep, first):
    rate = params[0][:, None]
    noise = params[1][:, None]
    scale = params[2][:, None]
    trans = jnp.exp(-rate) * keep
    prec = present * scale * jax.nn.softplus(logp)
    denom = 1.0 + noise * prec
    zeros = jnp.zeros_like(obs)
    elem_a = jnp.where(first, zeros, trans / denom)
    elem_b = jnp.where(first, prec * obs / (1.0 + prec), noise * prec * obs / denom)
    elem_c = jnp.where(first, 1.0 / (1.0 + prec), noise / denom)
    elem_e = jnp.where(first, zeros, trans * prec * obs / denom)
    elem_j = jnp.where(first, zeros, trans * trans * prec / denom)
    return (elem_a, elem_b, elem_c, elem_e, elem_j)


def conv_layer(extended, weights, bias, dilation):
    out_len = extended.shape[1] - 2 * DMAX
    acc = jnp.zeros((extended.shape[0], out_len, extended.shape[2]), jnp.float32)
    for tap in range(3):
        piece = lax.dynamic_slice_in_dim(extended, DMAX + (tap - 1) * dilation, out_len, 1)
        acc = acc + jnp.einsum(
            "tfw,wv->tfv", piece, weights[tap], preferred_element_type=jnp.float32
        )
    center = extended[:, DMAX : DMAX + out_len]
    return (center.astype(jnp.float32) + jax.nn.silu(acc + bias[None, None, :])).astype(
        jnp.bfloat16
    )


def per_device(
    frames,
    conv_weight,
    conv_bias,
    dilations,
    head_weight,
    present,
    frame_keep,
    channel_params,
    head_cotangent,
):
    block_len = frames.shape[1]
    position = lax.axis_index(("outer", "inner"))
    hidden = frames
    for layer in range(LAYERS):
        extended = extended_2(hidden, ((("outer", "inner"), 1),), DMAX)
        hidden = conv_layer(extended, conv_weight[layer], conv_bias[layer], dilations[layer])
    head = jnp.einsum("tfw,ws->tsf", hidden, head_weight, preferred_element_type=jnp.float32)
    obs = head[:, :STATE]
    logp = head[:, STATE:]
    places = position * block_len + jnp.arange(block_len, dtype=jnp.int32)
    first = (places == 0)[None, None, :]
    elems = elements(
        obs,
        logp,
        channel_params,
        present.astype(jnp.float32)[:, None, :],
        frame_keep[:, None, :],
        first,
    )
    local = doubling_prefix(elems, 2)
    totals = tuple((item[:, :, -1] for item in local))
    identity = (jnp.ones_like(totals[0]),) + tuple((jnp.zeros_like(item) for item in totals[1:]))
    prefix = prefix_2(totals, ("outer", "inner"), combine, identity)
    final = combine(tuple((item[:, :, None] for item in prefix)), local)
    grad_local = jnp.einsum(
        "tfw,tfs->ws", hidden, head_cotangent, preferred_element_type=jnp.float32
    )
    head_grad = lax.psum(grad_local, ("take", "outer", "inner"))
    return (final[1], head_grad)


def solution(mesh):
    return jax.shard_map(
        per_device,
        mesh=mesh,
        in_specs=(
            P("take", ("outer", "inner"), None),
            P(),
            P(),
            P(),
            P(),
            P("take", ("outer", "inner")),
            P("take", ("outer", "inner")),
            P(),
            P("take", ("outer", "inner"), None),
        ),
        out_specs=(P("take", None, ("outer", "inner")), P()),
        check_vma=False,
    )
```

profile of v0, /device:TPU:487, one launch (start us, length us, event | category | flops | bytes accessed | tf_op | source)
XLA Modules:
  0.0 688.3 jit_solution(7287627464374203176)
XLA Ops:
  7.3 1.1 fusion.92
  8.4 2.6 collective-permute-start.1
  10.9 1.3 collective-permute-start
  13.9 3.0 fusion.65
  24.2 1.1 copy-done.5
  25.3 1.1 add_convert_fusion.2
  26.5 1.3 collective-permute-start.2
  27.8 3.7 collective-permute-start.3
  33.0 1.1 add_convert_fusion.1
  34.1 1.3 collective-permute-start.4
  35.4 6.0 collective-permute-start.5
  42.7 2.0 add_convert_fusion
  44.8 1.1 convolution_bitcast_fusion.1
  46.9 0.8 divide_add_fusion.14
  47.7 1.1 divide_add_fusion.13
  48.8 1.3 divide_add_fusion.12
  50.1 1.3 divide_add_fusion.11
  51.4 1.3 divide_add_fusion.10
  52.7 1.3 divide_add_fusion.9
  54.0 1.3 divide_add_fusion.8
  55.4 1.4 fusion.36
  60.2 119.0 %all-gather.3 = f32[512,64,1]{1,2,0:T(1,128)} all-gather(f32[4,64,1]{1,2,0:T(1,128)S(1)} %copy.19), channel_id=5, replica_groups=mesh['take'=4,'outer'=16,'inner'=8] {'outer','inner'}, dimensions={0}, use_global_device_ids=true | all-gather | bytes 132096 | tf_op jit(solution)/shard_map/all_gather | solution.py:26
  179.2 106.2 %all-gather.4 = f32[512,64,1]{1,2,0:T(1,128)} all-gather(f32[4,64,1]{1,2,0:T(1,128)S(1)} %copy.20), channel_id=6, replica_groups=mesh['take'=4,'outer'=16,'inner'=8] {'outer','inner'}, dimensions={0}, use_global_device_ids=true | all-gather | bytes 132096 | tf_op jit(solution)/shard_map/all_gather | solution.py:26
  285.4 2.4 fusion.44
  288.1 1.1 slice.378
  289.3 1.0 slice.356
  290.4 99.6 %all-gather = f32[512,64,1]{1,2,0:T(1,128)S(1)} all-gather(f32[4,64,1]{1,2,0:T(1,128)S(1)} %copy.16), channel_id=2, replica_groups=mesh['take'=4,'outer'=16,'inner'=8] {'outer','inner'}, dimensions={0}, use_global_device_ids=true | all-gather | bytes 132096 | tf_op jit(solution)/shard_map/all_gather | solution.py:26
  390.0 98.2 %all-gather.2 = f32[512,64,1]{1,2,0:T(1,128)S(1)} all-gather(f32[4,64,1]{1,2,0:T(1,128)S(1)} %copy.18), channel_id=4, replica_groups=mesh['take'=4,'outer'=16,'inner'=8] {'outer','inner'}, dimensions={0}, use_global_device_ids=true | all-gather | bytes 132096 | tf_op jit(solution)/shard_map/all_gather | solution.py:26
  488.2 99.5 %all-gather.1 = f32[512,64,1]{1,2,0:T(1,128)S(1)} all-gather(f32[4,64,1]{1,2,0:T(1,128)S(1)} %copy.17), channel_id=3, replica_groups=mesh['take'=4,'outer'=16,'inner'=8] {'outer','inner'}, dimensions={0}, use_global_device_ids=true | all-gather | bytes 132096 | tf_op jit(solution)/shard_map/all_gather | solution.py:26
  587.7 91.1 %while.17 = (s32[]{:T(128)}, f32[4,64]{1,0:T(4,128)S(1)}, f32[4,64]{1,0:T(4,128)S(1)}, s32[]{:T(128)}, f32[128,4,64]{2,1,0:T(4,128)S(1)}, /*index=5*/f32[128,4,6...) while((s32[]{:T(128)}, f32[4,64]{1,0:T(4,128)S(1)}, ...), condition=%wide.region_1.2_spmd, body=%wide.region_0.1_spmd.sunk | while | flops 2821 | bytes 9379 | solution.py:34
  678.8 1.0 divide_add_fusion
  679.9 1.6 copy.37
  (198 shorter events, 99.5 us)
Async XLA Ops:
  7.2 37.6 %copy-start = (bf16[4,512,128]{2,1,0:T(8,128)(2,1)S(1)}, bf16[4,512,128]{2,1,0:T(8,128)(2,1)}, u32[]{:S(2)}) copy-start(bf16[4,512,128]{2,1,0:T(8,128)(2,1)} %param.19) | copy-start | bytes 1572868
  7.2 16.5 %copy-start.1 = (bf16[4,512,256]{2,1,0:T(8,128)(2,1)S(1)}, bf16[4,512,256]{2,1,0:T(8,128)(2,1)}, u32[]{:S(2)}) copy-start(bf16[4,512,256]{2,1,0:T(8,128)(2,1)} %param.11) | copy-start | bytes 3145732
  7.2 9.7 %copy-start.10 = (s32[3]{0:T(128)S(1)}, s32[3]{0:T(128)}, u32[]{:S(2)}) copy-start(s32[3]{0:T(128)} %param.14) | copy-start | bytes 40
  7.2 16.3 %copy-start.9 = (s32[4,512]{1,0:T(4,128)S(1)}, s32[4,512]{1,0:T(4,128)}, u32[]{:S(2)}) copy-start(s32[4,512]{1,0:T(4,128)} %param.16) | copy-start | bytes 24580
  7.2 672.6 %all-reduce.47.cloned.1.call-start = ((), (), s32[]{:S(2)}) async-start(), calls=%async_computation | async-start | bytes 262144 | tf_op jit(solution)/shard_map/psum | solution.py:135
  8.4 15.4 %collective-permute-start.1 = (bf16[4,64,256]{2,1,0:T(8,128)(2,1)S(1)}, bf16[4,64,256]{2,1,0:T(8,128)(2,1)S(1)}, u32[]{:S(2)}, u32[]{:S(2)}) collective-permute-start(bf16[4,64,256]{2,1,0:T(8,128)(2,1)S(1)} %get-tuple-element.198), channel_id=1, source_target_pairs={{1,0},{2,1},{3,2},{4,3},{5,4},{6,5},{7,6},{8,7},{9,8},{10,9},{11,1... | collective-permute-start | bytes 393224 | tf_op jit(solution)/shard_map/ppermute | solution.py:19
  10.9 12.7 %collective-permute-start = (bf16[4,64,256]{2,1,0:T(8,128)(2,1)S(1)}, bf16[4,64,256]{2,1,0:T(8,128)(2,1)S(1)}, u32[]{:S(2)}, u32[]{:S(2)}) collective-permute-start(bf16[4,64,256]{2,1,0:T(8,128)(2,1)S(1)} %get-tuple-element.199), channel_id=1, source_target_pairs={{0,1},{1,2},{2,3},{3,4},{4,5},{5,6},{6,7},{7,8},{8,9},{9,10},{10,1... | collective-permute-start | bytes 393224 | tf_op jit(solution)/shard_map/ppermute | solution.py:16
  16.9 6.9 %copy-start.6 = (bf16[3,3,256,256]{3,2,1,0:T(8,128)(2,1)S(1)}, bf16[3,3,256,256]{3,2,1,0:T(8,128)(2,1)}, u32[]{:S(2)}) copy-start(bf16[3,3,256,256]{3,2,1,0:T(8,128)(2,1)} %param.12) | copy-start | bytes 3538948
  23.7 1.6 copy-start.5
  26.5 5.4 collective-permute-start.2
  27.8 4.6 collective-permute-start.3
  34.1 7.7 %collective-permute-start.4 = (bf16[4,64,256]{2,1,0:T(8,128)(2,1)S(1)}, bf16[4,64,256]{2,1,0:T(8,128)(2,1)S(1)}, u32[]{:S(2)}, u32[]{:S(2)}) collective-permute-start(bf16[4,64,256]{2,1,0:T(8,128)(2,1)S(1)} %get-tuple-element.194), channel_id=1, source_target_pairs={{0,1},{1,2},{2,3},{3,4},{4,5},{5,6},{6,7},{7,8},{8,9},{9,10},{10,1... | collective-permute-start | bytes 393224 | tf_op jit(solution)/shard_map/ppermute | solution.py:16
  35.4 6.8 collective-permute-start.5
  42.7 3.2 copy-start.7
  45.9 1.0 copy-start.8
  57.7 1.3 copy-start.4
  287.9 390.9 %copy-start.2 = (f32[4,64,512]{2,1,0:T(8,128)S(1)}, f32[4,64,512]{2,1,0:T(8,128)}, u32[]{:S(2)}) copy-start(f32[4,64,512]{2,1,0:T(8,128)} %get-tuple-element.192) | copy-start | bytes 1572868
  287.9 391.0 %copy-start.3 = (f32[4,64,512]{2,1,0:T(8,128)S(1)}, f32[4,64,512]{2,1,0:T(8,128)}, u32[]{:S(2)}) copy-start(f32[4,64,512]{2,1,0:T(8,128)} %get-tuple-element.193) | copy-start | bytes 1572868
Sparse Core Ops, SparseCore 0:
  46.5 462.9 all-reduce.46
where the time goes:
time: 694 us; the launch traced here: 688 us
  blocking collectives  523 us (75%)
  other arithmetic  105 us (15%)
  between operations  20.5 us (3%)
  starting transfers between devices  16.2 us (2%)
  matrix products  11.1 us (2%)
  local copies, waits for them, and re-layouts  9.94 us (1%)
    all_gather x5, blocking collectives, prefix_2(): gathered = jax.tree.map(lambda a: lax.all_gather(a, axis), part)  523 us
    add x136, other arithmetic, combine(): new_c = a_two * a_two * c_one / denom + c_two  99 us
  transfers between devices with their start and end apart: 7, of which 2 were waited for; matrix products, arithmetic and copies ran while one was open for 17% of the time, Pallas kernels for 0%

commit v1 on v0

--- a/solution.py
+++ b/solution.py
@@ -64,6 +64,23 @@
     return result
 
 
+def exclusive_in_group(totals, axis):
+    place = lax.axis_index(axis)
+    gathered = lax.all_gather(totals, axis)
+    inclusive = doubling_prefix(tuple(gathered[:, k] for k in range(5)), 0)
+    inclusive = jnp.stack(inclusive, axis=1)
+    earlier = lax.dynamic_index_in_dim(inclusive, jnp.maximum(place - 1, 0), 0, False)
+    identity = jnp.zeros_like(earlier).at[0].set(1.0)
+    earlier = jnp.where(place > 0, earlier, identity)
+    return earlier, inclusive[-1]
+
+
+def block_prefix(totals):
+    inner_excl, group_total = exclusive_in_group(totals, "inner")
+    outer_excl, _ = exclusive_in_group(group_total, "outer")
+    return combine(tuple(outer_excl), tuple(inner_excl))
+
+
 def elements(obs, logp, params, present, keep, first):
     rate = params[0][:, None]
     noise = params[1][:, None]
@@ -125,14 +142,15 @@
         first,
     )
     local = doubling_prefix(elems, 2)
-    totals = tuple((item[:, :, -1] for item in local))
-    identity = (jnp.ones_like(totals[0]),) + tuple((jnp.zeros_like(item) for item in totals[1:]))
-    prefix = prefix_2(totals, ("outer", "inner"), combine, identity)
+    totals = jnp.stack([item[:, :, -1] for item in local])
+    prefix = block_prefix(totals)
     final = combine(tuple((item[:, :, None] for item in prefix)), local)
     grad_local = jnp.einsum(
         "tfw,tfs->ws", hidden, head_cotangent, preferred_element_type=jnp.float32
     )
-    head_grad = lax.psum(grad_local, ("take", "outer", "inner"))
+    head_grad = lax.psum(grad_local, "inner")
+    head_grad = lax.psum(head_grad, "outer")
+    head_grad = lax.psum(head_grad, "take")
     return (final[1], head_grad)
 
 

time: 694 us -> 393 us (0.57)
  the two profiles are of different devices: /device:TPU:487 before, /device:TPU:1 now
where the time goes in v1:
time: 393 us; the launch traced here: 392 us
  waiting for transfers between devices  274 us (70%)
  blocking collectives  46.1 us (12%)
  between operations  20.5 us (5%)
  starting transfers between devices  19.6 us (5%)
  other arithmetic  14.9 us (4%)
  matrix products  10.2 us (3%)
  local copies, waits for them, and re-layouts  6.28 us (2%)
    psum x1, waiting for transfers between devices, per_device(): head_grad = lax.psum(head_grad, 'outer')  130 us
    psum x1, waiting for transfers between devices, per_device(): head_grad = lax.psum(grad_local, 'inner')  75 us
    psum x1, waiting for transfers between devices, per_device(): head_grad = lax.psum(head_grad, 'take')  62.3 us
    all_gather x2, blocking collectives, exclusive_in_group(): gathered = lax.all_gather(totals, axis)  46.1 us
    ppermute x3, starting transfers between devices, extended_2(): lax.ppermute(lax.slice_in_dim(block, 0, width, axis=dim), axis, backward)  13.7 us
    add x13, other arithmetic, combine(): new_c = a_two * a_two * c_one / denom + c_two  9.96 us
    dot_general x9, matrix products, conv_layer(): jnp.einsum('tfw,wv->tfv', piece, weights[tap], preferred_element_type=jnp...  8.62 us
  transfers between devices with their start and end apart: 9, of which 5 were waited for; matrix products, arithmetic and copies ran while one was open for 2% of the time, Pallas kernels for 0%

profile of v1, /device:TPU:1, one launch (start us, length us, event | category | flops | bytes accessed | tf_op | source)
XLA Modules:
  0.0 391.6 jit_solution(5290036489453492107)
XLA Ops:
  7.3 1.1 fusion.141
  8.4 8.7 %collective-permute-start.1 = (bf16[4,64,256]{2,1,0:T(8,128)(2,1)S(1)}, bf16[4,64,256]{2,1,0:T(8,128)(2,1)S(1)}, u32[]{:S(2)}, u32[]{:S(2)}) collective-permute-start(bf16[4,64,256]{2,1,0:T(8,128)(2,1)S(1)} %get-tuple-element.109), channel_id=1, source_target_pairs={{1,0},{2,1},{3,2},{4,3},{5,4},{6,5},{7,6},{8,7},{9,8},{10,9},{11,1... | collective-permute-start | bytes 393224 | tf_op jit(solution)/shard_map/ppermute | solution.py:19
  17.1 1.9 collective-permute-start
  19.0 0.8 exponential_bitcast_fusion
  19.8 0.8 fusion.142
  20.6 3.0 fusion.60
  31.0 1.1 copy-done.2
  32.1 1.1 add_convert_fusion.2
  33.3 1.9 collective-permute-start.2
  35.2 2.4 collective-permute-start.3
  38.1 3.4 collective-permute-done.3
  42.0 1.1 add_convert_fusion.1
  43.2 1.9 collective-permute-start.4
  45.1 2.6 collective-permute-start.5
  48.1 3.2 collective-permute-done.5
  51.9 1.1 add_convert_fusion
  54.1 0.8 divide_add_fusion.14
  54.9 1.1 divide_add_fusion.13
  56.0 1.3 divide_add_fusion.12
  57.3 1.3 divide_add_fusion.11
  58.6 1.3 divide_add_fusion.10
  59.9 1.3 divide_add_fusion.9
  61.2 1.3 divide_add_fusion.8
  62.6 1.4 fusion.30
  66.6 14.7 %all-gather = f32[40,4,64]{2,1,0:T(4,128)S(1)} all-gather(f32[5,4,64]{2,1,0:T(4,128)S(1)} %constant_dynamic-update-slice_fusion.3), channel_id=2, replica_groups=mesh['take'=4,'outer'=16,'inner'=8] {'inner'}, dimensions={0}, use_global_device_ids=true | all-gather | bytes 46080 | tf_op jit(solution)/shard_map/all_gather | solution.py:69
  81.8 31.4 %all_gather.11 = f32[16,5,4,64]{3,2,0,1:T(4,128)S(1)} all-gather(f32[1,5,4,64]{3,2,0,1:T(4,128)S(1)} %slice.674), channel_id=1, replica_groups=mesh['take'=4,'outer'=16,'inner'=8] {'outer'}, dimensions={0}, use_global_device_ids=true | all-gather | bytes 87040 | tf_op jit(solution)/shard_map/all_gather | solution.py:69
  113.4 1.1 convolution_bitcast_fusion.1
  115.2 75.0 %all-reduce.84.cloned.1.call-done = f32[256,128]{1,0:T(8,128)} async-done(((f32[256,128]{1,0:T(8,128)}), f32[256,128]{1,0:T(8,128)}) %all-reduce.84.cloned.1.call-update) | async-done | bytes 131088 | tf_op jit(solution)/shard_map/psum | solution.py:151
  190.3 129.9 %all-reduce.86.cloned.1.call-done = f32[256,128]{1,0:T(8,128)} async-done(((f32[256,128]{1,0:T(8,128)}), f32[256,128]{1,0:T(8,128)}) %all-reduce.86.cloned.1.call-update) | async-done | bytes 131088 | tf_op jit(solution)/shard_map/psum | solution.py:152
  320.2 1.0 divide_add_fusion
  321.2 62.3 %all-reduce.88.cloned.1.call-done = f32[256,128]{1,0:T(8,128)} async-done(((f32[256,128]{1,0:T(8,128)}), f32[256,128]{1,0:T(8,128)}) %all-reduce.88.cloned.1.call-update) | async-done | bytes 131088 | tf_op jit(solution)/shard_map/psum | solution.py:153
  383.5 1.6 copy.267
  (113 shorter events, 7.9 us)
Async XLA Ops:
  7.2 106.3 %copy-start = (bf16[4,512,128]{2,1,0:T(8,128)(2,1)S(1)}, bf16[4,512,128]{2,1,0:T(8,128)(2,1)}, u32[]{:S(2)}) copy-start(bf16[4,512,128]{2,1,0:T(8,128)(2,1)} %param.21) | copy-start | bytes 1572868
  7.2 23.2 %copy-start.1 = (bf16[4,512,256]{2,1,0:T(8,128)(2,1)S(1)}, bf16[4,512,256]{2,1,0:T(8,128)(2,1)}, u32[]{:S(2)}) copy-start(bf16[4,512,256]{2,1,0:T(8,128)(2,1)} %param.13) | copy-start | bytes 3145732
  7.2 16.5 %copy-start.8 = (s32[3]{0:T(128)S(1)}, s32[3]{0:T(128)}, u32[]{:S(2)}) copy-start(s32[3]{0:T(128)} %param.16) | copy-start | bytes 40
  7.2 23.1 %copy-start.7 = (s32[4,512]{1,0:T(4,128)S(1)}, s32[4,512]{1,0:T(4,128)}, u32[]{:S(2)}) copy-start(s32[4,512]{1,0:T(4,128)} %param.18) | copy-start | bytes 24580
  7.2 183.0 %all-reduce.84.cloned.1.call-start = ((), (), s32[]{:S(2)}) async-start(), calls=%async_computation | async-start | bytes 262144 | tf_op jit(solution)/shard_map/psum | solution.py:151
  8.4 22.2 %collective-permute-start.1 = (bf16[4,64,256]{2,1,0:T(8,128)(2,1)S(1)}, bf16[4,64,256]{2,1,0:T(8,128)(2,1)S(1)}, u32[]{:S(2)}, u32[]{:S(2)}) collective-permute-start(bf16[4,64,256]{2,1,0:T(8,128)(2,1)S(1)} %get-tuple-element.109), channel_id=1, source_target_pairs={{1,0},{2,1},{3,2},{4,3},{5,4},{6,5},{7,6},{8,7},{9,8},{10,9},{11,1... | collective-permute-start | bytes 393224 | tf_op jit(solution)/shard_map/ppermute | solution.py:19
  17.1 13.3 %collective-permute-start = (bf16[4,64,256]{2,1,0:T(8,128)(2,1)S(1)}, bf16[4,64,256]{2,1,0:T(8,128)(2,1)S(1)}, u32[]{:S(2)}, u32[]{:S(2)}) collective-permute-start(bf16[4,64,256]{2,1,0:T(8,128)(2,1)S(1)} %get-tuple-element.110), channel_id=1, source_target_pairs={{0,1},{1,2},{2,3},{3,4},{4,5},{5,6},{6,7},{7,8},{8,9},{9,10},{10,1... | collective-permute-start | bytes 393224 | tf_op jit(solution)/shard_map/ppermute | solution.py:16
  23.7 6.9 %copy-start.3 = (bf16[3,3,256,256]{3,2,1,0:T(8,128)(2,1)S(1)}, bf16[3,3,256,256]{3,2,1,0:T(8,128)(2,1)}, u32[]{:S(2)}) copy-start(bf16[3,3,256,256]{3,2,1,0:T(8,128)(2,1)} %param.14) | copy-start | bytes 3538948
  30.5 1.6 copy-start.2
  33.3 4.8 %collective-permute-start.2 = (bf16[4,64,256]{2,1,0:T(8,128)(2,1)S(1)}, bf16[4,64,256]{2,1,0:T(8,128)(2,1)S(1)}, u32[]{:S(2)}, u32[]{:S(2)}) collective-permute-start(bf16[4,64,256]{2,1,0:T(8,128)(2,1)S(1)} %get-tuple-element.107), channel_id=1, source_target_pairs={{0,1},{1,2},{2,3},{3,4},{4,5},{5,6},{6,7},{7,8},{8,9},{9,10},{10,1... | collective-permute-start | bytes 393224 | tf_op jit(solution)/shard_map/ppermute | solution.py:16
  35.2 6.3 %collective-permute-start.3 = (bf16[4,64,256]{2,1,0:T(8,128)(2,1)S(1)}, bf16[4,64,256]{2,1,0:T(8,128)(2,1)S(1)}, u32[]{:S(2)}, u32[]{:S(2)}) collective-permute-start(bf16[4,64,256]{2,1,0:T(8,128)(2,1)S(1)} %get-tuple-element.108), channel_id=1, source_target_pairs={{1,0},{2,1},{3,2},{4,3},{5,4},{6,5},{7,6},{8,7},{9,8},{10,9},{11,1... | collective-permute-start | bytes 393224 | tf_op jit(solution)/shard_map/ppermute | solution.py:19
  43.2 5.0 %collective-permute-start.4 = (bf16[4,64,256]{2,1,0:T(8,128)(2,1)S(1)}, bf16[4,64,256]{2,1,0:T(8,128)(2,1)S(1)}, u32[]{:S(2)}, u32[]{:S(2)}) collective-permute-start(bf16[4,64,256]{2,1,0:T(8,128)(2,1)S(1)} %get-tuple-element.105), channel_id=1, source_target_pairs={{0,1},{1,2},{2,3},{3,4},{4,5},{5,6},{6,7},{7,8},{8,9},{9,10},{10,1... | collective-permute-start | bytes 393224 | tf_op jit(solution)/shard_map/ppermute | solution.py:16
  45.1 6.3 %collective-permute-start.5 = (bf16[4,64,256]{2,1,0:T(8,128)(2,1)S(1)}, bf16[4,64,256]{2,1,0:T(8,128)(2,1)S(1)}, u32[]{:S(2)}, u32[]{:S(2)}) collective-permute-start(bf16[4,64,256]{2,1,0:T(8,128)(2,1)S(1)} %get-tuple-element.106), channel_id=1, source_target_pairs={{1,0},{2,1},{3,2},{4,3},{5,4},{6,5},{7,6},{8,7},{9,8},{10,9},{11,1... | collective-permute-start | bytes 393224 | tf_op jit(solution)/shard_map/ppermute | solution.py:19
  51.9 1.2 copy-start.4
  53.1 0.9 copy-start.5
  113.4 1.8 copy-start.6
  114.6 205.6 %all-reduce.86.cloned.1.call-start = ((), (), s32[]{:S(2)}) async-start(), calls=%async_computation.1 | async-start | bytes 262144 | tf_op jit(solution)/shard_map/psum | solution.py:152
  190.2 193.3 %all-reduce.88.cloned.1.call-start = ((), (), s32[]{:S(2)}) async-start(), calls=%async_computation.2 | async-start | bytes 262144 | tf_op jit(solution)/shard_map/psum | solution.py:153
Sparse Core Ops, SparseCore 0:
  114.7 75.3 all-reduce.83
  192.5 127.6 all-reduce.85
  322.5 61.0 all-reduce.87

commit v2 on v0

--- a/solution.py
+++ b/solution.py
@@ -64,6 +64,34 @@
     return result
 
 
+def butterfly_sum(value, axis):
+    count = lax.axis_size(axis)
+    step = 1
+    while step < count:
+        pairs = [(i, i ^ step) for i in range(count)]
+        value = value + lax.ppermute(value, axis, pairs)
+        step = step * 2
+    return value
+
+
+def block_prefix(totals, axis):
+    count = lax.axis_size(axis)
+    place = lax.axis_index(axis)
+    identity = jnp.zeros_like(totals).at[0].set(1.0)
+
+    def shifted(value, step):
+        pairs = [(i, i + step) for i in range(count - step)]
+        return lax.ppermute(value, axis, pairs)
+
+    running = jnp.where(place >= 1, shifted(totals, 1), identity)
+    step = 1
+    while step < count:
+        early = shifted(running, step)
+        joined = jnp.stack(combine(tuple(early), tuple(running)))
+        running = jnp.where(place >= step, joined, running)
+        step = step * 2
+    return running
+
 def elements(obs, logp, params, present, keep, first):
     rate = params[0][:, None]
     noise = params[1][:, None]
@@ -125,14 +153,15 @@
         first,
     )
     local = doubling_prefix(elems, 2)
-    totals = tuple((item[:, :, -1] for item in local))
-    identity = (jnp.ones_like(totals[0]),) + tuple((jnp.zeros_like(item) for item in totals[1:]))
-    prefix = prefix_2(totals, ("outer", "inner"), combine, identity)
+    totals = jnp.stack([item[:, :, -1] for item in local])
+    prefix = block_prefix(totals, ("outer", "inner"))
     final = combine(tuple((item[:, :, None] for item in prefix)), local)
     grad_local = jnp.einsum(
         "tfw,tfs->ws", hidden, head_cotangent, preferred_element_type=jnp.float32
     )
-    head_grad = lax.psum(grad_local, ("take", "outer", "inner"))
+    head_grad = butterfly_sum(grad_local, "inner")
+    head_grad = butterfly_sum(head_grad, "outer")
+    head_grad = butterfly_sum(head_grad, "take")
     return (final[1], head_grad)
 
 

time: 694 us -> 222 us (0.32)
  the two profiles are of different devices: /device:TPU:487 before, /device:TPU:8 now
where the time goes in v2:
time: 222 us; the launch traced here: 221 us
  starting transfers between devices  119 us (54%)
  waiting for transfers between devices  66 us (30%)
  other arithmetic  14.5 us (7%)
  matrix products  9.51 us (4%)
  between operations  7.32 us (3%)
  local copies, waits for them, and re-layouts  4.56 us (2%)
    ppermute x8, starting transfers between devices, shifted(): return lax.ppermute(value, axis, pairs)  76 us
    ppermute x9, waiting for transfers between devices, butterfly_sum(): value = value + lax.ppermute(value, axis, pairs)  54.8 us
    ppermute x9, starting transfers between devices, butterfly_sum(): value = value + lax.ppermute(value, axis, pairs)  27.3 us
    ppermute x3, starting transfers between devices, extended_2(): lax.ppermute(lax.slice_in_dim(block, block.shape[dim] - width, None, axis...  11.5 us
    add x8, other arithmetic, combine(): new_c = a_two * a_two * c_one / denom + c_two  9.8 us
    dot_general x9, matrix products, conv_layer(): jnp.einsum('tfw,wv->tfv', piece, weights[tap], preferred_element_type=jnp...  8.56 us
    ppermute x8, waiting for transfers between devices, shifted(): return lax.ppermute(value, axis, pairs)  7.07 us
  transfers between devices with their start and end apart: 23, of which 16 were waited for; matrix products, arithmetic and copies ran while one was open for 3% of the time, Pallas kernels for 0%

profile of v2, /device:TPU:8, one launch (start us, length us, event | category | flops | bytes accessed | tf_op | source)
XLA Modules:
  0.0 220.8 jit_solution(12863108212357909023)
XLA Ops:
  1.8 1.7 collective-permute-start
  5.7 3.0 %fusion.60 = f32[4,512,256]{2,1,0:T(8,128)} fusion(bf16[4,512,256]{2,1,0:T(8,128)(2,1)} %param.11, bf16[3,3,256,256]{3,2,1,0:T(8,128)(2,1)} %param.12), kind=kOutput, calls=%fused_computation.134 | convolution fusion | flops 268435456 | bytes 3276800 | tf_op jit(solution)/shard_map/tfw,wv->tfv/dot_general | solution.py:116
  18.0 4.3 %collective-permute-start.2 = (bf16[4,64,256]{2,1,0:T(8,128)(2,1)S(1)}, bf16[4,64,256]{2,1,0:T(8,128)(2,1)S(1)}, u32[]{:S(2)}, u32[]{:S(2)}) collective-permute-start(bf16[4,64,256]{2,1,0:T(8,128)(2,1)S(1)} %get-tuple-element.93), channel_id=1, source_target_pairs={{0,1},{1,2},{2,3},{3,4},{4,5},{5,6},{6,7},{7,8},{8,9},{9,10},{10,1... | collective-permute-start | bytes 393224 | tf_op jit(solution)/shard_map/ppermute | solution.py:16
  24.1 2.7 %collective-permute-done.3 = bf16[4,64,256]{2,1,0:T(8,128)(2,1)S(1)} collective-permute-done((bf16[4,64,256]{2,1,0:T(8,128)(2,1)S(1)}, bf16[4,64,256]{2,1,0:T(8,128)(2,1)S(1)}, u32[]{:S(2)}, u32[]{:S(2)}) %collective-permute-start.3) | collective-permute-done | bytes 131104 | tf_op jit(solution)/shard_map/ppermute | solution.py:19
  28.5 5.5 %collective-permute-start.4 = (bf16[4,64,256]{2,1,0:T(8,128)(2,1)S(1)}, bf16[4,64,256]{2,1,0:T(8,128)(2,1)S(1)}, u32[]{:S(2)}, u32[]{:S(2)}) collective-permute-start(bf16[4,64,256]{2,1,0:T(8,128)(2,1)S(1)} %get-tuple-element.91), channel_id=1, source_target_pairs={{0,1},{1,2},{2,3},{3,4},{4,5},{5,6},{6,7},{7,8},{8,9},{9,10},{10,1... | collective-permute-start | bytes 393224 | tf_op jit(solution)/shard_map/ppermute | solution.py:16
  34.0 1.5 collective-permute-start.5
  48.3 1.4 fusion.30
  52.4 5.0 %collective-permute-start.6 = (f32[5,4,64]{2,1,0:T(4,128)S(1)}, f32[5,4,64]{2,1,0:T(4,128)S(1)}, u32[]{:S(2)}, u32[]{:S(2)}) collective-permute-start(f32[5,4,64]{2,1,0:T(4,128)S(1)} %constant_dynamic-update-slice_fusion.3), channel_id=1, source_target_pairs={{0,1},{1,2},{2,3},{3,4},{4,5},{5,6},{6,7},{7,8},{8,9},{9,10},{10,1... | collective-permute-start | bytes 15368 | tf_op jit(solution)/shard_map/ppermute | solution.py:84
  58.2 2.3 %collective-permute-start.7 = (f32[5,4,64]{2,1,0:T(4,128)S(1)}, f32[5,4,64]{2,1,0:T(4,128)S(1)}, u32[]{:S(2)}, u32[]{:S(2)}) collective-permute-start(f32[5,4,64]{2,1,0:T(4,128)S(1)} %broadcast_select_fusion.1), channel_id=1, source_target_pairs={{0,1},{1,2},{2,3},{3,4},{4,5},{5,6},{6,7},{7,8},{8,9},{9,10},{10,1... | collective-permute-start | bytes 15368 | tf_op jit(solution)/shard_map/ppermute | solution.py:84
  61.3 6.0 %collective-permute-start.8 = (f32[5,4,64]{2,1,0:T(4,128)S(1)}, f32[5,4,64]{2,1,0:T(4,128)S(1)}, u32[]{:S(2)}, u32[]{:S(2)}) collective-permute-start(f32[5,4,64]{2,1,0:T(4,128)S(1)} %broadcast_select_fusion), channel_id=1, source_target_pairs={{0,2},{1,3},{2,4},{3,5},{4,6},{5,7},{6,8},{7,9},{8,10},{9,11},{10,... | collective-permute-start | bytes 15368 | tf_op jit(solution)/shard_map/ppermute | solution.py:84
  68.8 10.6 %collective-permute-start.9 = (f32[5,4,64]{2,1,0:T(4,128)S(1)}, f32[5,4,64]{2,1,0:T(4,128)S(1)}, u32[]{:S(2)}, u32[]{:S(2)}) collective-permute-start(f32[5,4,64]{2,1,0:T(4,128)S(1)} %broadcast_select_fusion.2), channel_id=1, source_target_pairs={{0,4},{1,5},{2,6},{3,7},{4,8},{5,9},{6,10},{7,11},{8,12},{9,13},{1... | collective-permute-start | bytes 15368 | tf_op jit(solution)/shard_map/ppermute | solution.py:84
  80.9 13.3 %collective-permute-start.10 = (f32[5,4,64]{2,1,0:T(4,128)S(1)}, f32[5,4,64]{2,1,0:T(4,128)S(1)}, u32[]{:S(2)}, u32[]{:S(2)}) collective-permute-start(f32[5,4,64]{2,1,0:T(4,128)S(1)} %broadcast_select_fusion.3), channel_id=1, source_target_pairs={{0,8},{1,9},{2,10},{3,11},{4,12},{5,13},{6,14},{7,15},{8,16},{9,17... | collective-permute-start | bytes 15368 | tf_op jit(solution)/shard_map/ppermute | solution.py:84
  95.6 5.5 %collective-permute-start.11 = (f32[5,4,64]{2,1,0:T(4,128)S(1)}, f32[5,4,64]{2,1,0:T(4,128)S(1)}, u32[]{:S(2)}, u32[]{:S(2)}) collective-permute-start(f32[5,4,64]{2,1,0:T(4,128)S(1)} %broadcast_select_fusion.4), channel_id=1, source_target_pairs={{0,16},{1,17},{2,18},{3,19},{4,20},{5,21},{6,22},{7,23},{8,24},{9,... | collective-permute-start | bytes 15368 | tf_op jit(solution)/shard_map/ppermute | solution.py:84
  102.6 19.9 %collective-permute-start.12 = (f32[5,4,64]{2,1,0:T(4,128)S(1)}, f32[5,4,64]{2,1,0:T(4,128)S(1)}, u32[]{:S(2)}, u32[]{:S(2)}) collective-permute-start(f32[5,4,64]{2,1,0:T(4,128)S(1)} %broadcast_select_fusion.5), channel_id=1, source_target_pairs={{0,32},{1,33},{2,34},{3,35},{4,36},{5,37},{6,38},{7,39},{8,40},{9,... | collective-permute-start | bytes 15368 | tf_op jit(solution)/shard_map/ppermute | solution.py:84
  123.0 2.1 collective-permute-start.14
  125.2 13.5 %collective-permute-start.13 = (f32[5,4,64]{2,1,0:T(4,128)S(1)}, f32[5,4,64]{2,1,0:T(4,128)S(1)}, u32[]{:S(2)}, u32[]{:S(2)}) collective-permute-start(f32[5,4,64]{2,1,0:T(4,128)S(1)} %broadcast_select_fusion.6), channel_id=1, source_target_pairs={{0,64},{1,65},{2,66},{3,67},{4,68},{5,69},{6,70},{7,71},{8,72},{9,... | collective-permute-start | bytes 15368 | tf_op jit(solution)/shard_map/ppermute | solution.py:84
  138.7 1.9 collective-permute-start.15
  140.7 5.4 %collective-permute-done.15 = f32[256,128]{1,0:T(8,128)S(1)} collective-permute-done((f32[256,128]{1,0:T(8,128)S(1)}, f32[256,128]{1,0:T(8,128)S(1)}, u32[]{:S(2)}, u32[]{:S(2)}) %collective-permute-start.15) | collective-permute-done | bytes 131104 | tf_op jit(solution)/shard_map/ppermute | solution.py:72
  146.1 1.9 collective-permute-start.16
  148.0 6.4 %collective-permute-done.16 = f32[256,128]{1,0:T(8,128)S(1)} collective-permute-done((f32[256,128]{1,0:T(8,128)S(1)}, f32[256,128]{1,0:T(8,128)S(1)}, u32[]{:S(2)}, u32[]{:S(2)}) %collective-permute-start.16) | collective-permute-done | bytes 131104 | tf_op jit(solution)/shard_map/ppermute | solution.py:72
  154.4 1.9 collective-permute-start.17
  156.4 5.0 %collective-permute-done.17 = f32[256,128]{1,0:T(8,128)S(1)} collective-permute-done((f32[256,128]{1,0:T(8,128)S(1)}, f32[256,128]{1,0:T(8,128)S(1)}, u32[]{:S(2)}, u32[]{:S(2)}) %collective-permute-start.17) | collective-permute-done | bytes 131104 | tf_op jit(solution)/shard_map/ppermute | solution.py:72
  161.4 1.9 collective-permute-start.18
  163.4 7.3 %collective-permute-done.18 = f32[256,128]{1,0:T(8,128)S(1)} collective-permute-done((f32[256,128]{1,0:T(8,128)S(1)}, f32[256,128]{1,0:T(8,128)S(1)}, u32[]{:S(2)}, u32[]{:S(2)}) %collective-permute-start.18) | collective-permute-done | bytes 131104 | tf_op jit(solution)/shard_map/ppermute | solution.py:72
  170.7 5.8 %collective-permute-start.19 = (f32[256,128]{1,0:T(8,128)S(1)}, f32[256,128]{1,0:T(8,128)S(1)}, u32[]{:S(2)}, u32[]{:S(2)}) collective-permute-start(f32[256,128]{1,0:T(8,128)S(1)} %add.825), channel_id=1, source_target_pairs={{0,32},{8,40},{16,48},{24,56},{32,0},{40,8},{48,16},{56,24},{64,96... | collective-permute-start | bytes 393224 | tf_op jit(solution)/shard_map/ppermute | solution.py:72
  176.6 12.7 %collective-permute-done.19 = f32[256,128]{1,0:T(8,128)S(1)} collective-permute-done((f32[256,128]{1,0:T(8,128)S(1)}, f32[256,128]{1,0:T(8,128)S(1)}, u32[]{:S(2)}, u32[]{:S(2)}) %collective-permute-start.19) | collective-permute-done | bytes 131104 | tf_op jit(solution)/shard_map/ppermute | solution.py:72
  189.3 5.1 %collective-permute-start.20 = (f32[256,128]{1,0:T(8,128)S(1)}, f32[256,128]{1,0:T(8,128)S(1)}, u32[]{:S(2)}, u32[]{:S(2)}) collective-permute-start(f32[256,128]{1,0:T(8,128)S(1)} %add.826), channel_id=1, source_target_pairs={{0,64},{8,72},{16,80},{24,88},{32,96},{40,104},{48,112},{56,120},{... | collective-permute-start | bytes 393224 | tf_op jit(solution)/shard_map/ppermute | solution.py:72
  194.4 10.4 %collective-permute-done.20 = f32[256,128]{1,0:T(8,128)S(1)} collective-permute-done((f32[256,128]{1,0:T(8,128)S(1)}, f32[256,128]{1,0:T(8,128)S(1)}, u32[]{:S(2)}, u32[]{:S(2)}) %collective-permute-start.20) | collective-permute-done | bytes 131104 | tf_op jit(solution)/shard_map/ppermute | solution.py:72
  204.9 2.4 %collective-permute-start.21 = (f32[256,128]{1,0:T(8,128)S(1)}, f32[256,128]{1,0:T(8,128)S(1)}, u32[]{:S(2)}, u32[]{:S(2)}) collective-permute-start(f32[256,128]{1,0:T(8,128)S(1)} %add.827), channel_id=1, source_target_pairs={{0,128},{128,0},{256,384},{384,256},{1,129},{129,1},{257,385},{385... | collective-permute-start | bytes 393224 | tf_op jit(solution)/shard_map/ppermute | solution.py:72
  207.3 4.4 %collective-permute-done.21 = f32[256,128]{1,0:T(8,128)S(1)} collective-permute-done((f32[256,128]{1,0:T(8,128)S(1)}, f32[256,128]{1,0:T(8,128)S(1)}, u32[]{:S(2)}, u32[]{:S(2)}) %collective-permute-start.21) | collective-permute-done | bytes 131104 | tf_op jit(solution)/shard_map/ppermute | solution.py:72
  211.7 4.2 %collective-permute-start.22 = (f32[256,128]{1,0:T(8,128)S(1)}, f32[256,128]{1,0:T(8,128)S(1)}, u32[]{:S(2)}, u32[]{:S(2)}) collective-permute-start(f32[256,128]{1,0:T(8,128)S(1)} %add.828), channel_id=1, source_target_pairs={{0,256},{128,384},{256,0},{384,128},{1,257},{129,385},{257,1},{385... | collective-permute-start | bytes 393224 | tf_op jit(solution)/shard_map/ppermute | solution.py:72
  217.0 3.2 %collective-permute-done.22 = f32[256,128]{1,0:T(8,128)S(1)} collective-permute-done((f32[256,128]{1,0:T(8,128)S(1)}, f32[256,128]{1,0:T(8,128)S(1)}, u32[]{:S(2)}, u32[]{:S(2)}) %collective-permute-start.22) | collective-permute-done | bytes 131104 | tf_op jit(solution)/shard_map/ppermute | solution.py:72
  (146 shorter events, 35.2 us)
Async XLA Ops:
  0.6 121.9 %copy-start = (bf16[4,512,128]{2,1,0:T(8,128)(2,1)S(1)}, bf16[4,512,128]{2,1,0:T(8,128)(2,1)}, u32[]{:S(2)}) copy-start(bf16[4,512,128]{2,1,0:T(8,128)(2,1)} %param.19) | copy-start | bytes 1572868
  0.6 14.5 %copy-start.1 = (bf16[4,512,256]{2,1,0:T(8,128)(2,1)S(1)}, bf16[4,512,256]{2,1,0:T(8,128)(2,1)}, u32[]{:S(2)}) copy-start(bf16[4,512,256]{2,1,0:T(8,128)(2,1)} %param.11) | copy-start | bytes 3145732
  0.7 8.0 %copy-start.11 = (f32[3,64]{1,0:T(4,128)S(1)}, f32[3,64]{1,0:T(4,128)}, u32[]{:S(2)}) copy-start(f32[3,64]{1,0:T(4,128)} %param.18) | copy-start | bytes 2308
  0.7 8.0 %copy-start.10 = (s32[3]{0:T(128)S(1)}, s32[3]{0:T(128)}, u32[]{:S(2)}) copy-start(s32[3]{0:T(128)} %param.14) | copy-start | bytes 40
  0.7 14.4 %copy-start.9 = (s32[4,512]{1,0:T(4,128)S(1)}, s32[4,512]{1,0:T(4,128)}, u32[]{:S(2)}) copy-start(s32[4,512]{1,0:T(4,128)} %param.16) | copy-start | bytes 24580
  1.8 13.3 %collective-permute-start = (bf16[4,64,256]{2,1,0:T(8,128)(2,1)S(1)}, bf16[4,64,256]{2,1,0:T(8,128)(2,1)S(1)}, u32[]{:S(2)}, u32[]{:S(2)}) collective-permute-start(bf16[4,64,256]{2,1,0:T(8,128)(2,1)S(1)} %get-tuple-element.96), channel_id=1, source_target_pairs={{0,1},{1,2},{2,3},{3,4},{4,5},{5,6},{6,7},{7,8},{8,9},{9,10},{10,1... | collective-permute-start | bytes 393224 | tf_op jit(solution)/shard_map/ppermute | solution.py:16
  3.5 11.7 %collective-permute-start.1 = (bf16[4,64,256]{2,1,0:T(8,128)(2,1)S(1)}, bf16[4,64,256]{2,1,0:T(8,128)(2,1)S(1)}, u32[]{:S(2)}, u32[]{:S(2)}) collective-permute-start(bf16[4,64,256]{2,1,0:T(8,128)(2,1)S(1)} %get-tuple-element.95), channel_id=1, source_target_pairs={{1,0},{2,1},{3,2},{4,3},{5,4},{6,5},{7,6},{8,7},{9,8},{10,9},{11,1... | collective-permute-start | bytes 393224 | tf_op jit(solution)/shard_map/ppermute | solution.py:19
  8.7 6.6 %copy-start.5 = (bf16[3,3,256,256]{3,2,1,0:T(8,128)(2,1)S(1)}, bf16[3,3,256,256]{3,2,1,0:T(8,128)(2,1)}, u32[]{:S(2)}) copy-start(bf16[3,3,256,256]{3,2,1,0:T(8,128)(2,1)} %param.12) | copy-start | bytes 3538948
  15.3 1.6 copy-start.4
  18.0 6.0 %collective-permute-start.2 = (bf16[4,64,256]{2,1,0:T(8,128)(2,1)S(1)}, bf16[4,64,256]{2,1,0:T(8,128)(2,1)S(1)}, u32[]{:S(2)}, u32[]{:S(2)}) collective-permute-start(bf16[4,64,256]{2,1,0:T(8,128)(2,1)S(1)} %get-tuple-element.93), channel_id=1, source_target_pairs={{0,1},{1,2},{2,3},{3,4},{4,5},{5,6},{6,7},{7,8},{8,9},{9,10},{10,1... | collective-permute-start | bytes 393224 | tf_op jit(solution)/shard_map/ppermute | solution.py:16
  22.3 4.5 %collective-permute-start.3 = (bf16[4,64,256]{2,1,0:T(8,128)(2,1)S(1)}, bf16[4,64,256]{2,1,0:T(8,128)(2,1)S(1)}, u32[]{:S(2)}, u32[]{:S(2)}) collective-permute-start(bf16[4,64,256]{2,1,0:T(8,128)(2,1)S(1)} %get-tuple-element.94), channel_id=1, source_target_pairs={{1,0},{2,1},{3,2},{4,3},{5,4},{6,5},{7,6},{8,7},{9,8},{10,9},{11,1... | collective-permute-start | bytes 393224 | tf_op jit(solution)/shard_map/ppermute | solution.py:19
  28.5 7.4 %collective-permute-start.4 = (bf16[4,64,256]{2,1,0:T(8,128)(2,1)S(1)}, bf16[4,64,256]{2,1,0:T(8,128)(2,1)S(1)}, u32[]{:S(2)}, u32[]{:S(2)}) collective-permute-start(bf16[4,64,256]{2,1,0:T(8,128)(2,1)S(1)} %get-tuple-element.91), channel_id=1, source_target_pairs={{0,1},{1,2},{2,3},{3,4},{4,5},{5,6},{6,7},{7,8},{8,9},{9,10},{10,1... | collective-permute-start | bytes 393224 | tf_op jit(solution)/shard_map/ppermute | solution.py:16
  34.0 3.2 %collective-permute-start.5 = (bf16[4,64,256]{2,1,0:T(8,128)(2,1)S(1)}, bf16[4,64,256]{2,1,0:T(8,128)(2,1)S(1)}, u32[]{:S(2)}, u32[]{:S(2)}) collective-permute-start(bf16[4,64,256]{2,1,0:T(8,128)(2,1)S(1)} %get-tuple-element.92), channel_id=1, source_target_pairs={{1,0},{2,1},{3,2},{4,3},{5,4},{6,5},{7,6},{8,7},{9,8},{10,9},{11,1... | collective-permute-start | bytes 393224 | tf_op jit(solution)/shard_map/ppermute | solution.py:19
  51.2 7.0 %copy-start.7 = (f32[5,4,64]{2,1,0:T(4,128)S(1)}, f32[5,4,64]{2,1,0:T(4,128)}, u32[]{:S(2)}) copy-start(f32[5,4,64]{2,1,0:T(4,128)} %constant.111.clone.1) | copy-start | bytes 15364
  52.4 5.8 %collective-permute-start.6 = (f32[5,4,64]{2,1,0:T(4,128)S(1)}, f32[5,4,64]{2,1,0:T(4,128)S(1)}, u32[]{:S(2)}, u32[]{:S(2)}) collective-permute-start(f32[5,4,64]{2,1,0:T(4,128)S(1)} %constant_dynamic-update-slice_fusion.3), channel_id=1, source_target_pairs={{0,1},{1,2},{2,3},{3,4},{4,5},{5,6},{6,7},{7,8},{8,9},{9,10},{10,1... | collective-permute-start | bytes 15368 | tf_op jit(solution)/shard_map/ppermute | solution.py:84
  58.2 3.1 %collective-permute-start.7 = (f32[5,4,64]{2,1,0:T(4,128)S(1)}, f32[5,4,64]{2,1,0:T(4,128)S(1)}, u32[]{:S(2)}, u32[]{:S(2)}) collective-permute-start(f32[5,4,64]{2,1,0:T(4,128)S(1)} %broadcast_select_fusion.1), channel_id=1, source_target_pairs={{0,1},{1,2},{2,3},{3,4},{4,5},{5,6},{6,7},{7,8},{8,9},{9,10},{10,1... | collective-permute-start | bytes 15368 | tf_op jit(solution)/shard_map/ppermute | solution.py:84
  61.3 7.4 %collective-permute-start.8 = (f32[5,4,64]{2,1,0:T(4,128)S(1)}, f32[5,4,64]{2,1,0:T(4,128)S(1)}, u32[]{:S(2)}, u32[]{:S(2)}) collective-permute-start(f32[5,4,64]{2,1,0:T(4,128)S(1)} %broadcast_select_fusion), channel_id=1, source_target_pairs={{0,2},{1,3},{2,4},{3,5},{4,6},{5,7},{6,8},{7,9},{8,10},{9,11},{10,... | collective-permute-start | bytes 15368 | tf_op jit(solution)/shard_map/ppermute | solution.py:84
  68.8 12.0 %collective-permute-start.9 = (f32[5,4,64]{2,1,0:T(4,128)S(1)}, f32[5,4,64]{2,1,0:T(4,128)S(1)}, u32[]{:S(2)}, u32[]{:S(2)}) collective-permute-start(f32[5,4,64]{2,1,0:T(4,128)S(1)} %broadcast_select_fusion.2), channel_id=1, source_target_pairs={{0,4},{1,5},{2,6},{3,7},{4,8},{5,9},{6,10},{7,11},{8,12},{9,13},{1... | collective-permute-start | bytes 15368 | tf_op jit(solution)/shard_map/ppermute | solution.py:84
  80.9 14.6 %collective-permute-start.10 = (f32[5,4,64]{2,1,0:T(4,128)S(1)}, f32[5,4,64]{2,1,0:T(4,128)S(1)}, u32[]{:S(2)}, u32[]{:S(2)}) collective-permute-start(f32[5,4,64]{2,1,0:T(4,128)S(1)} %broadcast_select_fusion.3), channel_id=1, source_target_pairs={{0,8},{1,9},{2,10},{3,11},{4,12},{5,13},{6,14},{7,15},{8,16},{9,17... | collective-permute-start | bytes 15368 | tf_op jit(solution)/shard_map/ppermute | solution.py:84
  95.6 6.9 %collective-permute-start.11 = (f32[5,4,64]{2,1,0:T(4,128)S(1)}, f32[5,4,64]{2,1,0:T(4,128)S(1)}, u32[]{:S(2)}, u32[]{:S(2)}) collective-permute-start(f32[5,4,64]{2,1,0:T(4,128)S(1)} %broadcast_select_fusion.4), channel_id=1, source_target_pairs={{0,16},{1,17},{2,18},{3,19},{4,20},{5,21},{6,22},{7,23},{8,24},{9,... | collective-permute-start | bytes 15368 | tf_op jit(solution)/shard_map/ppermute | solution.py:84
  102.6 22.5 %collective-permute-start.12 = (f32[5,4,64]{2,1,0:T(4,128)S(1)}, f32[5,4,64]{2,1,0:T(4,128)S(1)}, u32[]{:S(2)}, u32[]{:S(2)}) collective-permute-start(f32[5,4,64]{2,1,0:T(4,128)S(1)} %broadcast_select_fusion.5), channel_id=1, source_target_pairs={{0,32},{1,33},{2,34},{3,35},{4,36},{5,37},{6,38},{7,39},{8,40},{9,... | collective-permute-start | bytes 15368 | tf_op jit(solution)/shard_map/ppermute | solution.py:84
  123.0 93.0 %copy-start.3 = (f32[4,64,512]{2,1,0:T(8,128)S(1)}, f32[4,64,512]{2,1,0:T(8,128)}, u32[]{:S(2)}) copy-start(f32[4,64,512]{2,1,0:T(8,128)} %copy-done.2) | copy-start | bytes 1572868
  123.0 15.7 %collective-permute-start.14 = (f32[256,128]{1,0:T(8,128)S(1)}, f32[256,128]{1,0:T(8,128)S(1)}, u32[]{:S(2)}, u32[]{:S(2)}) collective-permute-start(f32[256,128]{1,0:T(8,128)S(1)} %convolution_bitcast_fusion.1), channel_id=1, source_target_pairs={{0,1},{1,0},{2,3},{3,2},{4,5},{5,4},{6,7},{7,6},{8,9},{9,8},{10,11... | collective-permute-start | bytes 393224 | tf_op jit(solution)/shard_map/ppermute | solution.py:72
  125.2 15.5 %collective-permute-start.13 = (f32[5,4,64]{2,1,0:T(4,128)S(1)}, f32[5,4,64]{2,1,0:T(4,128)S(1)}, u32[]{:S(2)}, u32[]{:S(2)}) collective-permute-start(f32[5,4,64]{2,1,0:T(4,128)S(1)} %broadcast_select_fusion.6), channel_id=1, source_target_pairs={{0,64},{1,65},{2,66},{3,67},{4,68},{5,69},{6,70},{7,71},{8,72},{9,... | collective-permute-start | bytes 15368 | tf_op jit(solution)/shard_map/ppermute | solution.py:84
  138.7 7.3 %collective-permute-start.15 = (f32[256,128]{1,0:T(8,128)S(1)}, f32[256,128]{1,0:T(8,128)S(1)}, u32[]{:S(2)}, u32[]{:S(2)}) collective-permute-start(f32[256,128]{1,0:T(8,128)S(1)} %add.821), channel_id=1, source_target_pairs={{0,2},{1,3},{2,0},{3,1},{4,6},{5,7},{6,4},{7,5},{8,10},{9,11},{10,... | collective-permute-start | bytes 393224 | tf_op jit(solution)/shard_map/ppermute | solution.py:72
  146.1 8.4 %collective-permute-start.16 = (f32[256,128]{1,0:T(8,128)S(1)}, f32[256,128]{1,0:T(8,128)S(1)}, u32[]{:S(2)}, u32[]{:S(2)}) collective-permute-start(f32[256,128]{1,0:T(8,128)S(1)} %add.822), channel_id=1, source_target_pairs={{0,4},{1,5},{2,6},{3,7},{4,0},{5,1},{6,2},{7,3},{8,12},{9,13},{10,... | collective-permute-start | bytes 393224 | tf_op jit(solution)/shard_map/ppermute | solution.py:72
  154.4 7.0 %collective-permute-start.17 = (f32[256,128]{1,0:T(8,128)S(1)}, f32[256,128]{1,0:T(8,128)S(1)}, u32[]{:S(2)}, u32[]{:S(2)}) collective-permute-start(f32[256,128]{1,0:T(8,128)S(1)} %add.823), channel_id=1, source_target_pairs={{0,8},{8,0},{16,24},{24,16},{32,40},{40,32},{48,56},{56,48},{64,72... | collective-permute-start | bytes 393224 | tf_op jit(solution)/shard_map/ppermute | solution.py:72
  161.4 9.3 %collective-permute-start.18 = (f32[256,128]{1,0:T(8,128)S(1)}, f32[256,128]{1,0:T(8,128)S(1)}, u32[]{:S(2)}, u32[]{:S(2)}) collective-permute-start(f32[256,128]{1,0:T(8,128)S(1)} %add.824), channel_id=1, source_target_pairs={{0,16},{8,24},{16,0},{24,8},{32,48},{40,56},{48,32},{56,40},{64,80... | collective-permute-start | bytes 393224 | tf_op jit(solution)/shard_map/ppermute | solution.py:72
  170.7 18.5 %collective-permute-start.19 = (f32[256,128]{1,0:T(8,128)S(1)}, f32[256,128]{1,0:T(8,128)S(1)}, u32[]{:S(2)}, u32[]{:S(2)}) collective-permute-start(f32[256,128]{1,0:T(8,128)S(1)} %add.825), channel_id=1, source_target_pairs={{0,32},{8,40},{16,48},{24,56},{32,0},{40,8},{48,16},{56,24},{64,96... | collective-permute-start | bytes 393224 | tf_op jit(solution)/shard_map/ppermute | solution.py:72
  189.3 15.6 %collective-permute-start.20 = (f32[256,128]{1,0:T(8,128)S(1)}, f32[256,128]{1,0:T(8,128)S(1)}, u32[]{:S(2)}, u32[]{:S(2)}) collective-permute-start(f32[256,128]{1,0:T(8,128)S(1)} %add.826), channel_id=1, source_target_pairs={{0,64},{8,72},{16,80},{24,88},{32,96},{40,104},{48,112},{56,120},{... | collective-permute-start | bytes 393224 | tf_op jit(solution)/shard_map/ppermute | solution.py:72
  204.9 6.9 %collective-permute-start.21 = (f32[256,128]{1,0:T(8,128)S(1)}, f32[256,128]{1,0:T(8,128)S(1)}, u32[]{:S(2)}, u32[]{:S(2)}) collective-permute-start(f32[256,128]{1,0:T(8,128)S(1)} %add.827), channel_id=1, source_target_pairs={{0,128},{128,0},{256,384},{384,256},{1,129},{129,1},{257,385},{385... | collective-permute-start | bytes 393224 | tf_op jit(solution)/shard_map/ppermute | solution.py:72
  211.7 8.4 %collective-permute-start.22 = (f32[256,128]{1,0:T(8,128)S(1)}, f32[256,128]{1,0:T(8,128)S(1)}, u32[]{:S(2)}, u32[]{:S(2)}) collective-permute-start(f32[256,128]{1,0:T(8,128)S(1)} %add.828), channel_id=1, source_target_pairs={{0,256},{128,384},{256,0},{384,128},{1,257},{129,385},{257,1},{385... | collective-permute-start | bytes 393224 | tf_op jit(solution)/shard_map/ppermute | solution.py:72
  (3 other events, 2.9 us)

commit v3 on v0

--- a/solution.py
+++ b/solution.py
@@ -64,6 +64,36 @@
     return result
 
 
+def butterfly_sum(value, axis):
+    count = lax.axis_size(axis)
+    step = 1
+    while step < count:
+        pairs = [(i, i ^ step) for i in range(count)]
+        value = value + lax.ppermute(value, axis, pairs)
+        step = step * 2
+    return value
+
+
+def scan_and_sum(totals, grad, axes):
+    prefix = jnp.zeros_like(totals).at[0].set(1.0)
+    for axis in axes:
+        count = lax.axis_size(axis)
+        place = lax.axis_index(axis)
+        step = 1
+        while step < count:
+            pairs = [(i, i ^ step) for i in range(count)]
+            packed = jnp.concatenate([grad, totals.reshape(-1, grad.shape[1])])
+            packed = lax.ppermute(packed, axis, pairs)
+            other = packed[grad.shape[0] :].reshape(totals.shape)
+            grad = grad + packed[: grad.shape[0]]
+            lower = (place & step) != 0
+            prefix = jnp.where(lower, jnp.stack(combine(tuple(other), tuple(prefix))), prefix)
+            early = jnp.where(lower, other, totals)
+            late = jnp.where(lower, totals, other)
+            totals = jnp.stack(combine(tuple(early), tuple(late)))
+            step = step * 2
+    return prefix, grad
+
 def elements(obs, logp, params, present, keep, first):
     rate = params[0][:, None]
     noise = params[1][:, None]
@@ -124,15 +154,14 @@
         frame_keep[:, None, :],
         first,
     )
-    local = doubling_prefix(elems, 2)
-    totals = tuple((item[:, :, -1] for item in local))
-    identity = (jnp.ones_like(totals[0]),) + tuple((jnp.zeros_like(item) for item in totals[1:]))
-    prefix = prefix_2(totals, ("outer", "inner"), combine, identity)
-    final = combine(tuple((item[:, :, None] for item in prefix)), local)
     grad_local = jnp.einsum(
         "tfw,tfs->ws", hidden, head_cotangent, preferred_element_type=jnp.float32
     )
-    head_grad = lax.psum(grad_local, ("take", "outer", "inner"))
+    grad_local = butterfly_sum(grad_local, "take")
+    local = doubling_prefix(elems, 2)
+    totals = jnp.stack([item[:, :, -1] for item in local])
+    prefix, head_grad = scan_and_sum(totals, grad_local, ("inner", "outer"))
+    final = combine(tuple((item[:, :, None] for item in prefix)), local)
     return (final[1], head_grad)
 
 

time: 694 us -> 161 us (0.23)
  the two profiles are of different devices: /device:TPU:487 before, /device:TPU:1 now
where the time goes in v3:
time: 161 us
  starting transfers between devices  70.4 us (44%)
  waiting for transfers between devices  49.8 us (31%)
  other arithmetic  15.1 us (9%)
  matrix products  9.52 us (6%)
  local copies, waits for them, and re-layouts  8.47 us (5%)
  between operations  7.45 us (5%)
    ppermute x7, starting transfers between devices, scan_and_sum(): packed = lax.ppermute(packed, axis, pairs)  45.6 us
    ppermute x7, waiting for transfers between devices, scan_and_sum(): packed = lax.ppermute(packed, axis, pairs)  39.8 us
    ppermute x3, starting transfers between devices, extended_2(): lax.ppermute(lax.slice_in_dim(block, 0, width, axis=dim), axis, backward)  10.4 us
    add x8, other arithmetic, combine(): new_c = a_two * a_two * c_one / denom + c_two  9.58 us
    dot_general x9, matrix products, conv_layer(): jnp.einsum('tfw,wv->tfv', piece, weights[tap], preferred_element_type=jnp...  8.56 us
    ppermute x3, starting transfers between devices, extended_2(): lax.ppermute(lax.slice_in_dim(block, block.shape[dim] - width, None, axis...  8.34 us
    ppermute x3, waiting for transfers between devices, extended_2(): lax.ppermute(lax.slice_in_dim(block, 0, width, axis=dim), axis, backward)  6.85 us
    ppermute x2, starting transfers between devices, butterfly_sum(): value = value + lax.ppermute(value, axis, pairs)  6 us
  transfers between devices with their start and end apart: 15, of which 10 were waited for; matrix products, arithmetic and copies ran while one was open for 13% of the time, Pallas kernels for 0%

profile of v3, /device:TPU:1, one launch (start us, length us, event | category | flops | bytes accessed | tf_op | source)
XLA Modules:
  0.0 160.7 jit_solution(7565539509532107535)
XLA Ops:
  1.8 4.5 %collective-permute-start = (bf16[4,64,256]{2,1,0:T(8,128)(2,1)S(1)}, bf16[4,64,256]{2,1,0:T(8,128)(2,1)S(1)}, u32[]{:S(2)}, u32[]{:S(2)}) collective-permute-start(bf16[4,64,256]{2,1,0:T(8,128)(2,1)S(1)} %get-tuple-element.94), channel_id=1, source_target_pairs={{0,1},{1,2},{2,3},{3,4},{4,5},{5,6},{6,7},{7,8},{8,9},{9,10},{10,1... | collective-permute-start | bytes 393224 | tf_op jit(solution)/shard_map/ppermute | solution.py:16
  6.3 5.5 %collective-permute-start.1 = (bf16[4,64,256]{2,1,0:T(8,128)(2,1)S(1)}, bf16[4,64,256]{2,1,0:T(8,128)(2,1)S(1)}, u32[]{:S(2)}, u32[]{:S(2)}) collective-permute-start(bf16[4,64,256]{2,1,0:T(8,128)(2,1)S(1)} %get-tuple-element.93), channel_id=1, source_target_pairs={{1,0},{2,1},{3,2},{4,3},{5,4},{6,5},{7,6},{8,7},{9,8},{10,9},{11,1... | collective-permute-start | bytes 393224 | tf_op jit(solution)/shard_map/ppermute | solution.py:19
  12.7 3.0 %fusion.60 = f32[4,512,256]{2,1,0:T(8,128)} fusion(bf16[4,512,256]{2,1,0:T(8,128)(2,1)} %param.11, bf16[3,3,256,256]{3,2,1,0:T(8,128)(2,1)} %param.12), kind=kOutput, calls=%fused_computation.221 | convolution fusion | flops 268435456 | bytes 3276800 | tf_op jit(solution)/shard_map/tfw,wv->tfv/dot_general | solution.py:118
  25.0 1.9 %collective-permute-start.2 = (bf16[4,64,256]{2,1,0:T(8,128)(2,1)S(1)}, bf16[4,64,256]{2,1,0:T(8,128)(2,1)S(1)}, u32[]{:S(2)}, u32[]{:S(2)}) collective-permute-start(bf16[4,64,256]{2,1,0:T(8,128)(2,1)S(1)} %get-tuple-element.91), channel_id=1, source_target_pairs={{0,1},{1,2},{2,3},{3,4},{4,5},{5,6},{6,7},{7,8},{8,9},{9,10},{10,1... | collective-permute-start | bytes 393224 | tf_op jit(solution)/shard_map/ppermute | solution.py:16
  27.0 2.4 %collective-permute-start.3 = (bf16[4,64,256]{2,1,0:T(8,128)(2,1)S(1)}, bf16[4,64,256]{2,1,0:T(8,128)(2,1)S(1)}, u32[]{:S(2)}, u32[]{:S(2)}) collective-permute-start(bf16[4,64,256]{2,1,0:T(8,128)(2,1)S(1)} %get-tuple-element.92), channel_id=1, source_target_pairs={{1,0},{2,1},{3,2},{4,3},{5,4},{6,5},{7,6},{8,7},{9,8},{10,9},{11,1... | collective-permute-start | bytes 393224 | tf_op jit(solution)/shard_map/ppermute | solution.py:19
  29.8 3.4 %collective-permute-done.3 = bf16[4,64,256]{2,1,0:T(8,128)(2,1)S(1)} collective-permute-done((bf16[4,64,256]{2,1,0:T(8,128)(2,1)S(1)}, bf16[4,64,256]{2,1,0:T(8,128)(2,1)S(1)}, u32[]{:S(2)}, u32[]{:S(2)}) %collective-permute-start.3) | collective-permute-done | bytes 131104 | tf_op jit(solution)/shard_map/ppermute | solution.py:19
  34.9 1.9 %collective-permute-start.4 = (bf16[4,64,256]{2,1,0:T(8,128)(2,1)S(1)}, bf16[4,64,256]{2,1,0:T(8,128)(2,1)S(1)}, u32[]{:S(2)}, u32[]{:S(2)}) collective-permute-start(bf16[4,64,256]{2,1,0:T(8,128)(2,1)S(1)} %get-tuple-element.89), channel_id=1, source_target_pairs={{0,1},{1,2},{2,3},{3,4},{4,5},{5,6},{6,7},{7,8},{8,9},{9,10},{10,1... | collective-permute-start | bytes 393224 | tf_op jit(solution)/shard_map/ppermute | solution.py:16
  36.9 2.4 %collective-permute-start.5 = (bf16[4,64,256]{2,1,0:T(8,128)(2,1)S(1)}, bf16[4,64,256]{2,1,0:T(8,128)(2,1)S(1)}, u32[]{:S(2)}, u32[]{:S(2)}) collective-permute-start(bf16[4,64,256]{2,1,0:T(8,128)(2,1)S(1)} %get-tuple-element.90), channel_id=1, source_target_pairs={{1,0},{2,1},{3,2},{4,3},{5,4},{6,5},{7,6},{8,7},{9,8},{10,9},{11,1... | collective-permute-start | bytes 393224 | tf_op jit(solution)/shard_map/ppermute | solution.py:19
  39.7 3.4 %collective-permute-done.5 = bf16[4,64,256]{2,1,0:T(8,128)(2,1)S(1)} collective-permute-done((bf16[4,64,256]{2,1,0:T(8,128)(2,1)S(1)}, bf16[4,64,256]{2,1,0:T(8,128)(2,1)S(1)}, u32[]{:S(2)}, u32[]{:S(2)}) %collective-permute-start.5) | collective-permute-done | bytes 131104 | tf_op jit(solution)/shard_map/ppermute | solution.py:19
  45.3 2.1 %collective-permute-start.6 = (f32[256,128]{1,0:T(8,128)S(1)}, f32[256,128]{1,0:T(8,128)S(1)}, u32[]{:S(2)}, u32[]{:S(2)}) collective-permute-start(f32[256,128]{1,0:T(8,128)S(1)} %convolution_bitcast_fusion.1), channel_id=1, source_target_pairs={{0,128},{128,0},{256,384},{384,256},{1,129},{129,1},{257,385},{385... | collective-permute-start | bytes 393224 | tf_op jit(solution)/shard_map/ppermute | solution.py:72
  50.3 1.3 divide_add_fusion.12
  51.6 1.3 divide_add_fusion.11
  52.9 1.3 divide_add_fusion.10
  54.2 1.3 divide_add_fusion.9
  55.5 1.3 divide_add_fusion.8
  56.9 1.2 fusion.30
  60.9 3.9 %collective-permute-start.7 = (f32[256,128]{1,0:T(8,128)S(1)}, f32[256,128]{1,0:T(8,128)S(1)}, u32[]{:S(2)}, u32[]{:S(2)}) collective-permute-start(f32[256,128]{1,0:T(8,128)S(1)} %add.944), channel_id=1, source_target_pairs={{0,256},{128,384},{256,0},{384,128},{1,257},{129,385},{257,1},{385... | collective-permute-start | bytes 393224 | tf_op jit(solution)/shard_map/ppermute | solution.py:72
  64.9 3.2 %collective-permute-done.7 = f32[256,128]{1,0:T(8,128)S(1)} collective-permute-done((f32[256,128]{1,0:T(8,128)S(1)}, f32[256,128]{1,0:T(8,128)S(1)}, u32[]{:S(2)}, u32[]{:S(2)}) %collective-permute-start.7) | collective-permute-done | bytes 131104 | tf_op jit(solution)/shard_map/ppermute | solution.py:72
  68.2 1.9 %collective-permute-start.8 = (f32[266,128]{1,0:T(8,128)S(1)}, f32[266,128]{1,0:T(8,128)S(1)}, u32[]{:S(2)}, u32[]{:S(2)}) collective-permute-start(f32[266,128]{1,0:T(8,128)S(1)} %pad_maximum_fusion.2), channel_id=1, source_target_pairs={{0,1},{1,0},{2,3},{3,2},{4,5},{5,4},{6,7},{7,6},{8,9},{9,8},{10,11... | collective-permute-start | bytes 408584 | tf_op jit(solution)/shard_map/ppermute | solution.py:86
  70.1 1.3 collective-permute-done.8
  71.7 3.9 %collective-permute-start.9 = (f32[266,128]{1,0:T(8,128)S(1)}, f32[266,128]{1,0:T(8,128)S(1)}, u32[]{:S(2)}, u32[]{:S(2)}) collective-permute-start(f32[266,128]{1,0:T(8,128)S(1)} %pad_maximum_fusion.3), channel_id=1, source_target_pairs={{0,2},{1,3},{2,0},{3,1},{4,6},{5,7},{6,4},{7,5},{8,10},{9,11},{10,... | collective-permute-start | bytes 408584 | tf_op jit(solution)/shard_map/ppermute | solution.py:86
  76.2 3.2 %collective-permute-done.9 = f32[266,128]{1,0:T(8,128)S(1)} collective-permute-done((f32[266,128]{1,0:T(8,128)S(1)}, f32[266,128]{1,0:T(8,128)S(1)}, u32[]{:S(2)}, u32[]{:S(2)}) %collective-permute-start.9) | collective-permute-done | bytes 136224 | tf_op jit(solution)/shard_map/ppermute | solution.py:86
  79.7 9.8 %collective-permute-start.10 = (f32[266,128]{1,0:T(8,128)S(1)}, f32[266,128]{1,0:T(8,128)S(1)}, u32[]{:S(2)}, u32[]{:S(2)}) collective-permute-start(f32[266,128]{1,0:T(8,128)S(1)} %pad_maximum_fusion.4), channel_id=1, source_target_pairs={{0,4},{1,5},{2,6},{3,7},{4,0},{5,1},{6,2},{7,3},{8,12},{9,13},{10,... | collective-permute-start | bytes 408584 | tf_op jit(solution)/shard_map/ppermute | solution.py:86
  90.0 2.8 %collective-permute-done.10 = f32[266,128]{1,0:T(8,128)S(1)} collective-permute-done((f32[266,128]{1,0:T(8,128)S(1)}, f32[266,128]{1,0:T(8,128)S(1)}, u32[]{:S(2)}, u32[]{:S(2)}) %collective-permute-start.10) | collective-permute-done | bytes 136224 | tf_op jit(solution)/shard_map/ppermute | solution.py:86
  93.1 3.0 %collective-permute-start.11 = (f32[266,128]{1,0:T(8,128)S(1)}, f32[266,128]{1,0:T(8,128)S(1)}, u32[]{:S(2)}, u32[]{:S(2)}) collective-permute-start(f32[266,128]{1,0:T(8,128)S(1)} %pad_maximum_fusion.5), channel_id=1, source_target_pairs={{0,8},{8,0},{16,24},{24,16},{32,40},{40,32},{48,56},{56,48},{64,72... | collective-permute-start | bytes 408584 | tf_op jit(solution)/shard_map/ppermute | solution.py:86
  96.6 2.3 %collective-permute-done.11 = f32[266,128]{1,0:T(8,128)S(1)} collective-permute-done((f32[266,128]{1,0:T(8,128)S(1)}, f32[266,128]{1,0:T(8,128)S(1)}, u32[]{:S(2)}, u32[]{:S(2)}) %collective-permute-start.11) | collective-permute-done | bytes 136224 | tf_op jit(solution)/shard_map/ppermute | solution.py:86
  99.2 10.2 %collective-permute-start.12 = (f32[266,128]{1,0:T(8,128)S(1)}, f32[266,128]{1,0:T(8,128)S(1)}, u32[]{:S(2)}, u32[]{:S(2)}) collective-permute-start(f32[266,128]{1,0:T(8,128)S(1)} %pad_maximum_fusion.6), channel_id=1, source_target_pairs={{0,16},{8,24},{16,0},{24,8},{32,48},{40,56},{48,32},{56,40},{64,80... | collective-permute-start | bytes 408584 | tf_op jit(solution)/shard_map/ppermute | solution.py:86
  109.9 4.2 %collective-permute-done.12 = f32[266,128]{1,0:T(8,128)S(1)} collective-permute-done((f32[266,128]{1,0:T(8,128)S(1)}, f32[266,128]{1,0:T(8,128)S(1)}, u32[]{:S(2)}, u32[]{:S(2)}) %collective-permute-start.12) | collective-permute-done | bytes 136224 | tf_op jit(solution)/shard_map/ppermute | solution.py:86
  114.4 8.8 %collective-permute-start.13 = (f32[266,128]{1,0:T(8,128)S(1)}, f32[266,128]{1,0:T(8,128)S(1)}, u32[]{:S(2)}, u32[]{:S(2)}) collective-permute-start(f32[266,128]{1,0:T(8,128)S(1)} %pad_maximum_fusion.7), channel_id=1, source_target_pairs={{0,32},{8,40},{16,48},{24,56},{32,0},{40,8},{48,16},{56,24},{64,96... | collective-permute-start | bytes 408584 | tf_op jit(solution)/shard_map/ppermute | solution.py:86
  123.8 12.3 %collective-permute-done.13 = f32[266,128]{1,0:T(8,128)S(1)} collective-permute-done((f32[266,128]{1,0:T(8,128)S(1)}, f32[266,128]{1,0:T(8,128)S(1)}, u32[]{:S(2)}, u32[]{:S(2)}) %collective-permute-start.13) | collective-permute-done | bytes 136224 | tf_op jit(solution)/shard_map/ppermute | solution.py:86
  136.4 7.9 %collective-permute-start.14 = (f32[266,128]{1,0:T(8,128)S(1)}, f32[266,128]{1,0:T(8,128)S(1)}, u32[]{:S(2)}, u32[]{:S(2)}) collective-permute-start(f32[266,128]{1,0:T(8,128)S(1)} %pad_maximum_fusion.8), channel_id=1, source_target_pairs={{0,64},{8,72},{16,80},{24,88},{32,96},{40,104},{48,112},{56,120},{... | collective-permute-start | bytes 408584 | tf_op jit(solution)/shard_map/ppermute | solution.py:86
  144.8 13.7 %collective-permute-done.14 = f32[266,128]{1,0:T(8,128)S(1)} collective-permute-done((f32[266,128]{1,0:T(8,128)S(1)}, f32[266,128]{1,0:T(8,128)S(1)}, u32[]{:S(2)}, u32[]{:S(2)}) %collective-permute-start.14) | collective-permute-done | bytes 136224 | tf_op jit(solution)/shard_map/ppermute | solution.py:86
  (229 shorter events, 22.4 us)
Async XLA Ops:
  0.6 44.2 %copy-start = (bf16[4,512,128]{2,1,0:T(8,128)(2,1)S(1)}, bf16[4,512,128]{2,1,0:T(8,128)(2,1)}, u32[]{:S(2)}) copy-start(bf16[4,512,128]{2,1,0:T(8,128)(2,1)} %param.19) | copy-start | bytes 1572868
  0.6 21.5 %copy-start.1 = (bf16[4,512,256]{2,1,0:T(8,128)(2,1)S(1)}, bf16[4,512,256]{2,1,0:T(8,128)(2,1)}, u32[]{:S(2)}) copy-start(bf16[4,512,256]{2,1,0:T(8,128)(2,1)} %param.11) | copy-start | bytes 3145732
  0.7 15.0 %copy-start.9 = (f32[3,64]{1,0:T(4,128)S(1)}, f32[3,64]{1,0:T(4,128)}, u32[]{:S(2)}) copy-start(f32[3,64]{1,0:T(4,128)} %param.18) | copy-start | bytes 2308
  0.7 15.0 %copy-start.8 = (s32[3]{0:T(128)S(1)}, s32[3]{0:T(128)}, u32[]{:S(2)}) copy-start(s32[3]{0:T(128)} %param.14) | copy-start | bytes 40
  0.7 21.4 %copy-start.7 = (s32[4,512]{1,0:T(4,128)S(1)}, s32[4,512]{1,0:T(4,128)}, u32[]{:S(2)}) copy-start(s32[4,512]{1,0:T(4,128)} %param.16) | copy-start | bytes 24580
  1.8 20.4 %collective-permute-start = (bf16[4,64,256]{2,1,0:T(8,128)(2,1)S(1)}, bf16[4,64,256]{2,1,0:T(8,128)(2,1)S(1)}, u32[]{:S(2)}, u32[]{:S(2)}) collective-permute-start(bf16[4,64,256]{2,1,0:T(8,128)(2,1)S(1)} %get-tuple-element.94), channel_id=1, source_target_pairs={{0,1},{1,2},{2,3},{3,4},{4,5},{5,6},{6,7},{7,8},{8,9},{9,10},{10,1... | collective-permute-start | bytes 393224 | tf_op jit(solution)/shard_map/ppermute | solution.py:16
  6.3 16.0 %collective-permute-start.1 = (bf16[4,64,256]{2,1,0:T(8,128)(2,1)S(1)}, bf16[4,64,256]{2,1,0:T(8,128)(2,1)S(1)}, u32[]{:S(2)}, u32[]{:S(2)}) collective-permute-start(bf16[4,64,256]{2,1,0:T(8,128)(2,1)S(1)} %get-tuple-element.93), channel_id=1, source_target_pairs={{1,0},{2,1},{3,2},{4,3},{5,4},{6,5},{7,6},{8,7},{9,8},{10,9},{11,1... | collective-permute-start | bytes 393224 | tf_op jit(solution)/shard_map/ppermute | solution.py:19
  15.7 6.6 %copy-start.3 = (bf16[3,3,256,256]{3,2,1,0:T(8,128)(2,1)S(1)}, bf16[3,3,256,256]{3,2,1,0:T(8,128)(2,1)}, u32[]{:S(2)}) copy-start(bf16[3,3,256,256]{3,2,1,0:T(8,128)(2,1)} %param.12) | copy-start | bytes 3538948
  22.3 1.6 copy-start.2
  25.0 4.8 %collective-permute-start.2 = (bf16[4,64,256]{2,1,0:T(8,128)(2,1)S(1)}, bf16[4,64,256]{2,1,0:T(8,128)(2,1)S(1)}, u32[]{:S(2)}, u32[]{:S(2)}) collective-permute-start(bf16[4,64,256]{2,1,0:T(8,128)(2,1)S(1)} %get-tuple-element.91), channel_id=1, source_target_pairs={{0,1},{1,2},{2,3},{3,4},{4,5},{5,6},{6,7},{7,8},{8,9},{9,10},{10,1... | collective-permute-start | bytes 393224 | tf_op jit(solution)/shard_map/ppermute | solution.py:16
  27.0 6.3 %collective-permute-start.3 = (bf16[4,64,256]{2,1,0:T(8,128)(2,1)S(1)}, bf16[4,64,256]{2,1,0:T(8,128)(2,1)S(1)}, u32[]{:S(2)}, u32[]{:S(2)}) collective-permute-start(bf16[4,64,256]{2,1,0:T(8,128)(2,1)S(1)} %get-tuple-element.92), channel_id=1, source_target_pairs={{1,0},{2,1},{3,2},{4,3},{5,4},{6,5},{7,6},{8,7},{9,8},{10,9},{11,1... | collective-permute-start | bytes 393224 | tf_op jit(solution)/shard_map/ppermute | solution.py:19
  34.9 4.8 %collective-permute-start.4 = (bf16[4,64,256]{2,1,0:T(8,128)(2,1)S(1)}, bf16[4,64,256]{2,1,0:T(8,128)(2,1)S(1)}, u32[]{:S(2)}, u32[]{:S(2)}) collective-permute-start(bf16[4,64,256]{2,1,0:T(8,128)(2,1)S(1)} %get-tuple-element.89), channel_id=1, source_target_pairs={{0,1},{1,2},{2,3},{3,4},{4,5},{5,6},{6,7},{7,8},{8,9},{9,10},{10,1... | collective-permute-start | bytes 393224 | tf_op jit(solution)/shard_map/ppermute | solution.py:16
  36.9 6.3 %collective-permute-start.5 = (bf16[4,64,256]{2,1,0:T(8,128)(2,1)S(1)}, bf16[4,64,256]{2,1,0:T(8,128)(2,1)S(1)}, u32[]{:S(2)}, u32[]{:S(2)}) collective-permute-start(bf16[4,64,256]{2,1,0:T(8,128)(2,1)S(1)} %get-tuple-element.90), channel_id=1, source_target_pairs={{1,0},{2,1},{3,2},{4,3},{5,4},{6,5},{7,6},{8,7},{9,8},{10,9},{11,1... | collective-permute-start | bytes 393224 | tf_op jit(solution)/shard_map/ppermute | solution.py:19
  43.7 3.7 %copy-start.4 = (bf16[256,128]{1,0:T(8,128)(2,1)S(1)}, bf16[256,128]{1,0:T(8,128)(2,1)}, u32[]{:S(2)}) copy-start(bf16[256,128]{1,0:T(8,128)(2,1)} %param.15) | copy-start | bytes 196612
  44.8 3.6 %copy-start.5 = (f32[4,512]{1,0:T(4,128)S(1)}, f32[4,512]{1,0:T(4,128)}, u32[]{:S(2)}) copy-start(f32[4,512]{1,0:T(4,128)} %param.17) | copy-start | bytes 24580
  45.3 15.6 %collective-permute-start.6 = (f32[256,128]{1,0:T(8,128)S(1)}, f32[256,128]{1,0:T(8,128)S(1)}, u32[]{:S(2)}, u32[]{:S(2)}) collective-permute-start(f32[256,128]{1,0:T(8,128)S(1)} %convolution_bitcast_fusion.1), channel_id=1, source_target_pairs={{0,128},{128,0},{256,384},{384,256},{1,129},{129,1},{257,385},{385... | collective-permute-start | bytes 393224 | tf_op jit(solution)/shard_map/ppermute | solution.py:72
  60.0 16.2 %copy-start.6 = (f32[5,4,64]{2,1,0:T(4,128)S(1)}, f32[5,4,64]{2,1,0:T(4,128)}, u32[]{:S(2)}) copy-start(f32[5,4,64]{2,1,0:T(4,128)} %constant.114.clone.1) | copy-start | bytes 15364
  60.9 7.2 %collective-permute-start.7 = (f32[256,128]{1,0:T(8,128)S(1)}, f32[256,128]{1,0:T(8,128)S(1)}, u32[]{:S(2)}, u32[]{:S(2)}) collective-permute-start(f32[256,128]{1,0:T(8,128)S(1)} %add.944), channel_id=1, source_target_pairs={{0,256},{128,384},{256,0},{384,128},{1,257},{129,385},{257,1},{385... | collective-permute-start | bytes 393224 | tf_op jit(solution)/shard_map/ppermute | solution.py:72
  68.2 3.3 %collective-permute-start.8 = (f32[266,128]{1,0:T(8,128)S(1)}, f32[266,128]{1,0:T(8,128)S(1)}, u32[]{:S(2)}, u32[]{:S(2)}) collective-permute-start(f32[266,128]{1,0:T(8,128)S(1)} %pad_maximum_fusion.2), channel_id=1, source_target_pairs={{0,1},{1,0},{2,3},{3,2},{4,5},{5,4},{6,7},{7,6},{8,9},{9,8},{10,11... | collective-permute-start | bytes 408584 | tf_op jit(solution)/shard_map/ppermute | solution.py:86
  71.7 7.6 %collective-permute-start.9 = (f32[266,128]{1,0:T(8,128)S(1)}, f32[266,128]{1,0:T(8,128)S(1)}, u32[]{:S(2)}, u32[]{:S(2)}) collective-permute-start(f32[266,128]{1,0:T(8,128)S(1)} %pad_maximum_fusion.3), channel_id=1, source_target_pairs={{0,2},{1,3},{2,0},{3,1},{4,6},{5,7},{6,4},{7,5},{8,10},{9,11},{10,... | collective-permute-start | bytes 408584 | tf_op jit(solution)/shard_map/ppermute | solution.py:86
  79.7 13.1 %collective-permute-start.10 = (f32[266,128]{1,0:T(8,128)S(1)}, f32[266,128]{1,0:T(8,128)S(1)}, u32[]{:S(2)}, u32[]{:S(2)}) collective-permute-start(f32[266,128]{1,0:T(8,128)S(1)} %pad_maximum_fusion.4), channel_id=1, source_target_pairs={{0,4},{1,5},{2,6},{3,7},{4,0},{5,1},{6,2},{7,3},{8,12},{9,13},{10,... | collective-permute-start | bytes 408584 | tf_op jit(solution)/shard_map/ppermute | solution.py:86
  93.1 5.8 %collective-permute-start.11 = (f32[266,128]{1,0:T(8,128)S(1)}, f32[266,128]{1,0:T(8,128)S(1)}, u32[]{:S(2)}, u32[]{:S(2)}) collective-permute-start(f32[266,128]{1,0:T(8,128)S(1)} %pad_maximum_fusion.5), channel_id=1, source_target_pairs={{0,8},{8,0},{16,24},{24,16},{32,40},{40,32},{48,56},{56,48},{64,72... | collective-permute-start | bytes 408584 | tf_op jit(solution)/shard_map/ppermute | solution.py:86
  99.2 15.0 %collective-permute-start.12 = (f32[266,128]{1,0:T(8,128)S(1)}, f32[266,128]{1,0:T(8,128)S(1)}, u32[]{:S(2)}, u32[]{:S(2)}) collective-permute-start(f32[266,128]{1,0:T(8,128)S(1)} %pad_maximum_fusion.6), channel_id=1, source_target_pairs={{0,16},{8,24},{16,0},{24,8},{32,48},{40,56},{48,32},{56,40},{64,80... | collective-permute-start | bytes 408584 | tf_op jit(solution)/shard_map/ppermute | solution.py:86
  114.4 21.6 %collective-permute-start.13 = (f32[266,128]{1,0:T(8,128)S(1)}, f32[266,128]{1,0:T(8,128)S(1)}, u32[]{:S(2)}, u32[]{:S(2)}) collective-permute-start(f32[266,128]{1,0:T(8,128)S(1)} %pad_maximum_fusion.7), channel_id=1, source_target_pairs={{0,32},{8,40},{16,48},{24,56},{32,0},{40,8},{48,16},{56,24},{64,96... | collective-permute-start | bytes 408584 | tf_op jit(solution)/shard_map/ppermute | solution.py:86
  136.4 22.1 %collective-permute-start.14 = (f32[266,128]{1,0:T(8,128)S(1)}, f32[266,128]{1,0:T(8,128)S(1)}, u32[]{:S(2)}, u32[]{:S(2)}) collective-permute-start(f32[266,128]{1,0:T(8,128)S(1)} %pad_maximum_fusion.8), channel_id=1, source_target_pairs={{0,64},{8,72},{16,80},{24,88},{32,96},{40,104},{48,112},{56,120},{... | collective-permute-start | bytes 408584 | tf_op jit(solution)/shard_map/ppermute | solution.py:86

commit v4 on v3

--- a/solution.py
+++ b/solution.py
@@ -6,6 +6,7 @@
 STATE = 64
 LAYERS = 3
 DMAX = 64
+HALO = 136
 
 
 def extended_2(block, sides, width):
@@ -138,9 +139,17 @@
     block_len = frames.shape[1]
     position = lax.axis_index(("outer", "inner"))
     hidden = frames
+    halo = HALO
+    hidden = extended_2(hidden, ((("outer", "inner"), 1),), halo)
+    count = lax.axis_size(("outer", "inner"))
+    spots = position * block_len - halo + jnp.arange(block_len + 2 * halo, dtype=jnp.int32)
+    inside = ((spots >= 0) & (spots < count * block_len))[None, :, None]
+    pad = ((0, 0), (DMAX, DMAX), (0, 0))
     for layer in range(LAYERS):
-        extended = extended_2(hidden, ((("outer", "inner"), 1),), DMAX)
+        extended = jnp.pad(hidden, pad)
         hidden = conv_layer(extended, conv_weight[layer], conv_bias[layer], dilations[layer])
+        hidden = jnp.where(inside, hidden, jnp.zeros_like(hidden))
+    hidden = hidden[:, halo : halo + block_len]
     head = jnp.einsum("tfw,ws->tsf", hidden, head_weight, preferred_element_type=jnp.float32)
     obs = head[:, :STATE]
     logp = head[:, STATE:]

time: 161 us -> 139 us (0.86)
  the two profiles are of different devices: /device:TPU:1 before, /device:TPU:3 now
where the time goes in v4:
time: 139 us
  starting transfers between devices  55.5 us (40%)
  waiting for transfers between devices  40.3 us (29%)
  other arithmetic  16.8 us (12%)
  local copies, waits for them, and re-layouts  9.42 us (7%)
  matrix products  9.25 us (7%)
  between operations  7.32 us (5%)
    ppermute x7, starting transfers between devices, scan_and_sum(): packed = lax.ppermute(packed, axis, pairs)  42 us
    ppermute x7, waiting for transfers between devices, scan_and_sum(): packed = lax.ppermute(packed, axis, pairs)  37.4 us
    add x8, other arithmetic, combine(): new_c = a_two * a_two * c_one / denom + c_two  9.58 us
    dot_general x9, matrix products, conv_layer(): jnp.einsum('tfw,wv->tfv', piece, weights[tap], preferred_element_type=jnp...  8.29 us
    ppermute x2, starting transfers between devices, butterfly_sum(): value = value + lax.ppermute(value, axis, pairs)  7.91 us
    ppermute x1, starting transfers between devices, extended_2(): lax.ppermute(lax.slice_in_dim(block, block.shape[dim] - width, None, axis...  3.68 us
    ppermute x2, waiting for transfers between devices, butterfly_sum(): value = value + lax.ppermute(value, axis, pairs)  2.91 us
    another operation x42, local copies, waits for them, and re-layouts, scan_and_sum(): tuple(other)  2.88 us
  transfers between devices with their start and end apart: 11, of which 8 were waited for; matrix products, arithmetic and copies ran while one was open for 14% of the time, Pallas kernels for 0%

profile of v4, /device:TPU:3, one launch (start us, length us, event | category | flops | bytes accessed | tf_op | source)
XLA Modules:
  0.0 138.7 jit_solution(12538620759942100556)
XLA Ops:
  0.7 1.2 fusion.83
  1.9 3.7 %collective-permute-start = (bf16[4,136,256]{2,1,0:T(8,128)(2,1)S(1)}, bf16[4,136,256]{2,1,0:T(8,128)(2,1)S(1)}, u32[]{:S(2)}, u32[]{:S(2)}) collective-permute-start(bf16[4,136,256]{2,1,0:T(8,128)(2,1)S(1)} %get-tuple-element.90), channel_id=1, source_target_pairs={{0,1},{1,2},{2,3},{3,4},{4,5},{5,6},{6,7},{7,8},{8,9},{9,10},{10,1... | collective-permute-start | bytes 835592 | tf_op jit(solution)/shard_map/ppermute | solution.py:17
  5.5 1.9 %collective-permute-start.1 = (bf16[4,136,256]{2,1,0:T(8,128)(2,1)S(1)}, bf16[4,136,256]{2,1,0:T(8,128)(2,1)S(1)}, u32[]{:S(2)}, u32[]{:S(2)}) collective-permute-start(bf16[4,136,256]{2,1,0:T(8,128)(2,1)S(1)} %get-tuple-element.89), channel_id=1, source_target_pairs={{1,0},{2,1},{3,2},{4,3},{5,4},{6,5},{7,6},{8,7},{9,8},{10,9},{11,1... | collective-permute-start | bytes 835592 | tf_op jit(solution)/shard_map/ppermute | solution.py:20
  9.1 1.4 fusion.92
  17.2 1.1 copy-done.3
  19.5 2.0 %broadcast_select_fusion.1 = bf16[4,784,256]{2,1,0:T(8,128)(2,1)S(1)} fusion(pred[784]{0:T(1024)(128)(4,1)S(1)} %fusion.64, f32[256]{0:T(256)S(1)} %bitcast.195, s32[]{:T(128)S(6)} %select_n.141, bf16[4,784,256]{2,1,0:T(8,128)(2,1)S(1)} %constant_dynamic-update-slice_fusion, f32[4,784,256]{2,1,0:T(8,128)S(1)} %fusion.3, f32[4,784,256]{2,1,0:T(8,128)S(1)} %fusion.49, ...), kind=kOutput, calls=%fused_computation.21 | convolution fusion | flops 419872768 | bytes 11372548 | tf_op jit(solution)/shard_map/tfw,wv->tfv/dot_general | solution.py:119
  22.7 1.7 %broadcast_select_fusion = bf16[4,784,256]{2,1,0:T(8,128)(2,1)S(1)} fusion(pred[784]{0:T(1024)(128)(4,1)S(1)} %fusion.64, f32[256]{0:T(256)S(1)} %bitcast.194, f32[4,784,256]{2,1,0:T(8,128)S(1)} %fusion.6, f32[4,784,256]{2,1,0:T(8,128)S(1)} %fusion.5, bf16[4,784,256]{2,1,0:T(8,128)(2,1)S(1)} %broadcast_select_fusion.1, ...), kind=kOutput, calls=%fused_computation.20 | convolution fusion | flops 419872768 | bytes 11372544 | tf_op jit(solution)/shard_map/tfw,wv->tfv/dot_general | solution.py:119
  25.7 1.0 negate_exponential_fusion
  27.7 3.4 %collective-permute-start.2 = (f32[256,128]{1,0:T(8,128)S(1)}, f32[256,128]{1,0:T(8,128)S(1)}, u32[]{:S(2)}, u32[]{:S(2)}) collective-permute-start(f32[256,128]{1,0:T(8,128)S(1)} %convolution_bitcast_fusion.1), channel_id=1, source_target_pairs={{0,128},{128,0},{256,384},{384,256},{1,129},{129,1},{257,385},{385... | collective-permute-start | bytes 393224 | tf_op jit(solution)/shard_map/ppermute | solution.py:73
  32.9 1.1 divide_add_fusion.13
  34.0 1.3 divide_add_fusion.12
  35.3 1.3 divide_add_fusion.11
  36.6 1.3 divide_add_fusion.10
  37.9 1.3 divide_add_fusion.9
  39.2 1.3 divide_add_fusion.8
  40.5 1.2 fusion.20
  44.6 4.5 %collective-permute-start.3 = (f32[256,128]{1,0:T(8,128)S(1)}, f32[256,128]{1,0:T(8,128)S(1)}, u32[]{:S(2)}, u32[]{:S(2)}) collective-permute-start(f32[256,128]{1,0:T(8,128)S(1)} %add.963), channel_id=1, source_target_pairs={{0,256},{128,384},{256,0},{384,128},{1,257},{129,385},{257,1},{385... | collective-permute-start | bytes 393224 | tf_op jit(solution)/shard_map/ppermute | solution.py:73
  49.2 2.9 %collective-permute-done.3 = f32[256,128]{1,0:T(8,128)S(1)} collective-permute-done((f32[256,128]{1,0:T(8,128)S(1)}, f32[256,128]{1,0:T(8,128)S(1)}, u32[]{:S(2)}, u32[]{:S(2)}) %collective-permute-start.3) | collective-permute-done | bytes 131104 | tf_op jit(solution)/shard_map/ppermute | solution.py:73
  52.2 3.7 %collective-permute-start.4 = (f32[266,128]{1,0:T(8,128)S(1)}, f32[266,128]{1,0:T(8,128)S(1)}, u32[]{:S(2)}, u32[]{:S(2)}) collective-permute-start(f32[266,128]{1,0:T(8,128)S(1)} %pad_maximum_fusion), channel_id=1, source_target_pairs={{0,1},{1,0},{2,3},{3,2},{4,5},{5,4},{6,7},{7,6},{8,9},{9,8},{10,11... | collective-permute-start | bytes 408584 | tf_op jit(solution)/shard_map/ppermute | solution.py:87
  57.1 4.2 %collective-permute-start.5 = (f32[266,128]{1,0:T(8,128)S(1)}, f32[266,128]{1,0:T(8,128)S(1)}, u32[]{:S(2)}, u32[]{:S(2)}) collective-permute-start(f32[266,128]{1,0:T(8,128)S(1)} %pad_maximum_fusion.1), channel_id=1, source_target_pairs={{0,2},{1,3},{2,0},{3,1},{4,6},{5,7},{6,4},{7,5},{8,10},{9,11},{10,... | collective-permute-start | bytes 408584 | tf_op jit(solution)/shard_map/ppermute | solution.py:87
  61.9 3.2 %collective-permute-done.5 = f32[266,128]{1,0:T(8,128)S(1)} collective-permute-done((f32[266,128]{1,0:T(8,128)S(1)}, f32[266,128]{1,0:T(8,128)S(1)}, u32[]{:S(2)}, u32[]{:S(2)}) %collective-permute-start.5) | collective-permute-done | bytes 136224 | tf_op jit(solution)/shard_map/ppermute | solution.py:87
  65.3 3.0 %collective-permute-start.6 = (f32[266,128]{1,0:T(8,128)S(1)}, f32[266,128]{1,0:T(8,128)S(1)}, u32[]{:S(2)}, u32[]{:S(2)}) collective-permute-start(f32[266,128]{1,0:T(8,128)S(1)} %pad_maximum_fusion.2), channel_id=1, source_target_pairs={{0,4},{1,5},{2,6},{3,7},{4,0},{5,1},{6,2},{7,3},{8,12},{9,13},{10,... | collective-permute-start | bytes 408584 | tf_op jit(solution)/shard_map/ppermute | solution.py:87
  68.8 4.2 %collective-permute-done.6 = f32[266,128]{1,0:T(8,128)S(1)} collective-permute-done((f32[266,128]{1,0:T(8,128)S(1)}, f32[266,128]{1,0:T(8,128)S(1)}, u32[]{:S(2)}, u32[]{:S(2)}) %collective-permute-start.6) | collective-permute-done | bytes 136224 | tf_op jit(solution)/shard_map/ppermute | solution.py:87
  73.3 3.6 %collective-permute-start.7 = (f32[266,128]{1,0:T(8,128)S(1)}, f32[266,128]{1,0:T(8,128)S(1)}, u32[]{:S(2)}, u32[]{:S(2)}) collective-permute-start(f32[266,128]{1,0:T(8,128)S(1)} %pad_maximum_fusion.3), channel_id=1, source_target_pairs={{0,8},{8,0},{16,24},{24,16},{32,40},{40,32},{48,56},{56,48},{64,72... | collective-permute-start | bytes 408584 | tf_op jit(solution)/shard_map/ppermute | solution.py:87
  77.4 1.9 %collective-permute-done.7 = f32[266,128]{1,0:T(8,128)S(1)} collective-permute-done((f32[266,128]{1,0:T(8,128)S(1)}, f32[266,128]{1,0:T(8,128)S(1)}, u32[]{:S(2)}, u32[]{:S(2)}) %collective-permute-start.7) | collective-permute-done | bytes 136224 | tf_op jit(solution)/shard_map/ppermute | solution.py:87
  79.6 4.9 %collective-permute-start.8 = (f32[266,128]{1,0:T(8,128)S(1)}, f32[266,128]{1,0:T(8,128)S(1)}, u32[]{:S(2)}, u32[]{:S(2)}) collective-permute-start(f32[266,128]{1,0:T(8,128)S(1)} %pad_maximum_fusion.4), channel_id=1, source_target_pairs={{0,16},{8,24},{16,0},{24,8},{32,48},{40,56},{48,32},{56,40},{64,80... | collective-permute-start | bytes 408584 | tf_op jit(solution)/shard_map/ppermute | solution.py:87
  85.0 3.7 %collective-permute-done.8 = f32[266,128]{1,0:T(8,128)S(1)} collective-permute-done((f32[266,128]{1,0:T(8,128)S(1)}, f32[266,128]{1,0:T(8,128)S(1)}, u32[]{:S(2)}, u32[]{:S(2)}) %collective-permute-start.8) | collective-permute-done | bytes 136224 | tf_op jit(solution)/shard_map/ppermute | solution.py:87
  89.1 8.9 %collective-permute-start.9 = (f32[266,128]{1,0:T(8,128)S(1)}, f32[266,128]{1,0:T(8,128)S(1)}, u32[]{:S(2)}, u32[]{:S(2)}) collective-permute-start(f32[266,128]{1,0:T(8,128)S(1)} %pad_maximum_fusion.5), channel_id=1, source_target_pairs={{0,32},{8,40},{16,48},{24,56},{32,0},{40,8},{48,16},{56,24},{64,96... | collective-permute-start | bytes 408584 | tf_op jit(solution)/shard_map/ppermute | solution.py:87
  98.5 12.5 %collective-permute-done.9 = f32[266,128]{1,0:T(8,128)S(1)} collective-permute-done((f32[266,128]{1,0:T(8,128)S(1)}, f32[266,128]{1,0:T(8,128)S(1)}, u32[]{:S(2)}, u32[]{:S(2)}) %collective-permute-start.9) | collective-permute-done | bytes 136224 | tf_op jit(solution)/shard_map/ppermute | solution.py:87
  111.3 13.8 %collective-permute-start.10 = (f32[266,128]{1,0:T(8,128)S(1)}, f32[266,128]{1,0:T(8,128)S(1)}, u32[]{:S(2)}, u32[]{:S(2)}) collective-permute-start(f32[266,128]{1,0:T(8,128)S(1)} %pad_maximum_fusion.6), channel_id=1, source_target_pairs={{0,64},{8,72},{16,80},{24,88},{32,96},{40,104},{48,112},{56,120},{... | collective-permute-start | bytes 408584 | tf_op jit(solution)/shard_map/ppermute | solution.py:87
  125.6 10.9 %collective-permute-done.10 = f32[266,128]{1,0:T(8,128)S(1)} collective-permute-done((f32[266,128]{1,0:T(8,128)S(1)}, f32[266,128]{1,0:T(8,128)S(1)}, u32[]{:S(2)}, u32[]{:S(2)}) %collective-permute-start.10) | collective-permute-done | bytes 136224 | tf_op jit(solution)/shard_map/ppermute | solution.py:87
  137.0 1.0 divide_add_fusion
  (214 shorter events, 18.3 us)
Async XLA Ops:
  0.6 26.5 %copy-start = (bf16[4,512,128]{2,1,0:T(8,128)(2,1)S(1)}, bf16[4,512,128]{2,1,0:T(8,128)(2,1)}, u32[]{:S(2)}) copy-start(bf16[4,512,128]{2,1,0:T(8,128)(2,1)} %param.19) | copy-start | bytes 1572868
  0.6 16.5 %copy-start.2 = (bf16[4,512,256]{2,1,0:T(8,128)(2,1)S(1)}, bf16[4,512,256]{2,1,0:T(8,128)(2,1)}, u32[]{:S(2)}) copy-start(bf16[4,512,256]{2,1,0:T(8,128)(2,1)} %param.11) | copy-start | bytes 3145732
  1.9 15.2 %collective-permute-start = (bf16[4,136,256]{2,1,0:T(8,128)(2,1)S(1)}, bf16[4,136,256]{2,1,0:T(8,128)(2,1)S(1)}, u32[]{:S(2)}, u32[]{:S(2)}) collective-permute-start(bf16[4,136,256]{2,1,0:T(8,128)(2,1)S(1)} %get-tuple-element.90), channel_id=1, source_target_pairs={{0,1},{1,2},{2,3},{3,4},{4,5},{5,6},{6,7},{7,8},{8,9},{9,10},{10,1... | collective-permute-start | bytes 835592 | tf_op jit(solution)/shard_map/ppermute | solution.py:17
  5.5 11.6 %collective-permute-start.1 = (bf16[4,136,256]{2,1,0:T(8,128)(2,1)S(1)}, bf16[4,136,256]{2,1,0:T(8,128)(2,1)S(1)}, u32[]{:S(2)}, u32[]{:S(2)}) collective-permute-start(bf16[4,136,256]{2,1,0:T(8,128)(2,1)S(1)} %get-tuple-element.89), channel_id=1, source_target_pairs={{1,0},{2,1},{3,2},{4,3},{5,4},{6,5},{7,6},{8,7},{9,8},{10,9},{11,1... | collective-permute-start | bytes 835592 | tf_op jit(solution)/shard_map/ppermute | solution.py:20
  17.1 1.3 copy-start.3
  27.2 3.9 %copy-start.4 = (bf16[256,128]{1,0:T(8,128)(2,1)S(1)}, bf16[256,128]{1,0:T(8,128)(2,1)}, u32[]{:S(2)}) copy-start(bf16[256,128]{1,0:T(8,128)(2,1)} %param.15) | copy-start | bytes 196612
  27.7 4.3 %copy-start.5 = (f32[4,512]{1,0:T(4,128)S(1)}, f32[4,512]{1,0:T(4,128)}, u32[]{:S(2)}) copy-start(f32[4,512]{1,0:T(4,128)} %param.17) | copy-start | bytes 24580
  27.7 16.9 %collective-permute-start.2 = (f32[256,128]{1,0:T(8,128)S(1)}, f32[256,128]{1,0:T(8,128)S(1)}, u32[]{:S(2)}, u32[]{:S(2)}) collective-permute-start(f32[256,128]{1,0:T(8,128)S(1)} %convolution_bitcast_fusion.1), channel_id=1, source_target_pairs={{0,128},{128,0},{256,384},{384,256},{1,129},{129,1},{257,385},{385... | collective-permute-start | bytes 393224 | tf_op jit(solution)/shard_map/ppermute | solution.py:73
  43.7 18.2 %copy-start.6 = (f32[5,4,64]{2,1,0:T(4,128)S(1)}, f32[5,4,64]{2,1,0:T(4,128)}, u32[]{:S(2)}) copy-start(f32[5,4,64]{2,1,0:T(4,128)} %constant.123.clone.1) | copy-start | bytes 15364
  44.6 7.5 %collective-permute-start.3 = (f32[256,128]{1,0:T(8,128)S(1)}, f32[256,128]{1,0:T(8,128)S(1)}, u32[]{:S(2)}, u32[]{:S(2)}) collective-permute-start(f32[256,128]{1,0:T(8,128)S(1)} %add.963), channel_id=1, source_target_pairs={{0,256},{128,384},{256,0},{384,128},{1,257},{129,385},{257,1},{385... | collective-permute-start | bytes 393224 | tf_op jit(solution)/shard_map/ppermute | solution.py:73
  52.2 4.7 %collective-permute-start.4 = (f32[266,128]{1,0:T(8,128)S(1)}, f32[266,128]{1,0:T(8,128)S(1)}, u32[]{:S(2)}, u32[]{:S(2)}) collective-permute-start(f32[266,128]{1,0:T(8,128)S(1)} %pad_maximum_fusion), channel_id=1, source_target_pairs={{0,1},{1,0},{2,3},{3,2},{4,5},{5,4},{6,7},{7,6},{8,9},{9,8},{10,11... | collective-permute-start | bytes 408584 | tf_op jit(solution)/shard_map/ppermute | solution.py:87
  57.1 7.9 %collective-permute-start.5 = (f32[266,128]{1,0:T(8,128)S(1)}, f32[266,128]{1,0:T(8,128)S(1)}, u32[]{:S(2)}, u32[]{:S(2)}) collective-permute-start(f32[266,128]{1,0:T(8,128)S(1)} %pad_maximum_fusion.1), channel_id=1, source_target_pairs={{0,2},{1,3},{2,0},{3,1},{4,6},{5,7},{6,4},{7,5},{8,10},{9,11},{10,... | collective-permute-start | bytes 408584 | tf_op jit(solution)/shard_map/ppermute | solution.py:87
  65.3 7.7 %collective-permute-start.6 = (f32[266,128]{1,0:T(8,128)S(1)}, f32[266,128]{1,0:T(8,128)S(1)}, u32[]{:S(2)}, u32[]{:S(2)}) collective-permute-start(f32[266,128]{1,0:T(8,128)S(1)} %pad_maximum_fusion.2), channel_id=1, source_target_pairs={{0,4},{1,5},{2,6},{3,7},{4,0},{5,1},{6,2},{7,3},{8,12},{9,13},{10,... | collective-permute-start | bytes 408584 | tf_op jit(solution)/shard_map/ppermute | solution.py:87
  73.3 6.0 %collective-permute-start.7 = (f32[266,128]{1,0:T(8,128)S(1)}, f32[266,128]{1,0:T(8,128)S(1)}, u32[]{:S(2)}, u32[]{:S(2)}) collective-permute-start(f32[266,128]{1,0:T(8,128)S(1)} %pad_maximum_fusion.3), channel_id=1, source_target_pairs={{0,8},{8,0},{16,24},{24,16},{32,40},{40,32},{48,56},{56,48},{64,72... | collective-permute-start | bytes 408584 | tf_op jit(solution)/shard_map/ppermute | solution.py:87
  79.6 9.2 %collective-permute-start.8 = (f32[266,128]{1,0:T(8,128)S(1)}, f32[266,128]{1,0:T(8,128)S(1)}, u32[]{:S(2)}, u32[]{:S(2)}) collective-permute-start(f32[266,128]{1,0:T(8,128)S(1)} %pad_maximum_fusion.4), channel_id=1, source_target_pairs={{0,16},{8,24},{16,0},{24,8},{32,48},{40,56},{48,32},{56,40},{64,80... | collective-permute-start | bytes 408584 | tf_op jit(solution)/shard_map/ppermute | solution.py:87
  89.1 21.9 %collective-permute-start.9 = (f32[266,128]{1,0:T(8,128)S(1)}, f32[266,128]{1,0:T(8,128)S(1)}, u32[]{:S(2)}, u32[]{:S(2)}) collective-permute-start(f32[266,128]{1,0:T(8,128)S(1)} %pad_maximum_fusion.5), channel_id=1, source_target_pairs={{0,32},{8,40},{16,48},{24,56},{32,0},{40,8},{48,16},{56,24},{64,96... | collective-permute-start | bytes 408584 | tf_op jit(solution)/shard_map/ppermute | solution.py:87
  111.3 25.2 %collective-permute-start.10 = (f32[266,128]{1,0:T(8,128)S(1)}, f32[266,128]{1,0:T(8,128)S(1)}, u32[]{:S(2)}, u32[]{:S(2)}) collective-permute-start(f32[266,128]{1,0:T(8,128)S(1)} %pad_maximum_fusion.6), channel_id=1, source_target_pairs={{0,64},{8,72},{16,80},{24,88},{32,96},{40,104},{48,112},{56,120},{... | collective-permute-start | bytes 408584 | tf_op jit(solution)/shard_map/ppermute | solution.py:87
  125.4 13.2 %copy-start.1 = (bf16[4,512,128]{2,1,0:T(8,128)(2,1)S(1)}, bf16[4,512,128]{2,1,0:T(8,128)(2,1)}, u32[]{:S(2)}) copy-start(bf16[4,512,128]{2,1,0:T(8,128)(2,1)} %param.19) | copy-start | bytes 1572868

commit v5 on v4

--- a/solution.py
+++ b/solution.py
@@ -65,34 +65,67 @@
     return result
 
 
-def butterfly_sum(value, axis):
+def radices(count):
+    sizes = []
+    while count > 1:
+        size = 2 if count % 4 else 4
+        sizes.append(size)
+        count = count // size
+    if len(sizes) > 1 and sizes[-1] == 2:
+        sizes = sizes[-1:] + sizes[:-1]
+    return sizes
+
+
+def digit_round(own, axis, radix, step):
     count = lax.axis_size(axis)
+    digit = (lax.axis_index(axis) // step) % radix
+    received = [
+        lax.ppermute(own, axis, [(i, i ^ (k * step)) for i in range(count)])
+        for k in range(1, radix)
+    ]
+    slots = []
+    for j in range(radix):
+        value = own
+        for k in range(1, radix):
+            value = jnp.where(digit == (j ^ k), received[k - 1], value)
+        slots.append(value)
+    return digit, slots
+
+
+def group_sum(value, axis):
     step = 1
-    while step < count:
-        pairs = [(i, i ^ step) for i in range(count)]
-        value = value + lax.ppermute(value, axis, pairs)
-        step = step * 2
+    for radix in radices(lax.axis_size(axis)):
+        _, slots = digit_round(value, axis, radix, step)
+        value = slots[0]
+        for item in slots[1:]:
+            value = value + item
+        step = step * radix
     return value
 
 
 def scan_and_sum(totals, grad, axes):
     prefix = jnp.zeros_like(totals).at[0].set(1.0)
+    rows = grad.shape[0]
     for axis in axes:
-        count = lax.axis_size(axis)
-        place = lax.axis_index(axis)
         step = 1
-        while step < count:
-            pairs = [(i, i ^ step) for i in range(count)]
+        for radix in radices(lax.axis_size(axis)):
             packed = jnp.concatenate([grad, totals.reshape(-1, grad.shape[1])])
-            packed = lax.ppermute(packed, axis, pairs)
-            other = packed[grad.shape[0] :].reshape(totals.shape)
-            grad = grad + packed[: grad.shape[0]]
-            lower = (place & step) != 0
-            prefix = jnp.where(lower, jnp.stack(combine(tuple(other), tuple(prefix))), prefix)
-            early = jnp.where(lower, other, totals)
-            late = jnp.where(lower, totals, other)
-            totals = jnp.stack(combine(tuple(early), tuple(late)))
-            step = step * 2
+            digit, slots = digit_round(packed, axis, radix, step)
+            grad = slots[0][:rows]
+            for item in slots[1:]:
+                grad = grad + item[:rows]
+            parts = [item[rows:].reshape(totals.shape) for item in slots]
+            earlier = [jnp.zeros_like(totals).at[0].set(1.0)]
+            running = parts[0]
+            for item in parts[1:]:
+                earlier.append(running)
+                running = jnp.stack(combine(tuple(running), tuple(item)))
+            totals = running
+            chosen = earlier[0]
+            for j in range(1, radix):
+                chosen = jnp.where(digit == j, earlier[j], chosen)
+            prefix = jnp.stack(combine(tuple(chosen), tuple(prefix)))
+            step = step * radix
     return prefix, grad
 
 def elements(obs, logp, params, present, keep, first):
@@ -166,7 +199,7 @@
     grad_local = jnp.einsum(
         "tfw,tfs->ws", hidden, head_cotangent, preferred_element_type=jnp.float32
     )
-    grad_local = butterfly_sum(grad_local, "take")
+    grad_local = group_sum(grad_local, "take")
     local = doubling_prefix(elems, 2)
     totals = jnp.stack([item[:, :, -1] for item in local])
     prefix, head_grad = scan_and_sum(totals, grad_local, ("inner", "outer"))

time: 139 us -> 141 us (1.014)
  the two profiles are of different devices: /device:TPU:3 before, /device:TPU:1 now
where the time goes in v5:
time: 141 us; the launch traced here: 140 us
  starting transfers between devices  60.5 us (43%)
  waiting for transfers between devices  33.3 us (24%)
  other arithmetic  16.8 us (12%)
  local copies, waits for them, and re-layouts  12.4 us (9%)
  matrix products  9.26 us (7%)
  between operations  7.21 us (5%)
    ppermute x13, starting transfers between devices, digit_round(): lax.ppermute(own, axis, [(i, i ^ k * step) for i in range(count)])  50.4 us
    ppermute x13, waiting for transfers between devices, digit_round(): lax.ppermute(own, axis, [(i, i ^ k * step) for i in range(count)])  33.3 us
    add x9, other arithmetic, combine(): new_c = a_two * a_two * c_one / denom + c_two  9.6 us
    dot_general x9, matrix products, conv_layer(): jnp.einsum('tfw,wv->tfv', piece, weights[tap], preferred_element_type=jnp...  8.3 us
    ppermute x1, starting transfers between devices, extended_2(): lax.ppermute(lax.slice_in_dim(block, 0, width, axis=dim), axis, backward)  5.56 us
    another operation x80, local copies, waits for them, and re-layouts, scan_and_sum(): running = jnp.stack(combine(tuple(running), tuple(item)))  5.36 us
    ppermute x1, starting transfers between devices, extended_2(): lax.ppermute(lax.slice_in_dim(block, block.shape[dim] - width, None, axis...  4.5 us
  transfers between devices with their start and end apart: 15, of which 7 were waited for; matrix products, arithmetic and copies ran while one was open for 12% of the time, Pallas kernels for 0%

profile of v5, /device:TPU:1, one launch (start us, length us, event | category | flops | bytes accessed | tf_op | source)
XLA Modules:
  0.0 139.5 jit_solution(2665390176700196945)
XLA Ops:
  0.7 1.2 fusion.99
  1.9 4.5 %collective-permute-start = (bf16[4,136,256]{2,1,0:T(8,128)(2,1)S(1)}, bf16[4,136,256]{2,1,0:T(8,128)(2,1)S(1)}, u32[]{:S(2)}, u32[]{:S(2)}) collective-permute-start(bf16[4,136,256]{2,1,0:T(8,128)(2,1)S(1)} %get-tuple-element.154), channel_id=1, source_target_pairs={{0,1},{1,2},{2,3},{3,4},{4,5},{5,6},{6,7},{7,8},{8,9},{9,10},{10,1... | collective-permute-start | bytes 835592 | tf_op jit(solution)/shard_map/ppermute | solution.py:17
  6.4 5.6 %collective-permute-start.1 = (bf16[4,136,256]{2,1,0:T(8,128)(2,1)S(1)}, bf16[4,136,256]{2,1,0:T(8,128)(2,1)S(1)}, u32[]{:S(2)}, u32[]{:S(2)}) collective-permute-start(bf16[4,136,256]{2,1,0:T(8,128)(2,1)S(1)} %get-tuple-element.153), channel_id=1, source_target_pairs={{1,0},{2,1},{3,2},{4,3},{5,4},{6,5},{7,6},{8,7},{9,8},{10,9},{11,1... | collective-permute-start | bytes 835592 | tf_op jit(solution)/shard_map/ppermute | solution.py:20
  13.5 1.4 fusion.115
  21.5 1.1 copy-done.3
  23.8 2.0 %broadcast_select_fusion.1 = bf16[4,784,256]{2,1,0:T(8,128)(2,1)S(1)} fusion(pred[784]{0:T(1024)(128)(4,1)S(1)} %fusion.69, f32[256]{0:T(256)S(1)} %bitcast.287, s32[]{:T(128)S(6)} %select_n.394, bf16[4,784,256]{2,1,0:T(8,128)(2,1)S(1)} %constant_dynamic-update-slice_fusion, f32[4,784,256]{2,1,0:T(8,128)S(1)} %fusion.3, f32[4,784,256]{2,1,0:T(8,128)S(1)} %fusion.54, ...), kind=kOutput, calls=%fused_computation.21 | convolution fusion | flops 419872768 | bytes 11372548 | tf_op jit(solution)/shard_map/tfw,wv->tfv/dot_general | solution.py:152
  27.0 1.7 %broadcast_select_fusion = bf16[4,784,256]{2,1,0:T(8,128)(2,1)S(1)} fusion(pred[784]{0:T(1024)(128)(4,1)S(1)} %fusion.69, f32[256]{0:T(256)S(1)} %bitcast.286, f32[4,784,256]{2,1,0:T(8,128)S(1)} %fusion.6, f32[4,784,256]{2,1,0:T(8,128)S(1)} %fusion.5, bf16[4,784,256]{2,1,0:T(8,128)(2,1)S(1)} %broadcast_select_fusion.1, ...), kind=kOutput, calls=%fused_computation.20 | convolution fusion | flops 419872768 | bytes 11372544 | tf_op jit(solution)/shard_map/tfw,wv->tfv/dot_general | solution.py:152
  31.9 1.9 %collective-permute-start.2 = (f32[256,128]{1,0:T(8,128)S(1)}, f32[256,128]{1,0:T(8,128)S(1)}, u32[]{:S(2)}, u32[]{:S(2)}) collective-permute-start(f32[256,128]{1,0:T(8,128)S(1)} %convolution_bitcast_fusion.1), channel_id=1, source_target_pairs={{0,384},{128,256},{256,128},{384,0},{1,385},{129,257},{257,129},{3... | collective-permute-start | bytes 393224 | tf_op jit(solution)/shard_map/ppermute | solution.py:83
  33.9 1.9 %collective-permute-start.3 = (f32[256,128]{1,0:T(8,128)S(1)}, f32[256,128]{1,0:T(8,128)S(1)}, u32[]{:S(2)}, u32[]{:S(2)}) collective-permute-start(f32[256,128]{1,0:T(8,128)S(1)} %convolution_bitcast_fusion.1), channel_id=1, source_target_pairs={{0,256},{128,384},{256,0},{384,128},{1,257},{129,385},{257,1},{385... | collective-permute-start | bytes 393224 | tf_op jit(solution)/shard_map/ppermute | solution.py:83
  35.8 5.3 %collective-permute-start.4 = (f32[256,128]{1,0:T(8,128)S(1)}, f32[256,128]{1,0:T(8,128)S(1)}, u32[]{:S(2)}, u32[]{:S(2)}) collective-permute-start(f32[256,128]{1,0:T(8,128)S(1)} %convolution_bitcast_fusion.1), channel_id=1, source_target_pairs={{0,128},{128,0},{256,384},{384,256},{1,129},{129,1},{257,385},{385... | collective-permute-start | bytes 393224 | tf_op jit(solution)/shard_map/ppermute | solution.py:83
  44.0 1.3 divide_add_fusion.12
  45.3 1.3 divide_add_fusion.11
  46.6 1.3 divide_add_fusion.10
  47.9 1.3 divide_add_fusion.9
  49.2 1.3 divide_add_fusion.8
  50.6 1.2 fusion.20
  54.8 2.1 %collective-permute-start.5 = (f32[266,128]{1,0:T(8,128)S(1)}, f32[266,128]{1,0:T(8,128)S(1)}, u32[]{:S(2)}, u32[]{:S(2)}) collective-permute-start(f32[266,128]{1,0:T(8,128)S(1)} %pad_maximum_fusion.1), channel_id=1, source_target_pairs={{0,1},{1,0},{2,3},{3,2},{4,5},{5,4},{6,7},{7,6},{8,9},{9,8},{10,11... | collective-permute-start | bytes 408584 | tf_op jit(solution)/shard_map/ppermute | solution.py:83
  56.9 1.1 collective-permute-done.5
  59.1 1.9 %collective-permute-start.6 = (f32[266,128]{1,0:T(8,128)S(1)}, f32[266,128]{1,0:T(8,128)S(1)}, u32[]{:S(2)}, u32[]{:S(2)}) collective-permute-start(f32[266,128]{1,0:T(8,128)S(1)} %pad_maximum_fusion.2), channel_id=1, source_target_pairs={{0,6},{1,7},{2,4},{3,5},{4,2},{5,3},{6,0},{7,1},{8,14},{9,15},{10,... | collective-permute-start | bytes 408584 | tf_op jit(solution)/shard_map/ppermute | solution.py:83
  61.1 2.4 %collective-permute-start.7 = (f32[266,128]{1,0:T(8,128)S(1)}, f32[266,128]{1,0:T(8,128)S(1)}, u32[]{:S(2)}, u32[]{:S(2)}) collective-permute-start(f32[266,128]{1,0:T(8,128)S(1)} %pad_maximum_fusion.2), channel_id=1, source_target_pairs={{0,4},{1,5},{2,6},{3,7},{4,0},{5,1},{6,2},{7,3},{8,12},{9,13},{10,... | collective-permute-start | bytes 408584 | tf_op jit(solution)/shard_map/ppermute | solution.py:83
  63.4 4.7 %collective-permute-start.8 = (f32[266,128]{1,0:T(8,128)S(1)}, f32[266,128]{1,0:T(8,128)S(1)}, u32[]{:S(2)}, u32[]{:S(2)}) collective-permute-start(f32[266,128]{1,0:T(8,128)S(1)} %pad_maximum_fusion.2), channel_id=1, source_target_pairs={{0,2},{1,3},{2,0},{3,1},{4,6},{5,7},{6,4},{7,5},{8,10},{9,11},{10,... | collective-permute-start | bytes 408584 | tf_op jit(solution)/shard_map/ppermute | solution.py:83
  69.2 3.3 %collective-permute-done.8 = f32[266,128]{1,0:T(8,128)S(1)} collective-permute-done((f32[266,128]{1,0:T(8,128)S(1)}, f32[266,128]{1,0:T(8,128)S(1)}, u32[]{:S(2)}, u32[]{:S(2)}) %collective-permute-start.8) | collective-permute-done | bytes 136224 | tf_op jit(solution)/shard_map/ppermute | solution.py:83
  74.6 4.4 %collective-permute-start.10 = (f32[266,128]{1,0:T(8,128)S(1)}, f32[266,128]{1,0:T(8,128)S(1)}, u32[]{:S(2)}, u32[]{:S(2)}) collective-permute-start(f32[266,128]{1,0:T(8,128)S(1)} %pad_maximum_fusion.3), channel_id=1, source_target_pairs={{0,16},{8,24},{16,0},{24,8},{32,48},{40,56},{48,32},{56,40},{64,80... | collective-permute-start | bytes 408584 | tf_op jit(solution)/shard_map/ppermute | solution.py:83
  79.0 3.5 %collective-permute-start.11 = (f32[266,128]{1,0:T(8,128)S(1)}, f32[266,128]{1,0:T(8,128)S(1)}, u32[]{:S(2)}, u32[]{:S(2)}) collective-permute-start(f32[266,128]{1,0:T(8,128)S(1)} %pad_maximum_fusion.3), channel_id=1, source_target_pairs={{0,8},{8,0},{16,24},{24,16},{32,40},{40,32},{48,56},{56,48},{64,72... | collective-permute-start | bytes 408584 | tf_op jit(solution)/shard_map/ppermute | solution.py:83
  82.5 1.9 %collective-permute-start.9 = (f32[266,128]{1,0:T(8,128)S(1)}, f32[266,128]{1,0:T(8,128)S(1)}, u32[]{:S(2)}, u32[]{:S(2)}) collective-permute-start(f32[266,128]{1,0:T(8,128)S(1)} %pad_maximum_fusion.3), channel_id=1, source_target_pairs={{0,24},{8,16},{16,8},{24,0},{32,56},{40,48},{48,40},{56,32},{64,88... | collective-permute-start | bytes 408584 | tf_op jit(solution)/shard_map/ppermute | solution.py:83
  84.5 2.6 %collective-permute-done.11 = f32[266,128]{1,0:T(8,128)S(1)} collective-permute-done((f32[266,128]{1,0:T(8,128)S(1)}, f32[266,128]{1,0:T(8,128)S(1)}, u32[]{:S(2)}, u32[]{:S(2)}) %collective-permute-start.11) | collective-permute-done | bytes 136224 | tf_op jit(solution)/shard_map/ppermute | solution.py:83
  87.1 3.1 %collective-permute-done.9 = f32[266,128]{1,0:T(8,128)S(1)} collective-permute-done((f32[266,128]{1,0:T(8,128)S(1)}, f32[266,128]{1,0:T(8,128)S(1)}, u32[]{:S(2)}, u32[]{:S(2)}) %collective-permute-start.9) | collective-permute-done | bytes 136224 | tf_op jit(solution)/shard_map/ppermute | solution.py:83
  92.3 11.4 %collective-permute-start.12 = (f32[266,128]{1,0:T(8,128)S(1)}, f32[266,128]{1,0:T(8,128)S(1)}, u32[]{:S(2)}, u32[]{:S(2)}) collective-permute-start(f32[266,128]{1,0:T(8,128)S(1)} %pad_maximum_fusion), channel_id=1, source_target_pairs={{0,96},{8,104},{16,112},{24,120},{32,64},{40,72},{48,80},{56,88},{... | collective-permute-start | bytes 408584 | tf_op jit(solution)/shard_map/ppermute | solution.py:83
  103.7 4.9 %collective-permute-start.13 = (f32[266,128]{1,0:T(8,128)S(1)}, f32[266,128]{1,0:T(8,128)S(1)}, u32[]{:S(2)}, u32[]{:S(2)}) collective-permute-start(f32[266,128]{1,0:T(8,128)S(1)} %pad_maximum_fusion), channel_id=1, source_target_pairs={{0,64},{8,72},{16,80},{24,88},{32,96},{40,104},{48,112},{56,120},{... | collective-permute-start | bytes 408584 | tf_op jit(solution)/shard_map/ppermute | solution.py:83
  108.6 4.0 %collective-permute-start.14 = (f32[266,128]{1,0:T(8,128)S(1)}, f32[266,128]{1,0:T(8,128)S(1)}, u32[]{:S(2)}, u32[]{:S(2)}) collective-permute-start(f32[266,128]{1,0:T(8,128)S(1)} %pad_maximum_fusion), channel_id=1, source_target_pairs={{0,32},{8,40},{16,48},{24,56},{32,0},{40,8},{48,16},{56,24},{64,96... | collective-permute-start | bytes 408584 | tf_op jit(solution)/shard_map/ppermute | solution.py:83
  112.7 4.5 %collective-permute-done.12 = f32[266,128]{1,0:T(8,128)S(1)} collective-permute-done((f32[266,128]{1,0:T(8,128)S(1)}, f32[266,128]{1,0:T(8,128)S(1)}, u32[]{:S(2)}, u32[]{:S(2)}) %collective-permute-start.12) | collective-permute-done | bytes 136224 | tf_op jit(solution)/shard_map/ppermute | solution.py:83
  117.2 17.7 %collective-permute-done.13 = f32[266,128]{1,0:T(8,128)S(1)} collective-permute-done((f32[266,128]{1,0:T(8,128)S(1)}, f32[266,128]{1,0:T(8,128)S(1)}, u32[]{:S(2)}, u32[]{:S(2)}) %collective-permute-start.13) | collective-permute-done | bytes 136224 | tf_op jit(solution)/shard_map/ppermute | solution.py:83
  (225 shorter events, 24.6 us)
Async XLA Ops:
  0.6 30.8 %copy-start = (bf16[4,512,128]{2,1,0:T(8,128)(2,1)S(1)}, bf16[4,512,128]{2,1,0:T(8,128)(2,1)}, u32[]{:S(2)}) copy-start(bf16[4,512,128]{2,1,0:T(8,128)(2,1)} %param.27) | copy-start | bytes 1572868
  0.6 20.7 %copy-start.2 = (bf16[4,512,256]{2,1,0:T(8,128)(2,1)S(1)}, bf16[4,512,256]{2,1,0:T(8,128)(2,1)}, u32[]{:S(2)}) copy-start(bf16[4,512,256]{2,1,0:T(8,128)(2,1)} %param.19) | copy-start | bytes 3145732
  1.9 19.5 %collective-permute-start = (bf16[4,136,256]{2,1,0:T(8,128)(2,1)S(1)}, bf16[4,136,256]{2,1,0:T(8,128)(2,1)S(1)}, u32[]{:S(2)}, u32[]{:S(2)}) collective-permute-start(bf16[4,136,256]{2,1,0:T(8,128)(2,1)S(1)} %get-tuple-element.154), channel_id=1, source_target_pairs={{0,1},{1,2},{2,3},{3,4},{4,5},{5,6},{6,7},{7,8},{8,9},{9,10},{10,1... | collective-permute-start | bytes 835592 | tf_op jit(solution)/shard_map/ppermute | solution.py:17
  6.4 15.1 %collective-permute-start.1 = (bf16[4,136,256]{2,1,0:T(8,128)(2,1)S(1)}, bf16[4,136,256]{2,1,0:T(8,128)(2,1)S(1)}, u32[]{:S(2)}, u32[]{:S(2)}) collective-permute-start(bf16[4,136,256]{2,1,0:T(8,128)(2,1)S(1)} %get-tuple-element.153), channel_id=1, source_target_pairs={{1,0},{2,1},{3,2},{4,3},{5,4},{6,5},{7,6},{8,7},{9,8},{10,9},{11,1... | collective-permute-start | bytes 835592 | tf_op jit(solution)/shard_map/ppermute | solution.py:20
  21.3 1.3 copy-start.3
  31.4 9.7 %copy-start.8 = (bf16[256,128]{1,0:T(8,128)(2,1)S(1)}, bf16[256,128]{1,0:T(8,128)(2,1)}, u32[]{:S(2)}) copy-start(bf16[256,128]{1,0:T(8,128)(2,1)} %param.23) | copy-start | bytes 196612
  31.9 10.1 %copy-start.9 = (f32[4,512]{1,0:T(4,128)S(1)}, f32[4,512]{1,0:T(4,128)}, u32[]{:S(2)}) copy-start(f32[4,512]{1,0:T(4,128)} %param.25) | copy-start | bytes 24580
  31.9 22.8 %collective-permute-start.2 = (f32[256,128]{1,0:T(8,128)S(1)}, f32[256,128]{1,0:T(8,128)S(1)}, u32[]{:S(2)}, u32[]{:S(2)}) collective-permute-start(f32[256,128]{1,0:T(8,128)S(1)} %convolution_bitcast_fusion.1), channel_id=1, source_target_pairs={{0,384},{128,256},{256,128},{384,0},{1,385},{129,257},{257,129},{3... | collective-permute-start | bytes 393224 | tf_op jit(solution)/shard_map/ppermute | solution.py:83
  33.9 20.8 %collective-permute-start.3 = (f32[256,128]{1,0:T(8,128)S(1)}, f32[256,128]{1,0:T(8,128)S(1)}, u32[]{:S(2)}, u32[]{:S(2)}) collective-permute-start(f32[256,128]{1,0:T(8,128)S(1)} %convolution_bitcast_fusion.1), channel_id=1, source_target_pairs={{0,256},{128,384},{256,0},{384,128},{1,257},{129,385},{257,1},{385... | collective-permute-start | bytes 393224 | tf_op jit(solution)/shard_map/ppermute | solution.py:83
  35.8 18.9 %collective-permute-start.4 = (f32[256,128]{1,0:T(8,128)S(1)}, f32[256,128]{1,0:T(8,128)S(1)}, u32[]{:S(2)}, u32[]{:S(2)}) collective-permute-start(f32[256,128]{1,0:T(8,128)S(1)} %convolution_bitcast_fusion.1), channel_id=1, source_target_pairs={{0,128},{128,0},{256,384},{384,256},{1,129},{129,1},{257,385},{385... | collective-permute-start | bytes 393224 | tf_op jit(solution)/shard_map/ppermute | solution.py:83
  54.8 3.3 %collective-permute-start.5 = (f32[266,128]{1,0:T(8,128)S(1)}, f32[266,128]{1,0:T(8,128)S(1)}, u32[]{:S(2)}, u32[]{:S(2)}) collective-permute-start(f32[266,128]{1,0:T(8,128)S(1)} %pad_maximum_fusion.1), channel_id=1, source_target_pairs={{0,1},{1,0},{2,3},{3,2},{4,5},{5,4},{6,7},{7,6},{8,9},{9,8},{10,11... | collective-permute-start | bytes 408584 | tf_op jit(solution)/shard_map/ppermute | solution.py:83
  59.1 9.0 %collective-permute-start.6 = (f32[266,128]{1,0:T(8,128)S(1)}, f32[266,128]{1,0:T(8,128)S(1)}, u32[]{:S(2)}, u32[]{:S(2)}) collective-permute-start(f32[266,128]{1,0:T(8,128)S(1)} %pad_maximum_fusion.2), channel_id=1, source_target_pairs={{0,6},{1,7},{2,4},{3,5},{4,2},{5,3},{6,0},{7,1},{8,14},{9,15},{10,... | collective-permute-start | bytes 408584 | tf_op jit(solution)/shard_map/ppermute | solution.py:83
  61.1 8.2 %collective-permute-start.7 = (f32[266,128]{1,0:T(8,128)S(1)}, f32[266,128]{1,0:T(8,128)S(1)}, u32[]{:S(2)}, u32[]{:S(2)}) collective-permute-start(f32[266,128]{1,0:T(8,128)S(1)} %pad_maximum_fusion.2), channel_id=1, source_target_pairs={{0,4},{1,5},{2,6},{3,7},{4,0},{5,1},{6,2},{7,3},{8,12},{9,13},{10,... | collective-permute-start | bytes 408584 | tf_op jit(solution)/shard_map/ppermute | solution.py:83
  63.4 9.0 %collective-permute-start.8 = (f32[266,128]{1,0:T(8,128)S(1)}, f32[266,128]{1,0:T(8,128)S(1)}, u32[]{:S(2)}, u32[]{:S(2)}) collective-permute-start(f32[266,128]{1,0:T(8,128)S(1)} %pad_maximum_fusion.2), channel_id=1, source_target_pairs={{0,2},{1,3},{2,0},{3,1},{4,6},{5,7},{6,4},{7,5},{8,10},{9,11},{10,... | collective-permute-start | bytes 408584 | tf_op jit(solution)/shard_map/ppermute | solution.py:83
  74.6 9.9 %collective-permute-start.10 = (f32[266,128]{1,0:T(8,128)S(1)}, f32[266,128]{1,0:T(8,128)S(1)}, u32[]{:S(2)}, u32[]{:S(2)}) collective-permute-start(f32[266,128]{1,0:T(8,128)S(1)} %pad_maximum_fusion.3), channel_id=1, source_target_pairs={{0,16},{8,24},{16,0},{24,8},{32,48},{40,56},{48,32},{56,40},{64,80... | collective-permute-start | bytes 408584 | tf_op jit(solution)/shard_map/ppermute | solution.py:83
  79.0 8.1 %collective-permute-start.11 = (f32[266,128]{1,0:T(8,128)S(1)}, f32[266,128]{1,0:T(8,128)S(1)}, u32[]{:S(2)}, u32[]{:S(2)}) collective-permute-start(f32[266,128]{1,0:T(8,128)S(1)} %pad_maximum_fusion.3), channel_id=1, source_target_pairs={{0,8},{8,0},{16,24},{24,16},{32,40},{40,32},{48,56},{56,48},{64,72... | collective-permute-start | bytes 408584 | tf_op jit(solution)/shard_map/ppermute | solution.py:83
  82.5 7.7 %collective-permute-start.9 = (f32[266,128]{1,0:T(8,128)S(1)}, f32[266,128]{1,0:T(8,128)S(1)}, u32[]{:S(2)}, u32[]{:S(2)}) collective-permute-start(f32[266,128]{1,0:T(8,128)S(1)} %pad_maximum_fusion.3), channel_id=1, source_target_pairs={{0,24},{8,16},{16,8},{24,0},{32,56},{40,48},{48,40},{56,32},{64,88... | collective-permute-start | bytes 408584 | tf_op jit(solution)/shard_map/ppermute | solution.py:83
  84.5 50.5 %copy-start.10 = (f32[10,128]{1,0:T(8,128)S(1)}, f32[10,128]{1,0:T(8,128)}, u32[]{:S(2)}) copy-start(f32[10,128]{1,0:T(8,128)} %constant.260.clone.1) | copy-start | bytes 15364
  92.3 24.9 %collective-permute-start.12 = (f32[266,128]{1,0:T(8,128)S(1)}, f32[266,128]{1,0:T(8,128)S(1)}, u32[]{:S(2)}, u32[]{:S(2)}) collective-permute-start(f32[266,128]{1,0:T(8,128)S(1)} %pad_maximum_fusion), channel_id=1, source_target_pairs={{0,96},{8,104},{16,112},{24,120},{32,64},{40,72},{48,80},{56,88},{... | collective-permute-start | bytes 408584 | tf_op jit(solution)/shard_map/ppermute | solution.py:83
  103.7 31.2 %collective-permute-start.13 = (f32[266,128]{1,0:T(8,128)S(1)}, f32[266,128]{1,0:T(8,128)S(1)}, u32[]{:S(2)}, u32[]{:S(2)}) collective-permute-start(f32[266,128]{1,0:T(8,128)S(1)} %pad_maximum_fusion), channel_id=1, source_target_pairs={{0,64},{8,72},{16,80},{24,88},{32,96},{40,104},{48,112},{56,120},{... | collective-permute-start | bytes 408584 | tf_op jit(solution)/shard_map/ppermute | solution.py:83
  108.6 26.2 %collective-permute-start.14 = (f32[266,128]{1,0:T(8,128)S(1)}, f32[266,128]{1,0:T(8,128)S(1)}, u32[]{:S(2)}, u32[]{:S(2)}) collective-permute-start(f32[266,128]{1,0:T(8,128)S(1)} %pad_maximum_fusion), channel_id=1, source_target_pairs={{0,32},{8,40},{16,48},{24,56},{32,0},{40,8},{48,16},{56,24},{64,96... | collective-permute-start | bytes 408584 | tf_op jit(solution)/shard_map/ppermute | solution.py:83
  134.9 0.7 copy-start.4
  134.9 0.7 copy-start.6
  135.6 3.2 %copy-start.5 = (f32[266,128]{1,0:T(8,128)S(1)}, f32[266,128]{1,0:T(8,128)}, u32[]{:S(2)}) copy-start(f32[266,128]{1,0:T(8,128)} %copy-done.4) | copy-start | bytes 408580
  137.5 1.3 copy-start.7
  137.7 1.8 %copy-start.1 = (bf16[4,512,128]{2,1,0:T(8,128)(2,1)S(1)}, bf16[4,512,128]{2,1,0:T(8,128)(2,1)}, u32[]{:S(2)}) copy-start(bf16[4,512,128]{2,1,0:T(8,128)(2,1)} %param.27) | copy-start | bytes 1572868

commit v6 on v0

--- a/solution.py
+++ b/solution.py
@@ -6,6 +6,8 @@
 STATE = 64
 LAYERS = 3
 DMAX = 64
+HALO = 136
+TIME = ("high", "low", "x", "core")
 
 
 def extended_2(block, sides, width):
@@ -64,6 +66,38 @@
     return result
 
 
+def gather_sum(value, axis):
+    slots = lax.all_gather(value, axis)
+    total = slots[0]
+    for j in range(1, slots.shape[0]):
+        total = total + slots[j]
+    return total
+
+
+def scan_and_sum(totals, grad, axes):
+    prefix = jnp.zeros_like(totals).at[0].set(1.0)
+    rows = grad.shape[0]
+    for axis in axes:
+        digit = lax.axis_index(axis)
+        packed = jnp.concatenate([grad, totals.reshape(-1, grad.shape[1])])
+        slots = lax.all_gather(packed, axis)
+        radix = slots.shape[0]
+        grad = slots[0, :rows]
+        for j in range(1, radix):
+            grad = grad + slots[j, :rows]
+        parts = [slots[j, rows:].reshape(totals.shape) for j in range(radix)]
+        earlier = [jnp.zeros_like(totals).at[0].set(1.0)]
+        running = parts[0]
+        for item in parts[1:]:
+            earlier.append(running)
+            running = jnp.stack(combine(tuple(running), tuple(item)))
+        totals = running
+        chosen = earlier[0]
+        for j in range(1, radix):
+            chosen = jnp.where(digit == j, earlier[j], chosen)
+        prefix = jnp.stack(combine(tuple(chosen), tuple(prefix)))
+    return prefix, grad
+
 def elements(obs, logp, params, present, keep, first):
     rate = params[0][:, None]
     noise = params[1][:, None]
@@ -106,11 +140,19 @@
     head_cotangent,
 ):
     block_len = frames.shape[1]
-    position = lax.axis_index(("outer", "inner"))
+    position = lax.axis_index(TIME)
     hidden = frames
+    halo = HALO
+    hidden = extended_2(hidden, ((TIME, 1),), halo)
+    count = lax.axis_size(TIME)
+    spots = position * block_len - halo + jnp.arange(block_len + 2 * halo, dtype=jnp.int32)
+    inside = ((spots >= 0) & (spots < count * block_len))[None, :, None]
+    pad = ((0, 0), (DMAX, DMAX), (0, 0))
     for layer in range(LAYERS):
-        extended = extended_2(hidden, ((("outer", "inner"), 1),), DMAX)
+        extended = jnp.pad(hidden, pad)
         hidden = conv_layer(extended, conv_weight[layer], conv_bias[layer], dilations[layer])
+        hidden = jnp.where(inside, hidden, jnp.zeros_like(hidden))
+    hidden = hidden[:, halo : halo + block_len]
     head = jnp.einsum("tfw,ws->tsf", hidden, head_weight, preferred_element_type=jnp.float32)
     obs = head[:, :STATE]
     logp = head[:, STATE:]
@@ -124,33 +166,36 @@
         frame_keep[:, None, :],
         first,
     )
-    local = doubling_prefix(elems, 2)
-    totals = tuple((item[:, :, -1] for item in local))
-    identity = (jnp.ones_like(totals[0]),) + tuple((jnp.zeros_like(item) for item in totals[1:]))
-    prefix = prefix_2(totals, ("outer", "inner"), combine, identity)
-    final = combine(tuple((item[:, :, None] for item in prefix)), local)
     grad_local = jnp.einsum(
         "tfw,tfs->ws", hidden, head_cotangent, preferred_element_type=jnp.float32
     )
-    head_grad = lax.psum(grad_local, ("take", "outer", "inner"))
+    grad_local = gather_sum(grad_local, "take")
+    local = doubling_prefix(elems, 2)
+    totals = jnp.stack([item[:, :, -1] for item in local])
+    prefix, head_grad = scan_and_sum(totals, grad_local, ("core", "x", "low", "high"))
+    final = combine(tuple((item[:, :, None] for item in prefix)), local)
     return (final[1], head_grad)
 
 
 def solution(mesh):
+    outer = mesh.shape["outer"]
+    inner = mesh.shape["inner"]
+    devices = mesh.devices.reshape(mesh.shape["take"], outer // 4, 4, inner // 2, 2)
+    fine = jax.sharding.Mesh(devices, ("take",) + TIME)
     return jax.shard_map(
         per_device,
-        mesh=mesh,
+        mesh=fine,
         in_specs=(
-            P("take", ("outer", "inner"), None),
-            P(),
-            P(),
-            P(),
-            P(),
-            P("take", ("outer", "inner")),
-            P("take", ("outer", "inner")),
-            P(),
-            P("take", ("outer", "inner"), None),
+            P("take", TIME, None),
+            P(),
+            P(),
+            P(),
+            P(),
+            P("take", TIME),
+            P("take", TIME),
+            P(),
+            P("take", TIME, None),
         ),
-        out_specs=(P("take", None, ("outer", "inner")), P()),
+        out_specs=(P("take", None, TIME), P()),
         check_vma=False,
     )

time: 694 us -> 143 us (0.21)
  the two profiles are of different devices: /device:TPU:487 before, /device:TPU:2 now
where the time goes in v6:
time: 143 us
  blocking collectives  79.2 us (55%)
  local copies, waits for them, and re-layouts  24.7 us (17%)
  other arithmetic  17.9 us (13%)
  matrix products  9.25 us (6%)
  between operations  6.97 us (5%)
  starting transfers between devices  4.33 us (3%)
    all_gather x4, blocking collectives, scan_and_sum(): slots = lax.all_gather(packed, axis)  65.1 us
    another operation x73, local copies, waits for them, and re-layouts, scan_and_sum(): running = jnp.stack(combine(tuple(running), tuple(item)))  17.2 us
    all_gather x1, blocking collectives, gather_sum(): slots = lax.all_gather(value, axis)  14 us
    add x9, other arithmetic, combine(): new_c = a_two * a_two * c_one / denom + c_two  9.62 us
    dot_general x9, matrix products, conv_layer(): jnp.einsum('tfw,wv->tfv', piece, weights[tap], preferred_element_type=jnp...  8.29 us
  transfers between devices with their start and end apart: 2, of which 1 were waited for; matrix products, arithmetic and copies ran while one was open for 3% of the time, Pallas kernels for 0%

profile of v6, /device:TPU:2, one launch (start us, length us, event | category | flops | bytes accessed | tf_op | source)
XLA Modules:
  0.0 142.5 jit_solution(14542039403545338831)
XLA Ops:
  0.7 1.2 fusion.98
  1.9 1.9 %collective-permute-start.1 = (bf16[4,136,256]{2,1,0:T(8,128)(2,1)S(1)}, bf16[4,136,256]{2,1,0:T(8,128)(2,1)S(1)}, u32[]{:S(2)}, u32[]{:S(2)}) collective-permute-start(bf16[4,136,256]{2,1,0:T(8,128)(2,1)S(1)} %get-tuple-element.153), channel_id=1, source_target_pairs={{1,0},{2,1},{3,2},{4,3},{5,4},{6,5},{7,6},{8,7},{9,8},{10,9},{11,1... | collective-permute-start | bytes 835592 | tf_op jit(solution)/shard_map/ppermute | solution.py:21
  3.8 2.4 %collective-permute-start = (bf16[4,136,256]{2,1,0:T(8,128)(2,1)S(1)}, bf16[4,136,256]{2,1,0:T(8,128)(2,1)S(1)}, u32[]{:S(2)}, u32[]{:S(2)}) collective-permute-start(bf16[4,136,256]{2,1,0:T(8,128)(2,1)S(1)} %get-tuple-element.154), channel_id=1, source_target_pairs={{0,1},{1,2},{2,3},{3,4},{4,5},{5,6},{6,7},{7,8},{8,9},{9,10},{10,1... | collective-permute-start | bytes 835592 | tf_op jit(solution)/shard_map/ppermute | solution.py:18
  6.2 0.8 exponential_bitcast_fusion
  7.0 0.8 fusion.104
  7.8 1.4 fusion.105
  16.1 1.0 copy-done.4
  18.2 2.0 %broadcast_select_fusion.1 = bf16[4,784,256]{2,1,0:T(8,128)(2,1)S(1)} fusion(pred[784]{0:T(1024)(128)(4,1)S(1)} %fusion.68, f32[256]{0:T(256)S(1)} %bitcast.303, s32[]{:T(128)S(6)} %select_n.121, bf16[4,784,256]{2,1,0:T(8,128)(2,1)S(1)} %constant_dynamic-update-slice_fusion, f32[4,784,256]{2,1,0:T(8,128)S(1)} %fusion.3, f32[4,784,256]{2,1,0:T(8,128)S(1)} %fusion.53, ...), kind=kOutput, calls=%fused_computation.21 | convolution fusion | flops 419872768 | bytes 11372548 | tf_op jit(solution)/shard_map/tfw,wv->tfv/dot_general | solution.py:122
  21.4 1.7 %broadcast_select_fusion = bf16[4,784,256]{2,1,0:T(8,128)(2,1)S(1)} fusion(pred[784]{0:T(1024)(128)(4,1)S(1)} %fusion.68, f32[256]{0:T(256)S(1)} %bitcast.302, f32[4,784,256]{2,1,0:T(8,128)S(1)} %fusion.6, f32[4,784,256]{2,1,0:T(8,128)S(1)} %fusion.5, bf16[4,784,256]{2,1,0:T(8,128)(2,1)S(1)} %broadcast_select_fusion.1, ...), kind=kOutput, calls=%fused_computation.20 | convolution fusion | flops 419872768 | bytes 11372544 | tf_op jit(solution)/shard_map/tfw,wv->tfv/dot_general | solution.py:122
  24.3 1.0 negate_exponential_fusion
  27.2 14.0 %all-gather = f32[1024,128]{1,0:T(8,128)S(1)} all-gather(f32[256,128]{1,0:T(8,128)S(1)} %convolution_bitcast_fusion.1), channel_id=2, replica_groups=mesh['take'=4,'high'=4,'low'=4,'x'=4,'core'=2] {'take'}, dimensions={0}, use_global_device_ids=true | all-gather | bytes 655360 | tf_op jit(solution)/shard_map/all_gather | solution.py:70
  41.7 0.8 divide_add_fusion.14
  42.6 1.1 divide_add_fusion.13
  43.7 1.3 divide_add_fusion.12
  45.0 1.3 divide_add_fusion.11
  46.3 1.3 divide_add_fusion.10
  47.6 1.3 divide_add_fusion.9
  48.9 1.3 divide_add_fusion.8
  50.2 1.2 fusion.20
  51.6 0.8 fusion.21
  54.5 2.0 %all-gather.5 = f32[2,266,128]{2,1,0:T(8,128)S(1)} all-gather(f32[1,266,128]{2,1,0:T(8,128)S(1)} %maximum_bitcast_fusion), channel_id=3, replica_groups=mesh['take'=4,'high'=4,'low'=4,'x'=4,'core'=2] {'core'}, dimensions={0}, use_global_device_ids=true | all-gather | bytes 408576 | tf_op jit(solution)/shard_map/all_gather | solution.py:83
  57.5 15.4 %all-gather.6 = f32[4,266,128]{2,1,0:T(8,128)S(1)} all-gather(f32[1,266,128]{2,1,0:T(8,128)S(1)} %maximum_bitcast_fusion.1), channel_id=4, replica_groups=mesh['take'=4,'high'=4,'low'=4,'x'=4,'core'=2] {'x'}, dimensions={0}, use_global_device_ids=true | all-gather | bytes 680960 | tf_op jit(solution)/shard_map/all_gather | solution.py:83
  74.9 16.3 %all-gather.7 = f32[4,266,128]{2,1,0:T(8,128)S(1)} all-gather(f32[1,266,128]{2,1,0:T(8,128)S(1)} %maximum_bitcast_fusion.2), channel_id=5, replica_groups=mesh['take'=4,'high'=4,'low'=4,'x'=4,'core'=2] {'low'}, dimensions={0}, use_global_device_ids=true | all-gather | bytes 680960 | tf_op jit(solution)/shard_map/all_gather | solution.py:83
  91.2 0.8 copy-done.3
  94.5 31.5 %all-gather.8 = f32[4,266,128]{2,1,0:T(8,128)S(1)} all-gather(f32[1,266,128]{2,1,0:T(8,128)S(1)} %maximum_bitcast_fusion.3), channel_id=6, replica_groups=mesh['take'=4,'high'=4,'low'=4,'x'=4,'core'=2] {'high'}, dimensions={0}, use_global_device_ids=true | all-gather | bytes 680960 | tf_op jit(solution)/shard_map/all_gather | solution.py:83
  130.9 0.7 unstack.628
  131.6 0.8 unstack.626
  133.9 0.8 unstack.642
  136.8 0.8 unstack.646
  137.6 0.8 unstack.644
  138.3 0.8 unstack.640
  141.5 1.0 divide_add_fusion
  (187 shorter events, 25.4 us)
Async XLA Ops:
  0.6 25.2 %copy-start = (bf16[4,512,128]{2,1,0:T(8,128)(2,1)S(1)}, bf16[4,512,128]{2,1,0:T(8,128)(2,1)}, u32[]{:S(2)}) copy-start(bf16[4,512,128]{2,1,0:T(8,128)(2,1)} %param.27) | copy-start | bytes 1572868
  0.6 15.3 %copy-start.2 = (bf16[4,512,256]{2,1,0:T(8,128)(2,1)S(1)}, bf16[4,512,256]{2,1,0:T(8,128)(2,1)}, u32[]{:S(2)}) copy-start(bf16[4,512,256]{2,1,0:T(8,128)(2,1)} %param.19) | copy-start | bytes 3145732
  1.9 14.2 %collective-permute-start.1 = (bf16[4,136,256]{2,1,0:T(8,128)(2,1)S(1)}, bf16[4,136,256]{2,1,0:T(8,128)(2,1)S(1)}, u32[]{:S(2)}, u32[]{:S(2)}) collective-permute-start(bf16[4,136,256]{2,1,0:T(8,128)(2,1)S(1)} %get-tuple-element.153), channel_id=1, source_target_pairs={{1,0},{2,1},{3,2},{4,3},{5,4},{6,5},{7,6},{8,7},{9,8},{10,9},{11,1... | collective-permute-start | bytes 835592 | tf_op jit(solution)/shard_map/ppermute | solution.py:21
  3.8 12.1 %collective-permute-start = (bf16[4,136,256]{2,1,0:T(8,128)(2,1)S(1)}, bf16[4,136,256]{2,1,0:T(8,128)(2,1)S(1)}, u32[]{:S(2)}, u32[]{:S(2)}) collective-permute-start(bf16[4,136,256]{2,1,0:T(8,128)(2,1)S(1)} %get-tuple-element.154), channel_id=1, source_target_pairs={{0,1},{1,2},{2,3},{3,4},{4,5},{5,6},{6,7},{7,8},{8,9},{9,10},{10,1... | collective-permute-start | bytes 835592 | tf_op jit(solution)/shard_map/ppermute | solution.py:18
  15.8 1.3 copy-start.4
  25.9 0.8 copy-start.5
  27.2 14.5 %copy-start.6 = (f32[4,512]{1,0:T(4,128)S(1)}, f32[4,512]{1,0:T(4,128)}, u32[]{:S(2)}) copy-start(f32[4,512]{1,0:T(4,128)} %param.25) | copy-start | bytes 24580
  74.9 52.4 %copy-start.7 = (f32[1,10,128]{2,1,0:T(8,128)S(1)}, f32[1,10,128]{2,1,0:T(8,128)}, u32[]{:S(2)}) copy-start(f32[1,10,128]{2,1,0:T(8,128)} %constant.193.clone.1) | copy-start | bytes 15364
  91.2 0.8 copy-start.3
  126.6 15.9 %copy-start.1 = (bf16[4,512,128]{2,1,0:T(8,128)(2,1)S(1)}, bf16[4,512,128]{2,1,0:T(8,128)(2,1)}, u32[]{:S(2)}) copy-start(bf16[4,512,128]{2,1,0:T(8,128)(2,1)} %param.27) | copy-start | bytes 1572868

commit v7 on v6

--- a/solution.py
+++ b/solution.py
@@ -7,7 +7,8 @@
 LAYERS = 3
 DMAX = 64
 HALO = 136
-TIME = ("high", "low", "x", "core")
+TIME = ("z3", "z2", "z1", "z0", "xh", "xl", "core")
+TAKE = ("th", "tl")
 
 
 def extended_2(block, sides, width):
@@ -169,33 +170,31 @@
     grad_local = jnp.einsum(
         "tfw,tfs->ws", hidden, head_cotangent, preferred_element_type=jnp.float32
     )
-    grad_local = gather_sum(grad_local, "take")
+    grad_local = gather_sum(gather_sum(grad_local, "tl"), "th")
     local = doubling_prefix(elems, 2)
     totals = jnp.stack([item[:, :, -1] for item in local])
-    prefix, head_grad = scan_and_sum(totals, grad_local, ("core", "x", "low", "high"))
+    prefix, head_grad = scan_and_sum(totals, grad_local, TIME[::-1])
     final = combine(tuple((item[:, :, None] for item in prefix)), local)
     return (final[1], head_grad)
 
 
 def solution(mesh):
-    outer = mesh.shape["outer"]
-    inner = mesh.shape["inner"]
-    devices = mesh.devices.reshape(mesh.shape["take"], outer // 4, 4, inner // 2, 2)
-    fine = jax.sharding.Mesh(devices, ("take",) + TIME)
+    devices = mesh.devices.reshape((2,) * (len(TAKE) + len(TIME)))
+    fine = jax.sharding.Mesh(devices, TAKE + TIME)
     return jax.shard_map(
         per_device,
         mesh=fine,
         in_specs=(
-            P("take", TIME, None),
-            P(),
-            P(),
-            P(),
-            P(),
-            P("take", TIME),
-            P("take", TIME),
-            P(),
-            P("take", TIME, None),
+            P(TAKE, TIME, None),
+            P(),
+            P(),
+            P(),
+            P(),
+            P(TAKE, TIME),
+            P(TAKE, TIME),
+            P(),
+            P(TAKE, TIME, None),
         ),
-        out_specs=(P("take", None, TIME), P()),
+        out_specs=(P(TAKE, None, TIME), P()),
         check_vma=False,
     )

time: 143 us -> 143 us (level)
  the two profiles are of different devices: /device:TPU:2 before, /device:TPU:26 now
where the time goes in v7:
time: 143 us; the launch traced here: 142 us
  blocking collectives  84.9 us (59%)
  other arithmetic  20.5 us (14%)
  local copies, waits for them, and re-layouts  16.1 us (11%)
  matrix products  9.24 us (6%)
  between operations  7.16 us (5%)
  starting transfers between devices  4.33 us (3%)
    all_gather x7, blocking collectives, scan_and_sum(): slots = lax.all_gather(packed, axis)  70.2 us
    all_gather x2, blocking collectives, gather_sum(): slots = lax.all_gather(value, axis)  14.8 us
    add x9, other arithmetic, combine(): new_c = a_two * a_two * c_one / denom + c_two  9.64 us
    dot_general x9, matrix products, conv_layer(): jnp.einsum('tfw,wv->tfv', piece, weights[tap], preferred_element_type=jnp...  8.28 us
    another operation x66, local copies, waits for them, and re-layouts, scan_and_sum(): running = jnp.stack(combine(tuple(running), tuple(item)))  4.89 us
    unnamed x26, local copies, waits for them, and re-layouts  3.74 us
  transfers between devices with their start and end apart: 2, of which 0 were waited for; matrix products, arithmetic and copies ran while one was open for 3% of the time, Pallas kernels for 0%

profile of v7, /device:TPU:26, one launch (start us, length us, event | category | flops | bytes accessed | tf_op | source)
XLA Modules:
  0.0 142.2 jit_solution(15895815631883874227)
XLA Ops:
  0.7 1.2 fusion.91
  1.9 1.9 %collective-permute-start.1 = (bf16[4,136,256]{2,1,0:T(8,128)(2,1)S(1)}, bf16[4,136,256]{2,1,0:T(8,128)(2,1)S(1)}, u32[]{:S(2)}, u32[]{:S(2)}) collective-permute-start(bf16[4,136,256]{2,1,0:T(8,128)(2,1)S(1)} %get-tuple-element.133), channel_id=1, source_target_pairs={{1,0},{2,1},{3,2},{4,3},{5,4},{6,5},{7,6},{8,7},{9,8},{10,9},{11,1... | collective-permute-start | bytes 835592 | tf_op jit(solution)/shard_map/ppermute | solution.py:22
  3.8 2.4 %collective-permute-start = (bf16[4,136,256]{2,1,0:T(8,128)(2,1)S(1)}, bf16[4,136,256]{2,1,0:T(8,128)(2,1)S(1)}, u32[]{:S(2)}, u32[]{:S(2)}) collective-permute-start(bf16[4,136,256]{2,1,0:T(8,128)(2,1)S(1)} %get-tuple-element.134), channel_id=1, source_target_pairs={{0,1},{1,2},{2,3},{3,4},{4,5},{5,6},{6,7},{7,8},{8,9},{9,10},{10,1... | collective-permute-start | bytes 835592 | tf_op jit(solution)/shard_map/ppermute | solution.py:19
  6.2 0.8 exponential_bitcast_fusion
  7.0 0.8 fusion.105
  7.8 1.4 %fusion.106 = (s32[1]{0:T(128)}, s32[1]{0:T(128)}, s32[1]{0:T(128)}) fusion(s32[3]{0:T(128)} %param.28), kind=kLoop, calls=%fused_computation.281 | loop fusion | bytes 24 | tf_op jit(solution)/shard_map/slice | solution.py:154
  16.2 1.1 copy-done.6
  18.5 2.0 %broadcast_select_fusion.1 = bf16[4,784,256]{2,1,0:T(8,128)(2,1)S(1)} fusion(pred[784]{0:T(1024)(128)(4,1)S(1)} %fusion.71, f32[256]{0:T(256)S(1)} %bitcast.219, s32[]{:T(128)S(6)} %select_n.100, bf16[4,784,256]{2,1,0:T(8,128)(2,1)S(1)} %constant_dynamic-update-slice_fusion, f32[4,784,256]{2,1,0:T(8,128)S(1)} %fusion.3, f32[4,784,256]{2,1,0:T(8,128)S(1)} %fusion.56, ...), kind=kOutput, calls=%fused_computation.21 | convolution fusion | flops 419872768 | bytes 11372548 | tf_op jit(solution)/shard_map/tfw,wv->tfv/dot_general | solution.py:123
  21.7 1.7 %broadcast_select_fusion = bf16[4,784,256]{2,1,0:T(8,128)(2,1)S(1)} fusion(pred[784]{0:T(1024)(128)(4,1)S(1)} %fusion.71, f32[256]{0:T(256)S(1)} %bitcast.218, f32[4,784,256]{2,1,0:T(8,128)S(1)} %fusion.6, f32[4,784,256]{2,1,0:T(8,128)S(1)} %fusion.5, bf16[4,784,256]{2,1,0:T(8,128)(2,1)S(1)} %broadcast_select_fusion.1, ...), kind=kOutput, calls=%fused_computation.20 | convolution fusion | flops 419872768 | bytes 11372544 | tf_op jit(solution)/shard_map/tfw,wv->tfv/dot_general | solution.py:123
  24.6 1.0 negate_exponential_fusion
  27.4 6.9 %all-gather = f32[512,128]{1,0:T(8,128)S(1)} all-gather(f32[256,128]{1,0:T(8,128)S(1)} %convolution_bitcast_fusion.1), channel_id=2, replica_groups=mesh['th'=2,'tl'=2,'z3'=2,'z2'=2,'z1'=2,'z0'=2,'xh'=2,'xl'=2,'core'=2] {..., dimensions={0}, use_global_device_ids=true | all-gather | bytes 393216 | tf_op jit(solution)/shard_map/all_gather | solution.py:71
  34.4 7.9 %all-gather.8 = f32[512,128]{1,0:T(8,128)S(1)} all-gather(f32[256,128]{1,0:T(8,128)S(1)} %slice_add_fusion.10), channel_id=10, replica_groups=mesh['th'=2,'tl'=2,'z3'=2,'z2'=2,'z1'=2,'z0'=2,'xh'=2,'xl'=2,'core'=2] {..., dimensions={0}, use_global_device_ids=true | all-gather | bytes 393216 | tf_op jit(solution)/shard_map/all_gather | solution.py:71
  42.7 0.8 divide_add_fusion.14
  43.5 1.1 divide_add_fusion.13
  44.7 1.3 divide_add_fusion.12
  46.0 1.3 divide_add_fusion.11
  47.3 1.3 divide_add_fusion.10
  48.6 1.3 divide_add_fusion.9
  49.9 1.3 divide_add_fusion.8
  51.2 1.2 fusion.20
  52.5 0.8 fusion.21
  55.4 2.0 %all-gather.9 = f32[2,266,128]{2,1,0:T(8,128)S(1)} all-gather(f32[1,266,128]{2,1,0:T(8,128)S(1)} %maximum_bitcast_fusion), channel_id=3, replica_groups=mesh['th'=2,'tl'=2,'z3'=2,'z2'=2,'z1'=2,'z0'=2,'xh'=2,'xl'=2,'core'=2] {..., dimensions={0}, use_global_device_ids=true | all-gather | bytes 408576 | tf_op jit(solution)/shard_map/all_gather | solution.py:84
  58.5 6.4 %all-gather.10 = f32[2,266,128]{2,1,0:T(8,128)S(1)} all-gather(f32[1,266,128]{2,1,0:T(8,128)S(1)} %maximum_bitcast_fusion.1), channel_id=4, replica_groups=mesh['th'=2,'tl'=2,'z3'=2,'z2'=2,'z1'=2,'z0'=2,'xh'=2,'xl'=2,'core'=2] {..., dimensions={0}, use_global_device_ids=true | all-gather | bytes 408576 | tf_op jit(solution)/shard_map/all_gather | solution.py:84
  65.9 7.2 %all-gather.11 = f32[2,266,128]{2,1,0:T(8,128)S(1)} all-gather(f32[1,266,128]{2,1,0:T(8,128)S(1)} %maximum_bitcast_fusion.2), channel_id=5, replica_groups=mesh['th'=2,'tl'=2,'z3'=2,'z2'=2,'z1'=2,'z0'=2,'xh'=2,'xl'=2,'core'=2] {..., dimensions={0}, use_global_device_ids=true | all-gather | bytes 408576 | tf_op jit(solution)/shard_map/all_gather | solution.py:84
  74.1 5.7 %all-gather.12 = f32[2,266,128]{2,1,0:T(8,128)S(1)} all-gather(f32[1,266,128]{2,1,0:T(8,128)S(1)} %maximum_bitcast_fusion.3), channel_id=6, replica_groups=mesh['th'=2,'tl'=2,'z3'=2,'z2'=2,'z1'=2,'z0'=2,'xh'=2,'xl'=2,'core'=2] {..., dimensions={0}, use_global_device_ids=true | all-gather | bytes 408576 | tf_op jit(solution)/shard_map/all_gather | solution.py:84
  82.2 0.9 maximum_bitcast_fusion.4
  83.2 8.5 %all-gather.13 = f32[2,266,128]{2,1,0:T(8,128)S(1)} all-gather(f32[1,266,128]{2,1,0:T(8,128)S(1)} %maximum_bitcast_fusion.4), channel_id=7, replica_groups=mesh['th'=2,'tl'=2,'z3'=2,'z2'=2,'z1'=2,'z0'=2,'xh'=2,'xl'=2,'core'=2] {..., dimensions={0}, use_global_device_ids=true | all-gather | bytes 408576 | tf_op jit(solution)/shard_map/all_gather | solution.py:84
  94.0 0.9 maximum_bitcast_fusion.5
  94.9 16.9 %all-gather.14 = f32[2,266,128]{2,1,0:T(8,128)S(1)} all-gather(f32[1,266,128]{2,1,0:T(8,128)S(1)} %maximum_bitcast_fusion.5), channel_id=8, replica_groups=mesh['th'=2,'tl'=2,'z3'=2,'z2'=2,'z1'=2,'z0'=2,'xh'=2,'xl'=2,'core'=2] {..., dimensions={0}, use_global_device_ids=true | all-gather | bytes 408576 | tf_op jit(solution)/shard_map/all_gather | solution.py:84
  113.5 23.5 %all-gather.15 = f32[2,266,128]{2,1,0:T(8,128)S(1)} all-gather(f32[1,266,128]{2,1,0:T(8,128)S(1)} %maximum_bitcast_fusion.6), channel_id=9, replica_groups=mesh['th'=2,'tl'=2,'z3'=2,'z2'=2,'z1'=2,'z0'=2,'xh'=2,'xl'=2,'core'=2] {..., dimensions={0}, use_global_device_ids=true | all-gather | bytes 408576 | tf_op jit(solution)/shard_map/all_gather | solution.py:84
  137.7 0.7 slice_select_fusion
  141.2 1.0 divide_add_fusion
  (216 shorter events, 21.7 us)
Async XLA Ops:
  0.6 25.5 %copy-start = (bf16[4,512,128]{2,1,0:T(8,128)(2,1)S(1)}, bf16[4,512,128]{2,1,0:T(8,128)(2,1)}, u32[]{:S(2)}) copy-start(bf16[4,512,128]{2,1,0:T(8,128)(2,1)} %param.33) | copy-start | bytes 1572868
  0.6 15.4 %copy-start.2 = (bf16[4,512,256]{2,1,0:T(8,128)(2,1)S(1)}, bf16[4,512,256]{2,1,0:T(8,128)(2,1)}, u32[]{:S(2)}) copy-start(bf16[4,512,256]{2,1,0:T(8,128)(2,1)} %param.25) | copy-start | bytes 3145732
  1.9 14.3 %collective-permute-start.1 = (bf16[4,136,256]{2,1,0:T(8,128)(2,1)S(1)}, bf16[4,136,256]{2,1,0:T(8,128)(2,1)S(1)}, u32[]{:S(2)}, u32[]{:S(2)}) collective-permute-start(bf16[4,136,256]{2,1,0:T(8,128)(2,1)S(1)} %get-tuple-element.133), channel_id=1, source_target_pairs={{1,0},{2,1},{3,2},{4,3},{5,4},{6,5},{7,6},{8,7},{9,8},{10,9},{11,1... | collective-permute-start | bytes 835592 | tf_op jit(solution)/shard_map/ppermute | solution.py:22
  3.8 12.2 %collective-permute-start = (bf16[4,136,256]{2,1,0:T(8,128)(2,1)S(1)}, bf16[4,136,256]{2,1,0:T(8,128)(2,1)S(1)}, u32[]{:S(2)}, u32[]{:S(2)}) collective-permute-start(bf16[4,136,256]{2,1,0:T(8,128)(2,1)S(1)} %get-tuple-element.134), channel_id=1, source_target_pairs={{0,1},{1,2},{2,3},{3,4},{4,5},{5,6},{6,7},{7,8},{8,9},{9,10},{10,1... | collective-permute-start | bytes 835592 | tf_op jit(solution)/shard_map/ppermute | solution.py:19
  16.0 1.3 copy-start.6
  26.1 0.8 copy-start.7
  27.4 15.3 %copy-start.8 = (f32[4,512]{1,0:T(4,128)S(1)}, f32[4,512]{1,0:T(4,128)}, u32[]{:S(2)}) copy-start(f32[4,512]{1,0:T(4,128)} %param.31) | copy-start | bytes 24580
  79.9 0.7 copy-start.3
  83.1 54.5 %copy-start.9 = (f32[1,10,128]{2,1,0:T(8,128)S(1)}, f32[1,10,128]{2,1,0:T(8,128)}, u32[]{:S(2)}) copy-start(f32[1,10,128]{2,1,0:T(8,128)} %constant.250.clone.1) | copy-start | bytes 15364
  91.6 0.7 copy-start.4
  111.8 0.7 copy-start.5
  137.0 5.2 %copy-start.1 = (bf16[4,512,128]{2,1,0:T(8,128)(2,1)S(1)}, bf16[4,512,128]{2,1,0:T(8,128)(2,1)}, u32[]{:S(2)}) copy-start(bf16[4,512,128]{2,1,0:T(8,128)(2,1)} %param.33) | copy-start | bytes 1572868

commit v8 on v7

--- a/solution.py
+++ b/solution.py
@@ -65,6 +65,10 @@
         result = combine(tuple(moved), result)
         offset = offset * 2
     return result
+
+
+def pair_sum(value, axis):
+    return value + lax.ppermute(value, axis, [(0, 1), (1, 0)])
 
 
 def gather_sum(value, axis):
@@ -170,7 +174,7 @@
     grad_local = jnp.einsum(
         "tfw,tfs->ws", hidden, head_cotangent, preferred_element_type=jnp.float32
     )
-    grad_local = gather_sum(gather_sum(grad_local, "tl"), "th")
+    grad_local = pair_sum(pair_sum(grad_local, "tl"), "th")
     local = doubling_prefix(elems, 2)
     totals = jnp.stack([item[:, :, -1] for item in local])
     prefix, head_grad = scan_and_sum(totals, grad_local, TIME[::-1])

time: 143 us -> 165 us (1.15)
  the two profiles are of different devices: /device:TPU:26 before, /device:TPU:1 now
where the time goes in v8:
time: 165 us; the launch traced here: 164 us
  blocking collectives  69.5 us (42%)
  other arithmetic  39.4 us (24%)
  local copies, waits for them, and re-layouts  17.8 us (11%)
  starting transfers between devices  14.3 us (9%)
  matrix products  9.29 us (6%)
  between operations  6.98 us (4%)
  waiting for transfers between devices  6.3 us (4%)
    all_gather x7, blocking collectives, scan_and_sum(): slots = lax.all_gather(packed, axis)  69.5 us
    unnamed x31, other arithmetic  16.9 us
    add x9, other arithmetic, combine(): new_c = a_two * a_two * c_one / denom + c_two  9.63 us
    dot_general x9, matrix products, conv_layer(): jnp.einsum('tfw,wv->tfv', piece, weights[tap], preferred_element_type=jnp...  8.32 us
    ppermute x2, waiting for transfers between devices, pair_sum(): return value + lax.ppermute(value, axis, [(0, 1), (1, 0)])  6.29 us
    ppermute x1, starting transfers between devices, extended_2(): lax.ppermute(lax.slice_in_dim(block, 0, width, axis=dim), axis, backward)  5.56 us
    another operation x66, local copies, waits for them, and re-layouts, scan_and_sum(): running = jnp.stack(combine(tuple(running), tuple(item)))  4.91 us
    reshape x7, local copies, waits for them, and re-layouts, scan_and_sum(): packed = jnp.concatenate([grad, totals.reshape(-1, grad.shape[1])])  4.75 us
  transfers between devices with their start and end apart: 4, of which 1 were waited for; matrix products, arithmetic and copies ran while one was open for 11% of the time, Pallas kernels for 0%

profile of v8, /device:TPU:1, one launch (start us, length us, event | category | flops | bytes accessed | tf_op | source)
XLA Modules:
  0.0 163.6 jit_solution(568743164847619992)
XLA Ops:
  0.7 1.2 fusion.91
  1.9 4.5 %collective-permute-start = (bf16[4,136,256]{2,1,0:T(8,128)(2,1)S(1)}, bf16[4,136,256]{2,1,0:T(8,128)(2,1)S(1)}, u32[]{:S(2)}, u32[]{:S(2)}) collective-permute-start(bf16[4,136,256]{2,1,0:T(8,128)(2,1)S(1)} %get-tuple-element.134), channel_id=1, source_target_pairs={{0,1},{1,2},{2,3},{3,4},{4,5},{5,6},{6,7},{7,8},{8,9},{9,10},{10,1... | collective-permute-start | bytes 835592 | tf_op jit(solution)/shard_map/ppermute | solution.py:19
  6.4 5.6 %collective-permute-start.1 = (bf16[4,136,256]{2,1,0:T(8,128)(2,1)S(1)}, bf16[4,136,256]{2,1,0:T(8,128)(2,1)S(1)}, u32[]{:S(2)}, u32[]{:S(2)}) collective-permute-start(bf16[4,136,256]{2,1,0:T(8,128)(2,1)S(1)} %get-tuple-element.133), channel_id=1, source_target_pairs={{1,0},{2,1},{3,2},{4,3},{5,4},{6,5},{7,6},{8,7},{9,8},{10,9},{11,1... | collective-permute-start | bytes 835592 | tf_op jit(solution)/shard_map/ppermute | solution.py:22
  11.9 0.8 fusion.105
  12.7 0.8 exponential_bitcast_fusion
  13.5 1.4 fusion.106
  21.6 1.1 copy-done.6
  23.9 2.0 %broadcast_select_fusion.1 = bf16[4,784,256]{2,1,0:T(8,128)(2,1)S(1)} fusion(pred[784]{0:T(1024)(128)(4,1)S(1)} %fusion.71, f32[256]{0:T(256)S(1)} %bitcast.219, s32[]{:T(128)S(6)} %select_n.100, bf16[4,784,256]{2,1,0:T(8,128)(2,1)S(1)} %constant_dynamic-update-slice_fusion, f32[4,784,256]{2,1,0:T(8,128)S(1)} %fusion.3, f32[4,784,256]{2,1,0:T(8,128)S(1)} %fusion.56, ...), kind=kOutput, calls=%fused_computation.21 | convolution fusion | flops 419872768 | bytes 11372548 | tf_op jit(solution)/shard_map/tfw,wv->tfv/dot_general | solution.py:127
  27.1 1.7 %broadcast_select_fusion = bf16[4,784,256]{2,1,0:T(8,128)(2,1)S(1)} fusion(pred[784]{0:T(1024)(128)(4,1)S(1)} %fusion.71, f32[256]{0:T(256)S(1)} %bitcast.218, f32[4,784,256]{2,1,0:T(8,128)S(1)} %fusion.6, f32[4,784,256]{2,1,0:T(8,128)S(1)} %fusion.5, bf16[4,784,256]{2,1,0:T(8,128)(2,1)S(1)} %broadcast_select_fusion.1, ...), kind=kOutput, calls=%fused_computation.20 | convolution fusion | flops 419872768 | bytes 11372544 | tf_op jit(solution)/shard_map/tfw,wv->tfv/dot_general | solution.py:127
  30.1 1.0 negate_exponential_fusion
  32.1 2.1 %collective-permute-start.2 = (f32[256,128]{1,0:T(8,128)S(1)}, f32[256,128]{1,0:T(8,128)S(1)}, u32[]{:S(2)}, u32[]{:S(2)}) collective-permute-start(f32[256,128]{1,0:T(8,128)S(1)} %convolution_bitcast_fusion.1), channel_id=1, source_target_pairs={{0,128},{128,0},{1,129},{129,1},{2,130},{130,2},{3,131},{131,3},{4... | collective-permute-start | bytes 393224 | tf_op jit(solution)/shard_map/ppermute | solution.py:71
  35.2 0.8 divide_add_fusion.14
  36.0 1.1 divide_add_fusion.13
  37.1 1.3 divide_add_fusion.12
  38.4 1.3 divide_add_fusion.11
  39.7 1.3 divide_add_fusion.10
  41.0 1.3 divide_add_fusion.9
  42.3 1.3 divide_add_fusion.8
  43.7 1.2 fusion.20
  47.8 2.2 %collective-permute-start.3 = (f32[256,128]{1,0:T(8,128)S(1)}, f32[256,128]{1,0:T(8,128)S(1)}, u32[]{:S(2)}, u32[]{:S(2)}) collective-permute-start(f32[256,128]{1,0:T(8,128)S(1)} %add.1378), channel_id=1, source_target_pairs={{0,256},{256,0},{1,257},{257,1},{2,258},{258,2},{3,259},{259,3},{4... | collective-permute-start | bytes 393224 | tf_op jit(solution)/shard_map/ppermute | solution.py:71
  50.1 6.3 %collective-permute-done.3 = f32[256,128]{1,0:T(8,128)S(1)} collective-permute-done((f32[256,128]{1,0:T(8,128)S(1)}, f32[256,128]{1,0:T(8,128)S(1)}, u32[]{:S(2)}, u32[]{:S(2)}) %collective-permute-start.3) | collective-permute-done | bytes 131104 | tf_op jit(solution)/shard_map/ppermute | solution.py:71
  56.4 2.0 %all-gather.7 = f32[2,266,128]{2,1,0:T(8,128)S(1)} all-gather(f32[1,266,128]{2,1,0:T(8,128)S(1)} %maximum_bitcast_fusion), channel_id=2, replica_groups=mesh['th'=2,'tl'=2,'z3'=2,'z2'=2,'z1'=2,'z0'=2,'xh'=2,'xl'=2,'core'=2] {..., dimensions={0}, use_global_device_ids=true | all-gather | bytes 408576 | tf_op jit(solution)/shard_map/all_gather | solution.py:88
  63.0 5.5 %all-gather.8 = f32[2,266,128]{2,1,0:T(8,128)S(1)} all-gather(f32[1,266,128]{2,1,0:T(8,128)S(1)} %maximum_bitcast_fusion.1), channel_id=3, replica_groups=mesh['th'=2,'tl'=2,'z3'=2,'z2'=2,'z1'=2,'z0'=2,'xh'=2,'xl'=2,'core'=2] {..., dimensions={0}, use_global_device_ids=true | all-gather | bytes 408576 | tf_op jit(solution)/shard_map/all_gather | solution.py:88
  73.2 6.1 %all-gather.9 = f32[2,266,128]{2,1,0:T(8,128)S(1)} all-gather(f32[1,266,128]{2,1,0:T(8,128)S(1)} %maximum_bitcast_fusion.2), channel_id=4, replica_groups=mesh['th'=2,'tl'=2,'z3'=2,'z2'=2,'z1'=2,'z0'=2,'xh'=2,'xl'=2,'core'=2] {..., dimensions={0}, use_global_device_ids=true | all-gather | bytes 408576 | tf_op jit(solution)/shard_map/all_gather | solution.py:88
  83.8 4.8 %all-gather.10 = f32[2,266,128]{2,1,0:T(8,128)S(1)} all-gather(f32[1,266,128]{2,1,0:T(8,128)S(1)} %maximum_bitcast_fusion.3), channel_id=5, replica_groups=mesh['th'=2,'tl'=2,'z3'=2,'z2'=2,'z1'=2,'z0'=2,'xh'=2,'xl'=2,'core'=2] {..., dimensions={0}, use_global_device_ids=true | all-gather | bytes 408576 | tf_op jit(solution)/shard_map/all_gather | solution.py:88
  93.9 0.9 maximum_bitcast_fusion.4
  94.8 7.6 %all-gather.11 = f32[2,266,128]{2,1,0:T(8,128)S(1)} all-gather(f32[1,266,128]{2,1,0:T(8,128)S(1)} %maximum_bitcast_fusion.4), channel_id=6, replica_groups=mesh['th'=2,'tl'=2,'z3'=2,'z2'=2,'z1'=2,'z0'=2,'xh'=2,'xl'=2,'core'=2] {..., dimensions={0}, use_global_device_ids=true | all-gather | bytes 408576 | tf_op jit(solution)/shard_map/all_gather | solution.py:88
  107.8 0.9 maximum_bitcast_fusion.5
  108.7 21.0 %all-gather.12 = f32[2,266,128]{2,1,0:T(8,128)S(1)} all-gather(f32[1,266,128]{2,1,0:T(8,128)S(1)} %maximum_bitcast_fusion.5), channel_id=7, replica_groups=mesh['th'=2,'tl'=2,'z3'=2,'z2'=2,'z1'=2,'z0'=2,'xh'=2,'xl'=2,'core'=2] {..., dimensions={0}, use_global_device_ids=true | all-gather | bytes 408576 | tf_op jit(solution)/shard_map/all_gather | solution.py:88
  135.0 0.9 maximum_bitcast_fusion.6
  136.0 22.4 %all-gather.13 = f32[2,266,128]{2,1,0:T(8,128)S(1)} all-gather(f32[1,266,128]{2,1,0:T(8,128)S(1)} %maximum_bitcast_fusion.6), channel_id=8, replica_groups=mesh['th'=2,'tl'=2,'z3'=2,'z2'=2,'z1'=2,'z0'=2,'xh'=2,'xl'=2,'core'=2] {..., dimensions={0}, use_global_device_ids=true | all-gather | bytes 408576 | tf_op jit(solution)/shard_map/all_gather | solution.py:88
  162.6 1.0 divide_add_fusion
  (218 shorter events, 43.1 us)
Async XLA Ops:
  0.6 31.0 %copy-start = (bf16[4,512,128]{2,1,0:T(8,128)(2,1)S(1)}, bf16[4,512,128]{2,1,0:T(8,128)(2,1)}, u32[]{:S(2)}) copy-start(bf16[4,512,128]{2,1,0:T(8,128)(2,1)} %param.33) | copy-start | bytes 1572868
  0.6 20.9 %copy-start.2 = (bf16[4,512,256]{2,1,0:T(8,128)(2,1)S(1)}, bf16[4,512,256]{2,1,0:T(8,128)(2,1)}, u32[]{:S(2)}) copy-start(bf16[4,512,256]{2,1,0:T(8,128)(2,1)} %param.25) | copy-start | bytes 3145732
  1.9 19.6 %collective-permute-start = (bf16[4,136,256]{2,1,0:T(8,128)(2,1)S(1)}, bf16[4,136,256]{2,1,0:T(8,128)(2,1)S(1)}, u32[]{:S(2)}, u32[]{:S(2)}) collective-permute-start(bf16[4,136,256]{2,1,0:T(8,128)(2,1)S(1)} %get-tuple-element.134), channel_id=1, source_target_pairs={{0,1},{1,2},{2,3},{3,4},{4,5},{5,6},{6,7},{7,8},{8,9},{9,10},{10,1... | collective-permute-start | bytes 835592 | tf_op jit(solution)/shard_map/ppermute | solution.py:19
  6.4 15.2 %collective-permute-start.1 = (bf16[4,136,256]{2,1,0:T(8,128)(2,1)S(1)}, bf16[4,136,256]{2,1,0:T(8,128)(2,1)S(1)}, u32[]{:S(2)}, u32[]{:S(2)}) collective-permute-start(bf16[4,136,256]{2,1,0:T(8,128)(2,1)S(1)} %get-tuple-element.133), channel_id=1, source_target_pairs={{1,0},{2,1},{3,2},{4,3},{5,4},{6,5},{7,6},{8,7},{9,8},{10,9},{11,1... | collective-permute-start | bytes 835592 | tf_op jit(solution)/shard_map/ppermute | solution.py:22
  21.5 1.3 copy-start.6
  31.6 2.6 %copy-start.7 = (bf16[256,128]{1,0:T(8,128)(2,1)S(1)}, bf16[256,128]{1,0:T(8,128)(2,1)}, u32[]{:S(2)}) copy-start(bf16[256,128]{1,0:T(8,128)(2,1)} %param.29) | copy-start | bytes 196612
  32.1 3.1 %copy-start.8 = (f32[4,512]{1,0:T(4,128)S(1)}, f32[4,512]{1,0:T(4,128)}, u32[]{:S(2)}) copy-start(f32[4,512]{1,0:T(4,128)} %param.31) | copy-start | bytes 24580
  32.1 15.7 %collective-permute-start.2 = (f32[256,128]{1,0:T(8,128)S(1)}, f32[256,128]{1,0:T(8,128)S(1)}, u32[]{:S(2)}, u32[]{:S(2)}) collective-permute-start(f32[256,128]{1,0:T(8,128)S(1)} %convolution_bitcast_fusion.1), channel_id=1, source_target_pairs={{0,128},{128,0},{1,129},{129,1},{2,130},{130,2},{3,131},{131,3},{4... | collective-permute-start | bytes 393224 | tf_op jit(solution)/shard_map/ppermute | solution.py:71
  47.8 8.6 %collective-permute-start.3 = (f32[256,128]{1,0:T(8,128)S(1)}, f32[256,128]{1,0:T(8,128)S(1)}, u32[]{:S(2)}, u32[]{:S(2)}) collective-permute-start(f32[256,128]{1,0:T(8,128)S(1)} %add.1378), channel_id=1, source_target_pairs={{0,256},{256,0},{1,257},{257,1},{2,258},{258,2},{3,259},{259,3},{4... | collective-permute-start | bytes 393224 | tf_op jit(solution)/shard_map/ppermute | solution.py:71
  88.6 47.3 %copy-start.3 = (f32[2,266,128]{2,1,0:T(8,128)}, f32[2,266,128]{2,1,0:T(8,128)S(1)}, u32[]{:S(2)}) copy-start(f32[2,266,128]{2,1,0:T(8,128)S(1)} %all-gather.10) | copy-start | bytes 817156
  94.8 64.2 %copy-start.9 = (f32[1,10,128]{2,1,0:T(8,128)S(1)}, f32[1,10,128]{2,1,0:T(8,128)}, u32[]{:S(2)}) copy-start(f32[1,10,128]{2,1,0:T(8,128)} %constant.250.clone.1) | copy-start | bytes 15364
  102.4 0.8 copy-start.4
  129.7 0.8 copy-start.5
  158.4 5.2 %copy-start.1 = (bf16[4,512,128]{2,1,0:T(8,128)(2,1)S(1)}, bf16[4,512,128]{2,1,0:T(8,128)(2,1)}, u32[]{:S(2)}) copy-start(bf16[4,512,128]{2,1,0:T(8,128)(2,1)} %param.33) | copy-start | bytes 1572868

commit v9 on v7

--- a/solution.py
+++ b/solution.py
@@ -76,27 +76,31 @@
 
 
 def scan_and_sum(totals, grad, axes):
-    prefix = jnp.zeros_like(totals).at[0].set(1.0)
+    identity = (jnp.ones_like(totals[0]),) + tuple(jnp.zeros_like(item) for item in totals[1:])
+    prefix = identity
     rows = grad.shape[0]
+    width = totals[0].shape[0]
     for axis in axes:
         digit = lax.axis_index(axis)
-        packed = jnp.concatenate([grad, totals.reshape(-1, grad.shape[1])])
-        slots = lax.all_gather(packed, axis)
+        slots = lax.all_gather(jnp.concatenate((grad,) + tuple(totals)), axis)
         radix = slots.shape[0]
         grad = slots[0, :rows]
         for j in range(1, radix):
             grad = grad + slots[j, :rows]
-        parts = [slots[j, rows:].reshape(totals.shape) for j in range(radix)]
-        earlier = [jnp.zeros_like(totals).at[0].set(1.0)]
+        parts = [
+            tuple(slots[j, rows + k * width : rows + (k + 1) * width] for k in range(len(totals)))
+            for j in range(radix)
+        ]
+        earlier = [identity]
         running = parts[0]
         for item in parts[1:]:
             earlier.append(running)
-            running = jnp.stack(combine(tuple(running), tuple(item)))
+            running = combine(running, item)
         totals = running
         chosen = earlier[0]
         for j in range(1, radix):
-            chosen = jnp.where(digit == j, earlier[j], chosen)
-        prefix = jnp.stack(combine(tuple(chosen), tuple(prefix)))
+            chosen = tuple(jnp.where(digit == j, e, c) for e, c in zip(earlier[j], chosen))
+        prefix = combine(chosen, prefix)
     return prefix, grad
 
 def elements(obs, logp, params, present, keep, first):
@@ -172,9 +176,10 @@
     )
     grad_local = gather_sum(gather_sum(grad_local, "tl"), "th")
     local = doubling_prefix(elems, 2)
-    totals = jnp.stack([item[:, :, -1] for item in local])
+    totals = tuple(item[:, :, -1].reshape(-1, grad_local.shape[1]) for item in local)
     prefix, head_grad = scan_and_sum(totals, grad_local, TIME[::-1])
-    final = combine(tuple((item[:, :, None] for item in prefix)), local)
+    prefix = tuple(item.reshape(local[0].shape[:2])[:, :, None] for item in prefix)
+    final = combine(prefix, local)
     return (final[1], head_grad)
 
 

time: 143 us -> 137 us (0.958)
  the two profiles are of different devices: /device:TPU:26 before, /device:TPU:1 now
where the time goes in v9:
time: 137 us
  blocking collectives  78.8 us (58%)
  other arithmetic  19 us (14%)
  local copies, waits for them, and re-layouts  12.1 us (9%)
  starting transfers between devices  10.7 us (8%)
  matrix products  9.26 us (7%)
  between operations  7.06 us (5%)
    all_gather x7, blocking collectives, scan_and_sum(): slots = lax.all_gather(jnp.concatenate((grad,) + tuple(totals)), axis)  67.4 us
    all_gather x2, blocking collectives, gather_sum(): slots = lax.all_gather(value, axis)  11.4 us
    add x9, other arithmetic, combine(): new_c = a_two * a_two * c_one / denom + c_two  9.63 us
    ppermute x1, starting transfers between devices, extended_2(): lax.ppermute(lax.slice_in_dim(block, 0, width, axis=dim), axis, backward)  8.75 us
    dot_general x9, matrix products, conv_layer(): jnp.einsum('tfw,wv->tfv', piece, weights[tap], preferred_element_type=jnp...  8.3 us
    unnamed x24, local copies, waits for them, and re-layouts  2.97 us
  transfers between devices with their start and end apart: 2, of which 0 were waited for; matrix products, arithmetic and copies ran while one was open for 3% of the time, Pallas kernels for 0%

profile of v9, /device:TPU:1, one launch (start us, length us, event | category | flops | bytes accessed | tf_op | source)
XLA Modules:
  0.0 136.8 jit_solution(7240918811711222477)
XLA Ops:
  0.7 1.2 fusion.169
  1.9 8.7 %collective-permute-start.1 = (bf16[4,136,256]{2,1,0:T(8,128)(2,1)S(1)}, bf16[4,136,256]{2,1,0:T(8,128)(2,1)S(1)}, u32[]{:S(2)}, u32[]{:S(2)}) collective-permute-start(bf16[4,136,256]{2,1,0:T(8,128)(2,1)S(1)} %get-tuple-element.77), channel_id=1, source_target_pairs={{1,0},{2,1},{3,2},{4,3},{5,4},{6,5},{7,6},{8,7},{9,8},{10,9},{11,1... | collective-permute-start | bytes 835592 | tf_op jit(solution)/shard_map/ppermute | solution.py:22
  10.6 1.9 %collective-permute-start = (bf16[4,136,256]{2,1,0:T(8,128)(2,1)S(1)}, bf16[4,136,256]{2,1,0:T(8,128)(2,1)S(1)}, u32[]{:S(2)}, u32[]{:S(2)}) collective-permute-start(bf16[4,136,256]{2,1,0:T(8,128)(2,1)S(1)} %get-tuple-element.78), channel_id=1, source_target_pairs={{0,1},{1,2},{2,3},{3,4},{4,5},{5,6},{6,7},{7,8},{8,9},{9,10},{10,1... | collective-permute-start | bytes 835592 | tf_op jit(solution)/shard_map/ppermute | solution.py:19
  12.6 0.8 exponential_bitcast_fusion
  13.4 0.8 fusion.170
  14.2 1.4 %fusion.171 = (s32[1]{0:T(128)}, s32[1]{0:T(128)}, s32[1]{0:T(128)}) fusion(s32[3]{0:T(128)} %param.12), kind=kLoop, calls=%fused_computation.401 | loop fusion | bytes 24 | tf_op jit(solution)/shard_map/slice | solution.py:158
  22.4 1.1 copy-done.8
  24.7 2.0 %broadcast_select_fusion.1 = bf16[4,784,256]{2,1,0:T(8,128)(2,1)S(1)} fusion(pred[784]{0:T(1024)(128)(4,1)S(1)} %fusion.71, f32[256]{0:T(256)S(1)} %bitcast.695, s32[]{:T(128)S(6)} %select_n.474, bf16[4,784,256]{2,1,0:T(8,128)(2,1)S(1)} %constant_dynamic-update-slice_fusion, f32[4,784,256]{2,1,0:T(8,128)S(1)} %fusion.3, f32[4,784,256]{2,1,0:T(8,128)S(1)} %fusion.56, ...), kind=kOutput, calls=%fused_computation.21 | convolution fusion | flops 419872768 | bytes 11372548 | tf_op jit(solution)/shard_map/tfw,wv->tfv/dot_general | solution.py:127
  28.0 1.7 %broadcast_select_fusion = bf16[4,784,256]{2,1,0:T(8,128)(2,1)S(1)} fusion(pred[784]{0:T(1024)(128)(4,1)S(1)} %fusion.71, f32[256]{0:T(256)S(1)} %bitcast.694, f32[4,784,256]{2,1,0:T(8,128)S(1)} %fusion.6, f32[4,784,256]{2,1,0:T(8,128)S(1)} %fusion.5, bf16[4,784,256]{2,1,0:T(8,128)(2,1)S(1)} %broadcast_select_fusion.1, ...), kind=kOutput, calls=%fused_computation.20 | convolution fusion | flops 419872768 | bytes 11372544 | tf_op jit(solution)/shard_map/tfw,wv->tfv/dot_general | solution.py:127
  30.9 1.0 negate_exponential_fusion
  33.7 5.2 %all-gather = f32[512,128]{1,0:T(8,128)S(1)} all-gather(f32[256,128]{1,0:T(8,128)S(1)} %convolution_bitcast_fusion.1), channel_id=2, replica_groups=mesh['th'=2,'tl'=2,'z3'=2,'z2'=2,'z1'=2,'z0'=2,'xh'=2,'xl'=2,'core'=2] {..., dimensions={0}, use_global_device_ids=true | all-gather | bytes 393216 | tf_op jit(solution)/shard_map/all_gather | solution.py:71
  39.0 6.2 %all-gather.8 = f32[512,128]{1,0:T(8,128)S(1)} all-gather(f32[256,128]{1,0:T(8,128)S(1)} %slice_add_fusion.10), channel_id=10, replica_groups=mesh['th'=2,'tl'=2,'z3'=2,'z2'=2,'z1'=2,'z0'=2,'xh'=2,'xl'=2,'core'=2] {..., dimensions={0}, use_global_device_ids=true | all-gather | bytes 393216 | tf_op jit(solution)/shard_map/all_gather | solution.py:71
  45.6 0.8 divide_add_fusion.14
  46.5 1.1 divide_add_fusion.13
  47.6 1.3 divide_add_fusion.12
  48.9 1.3 divide_add_fusion.11
  50.2 1.3 divide_add_fusion.10
  51.5 1.3 divide_add_fusion.9
  52.8 1.3 divide_add_fusion.8
  54.1 1.2 fusion.20
  56.2 0.8 slice.700
  59.1 1.5 %fusion.28 = (f32[4,64,512]{2,1,0:T(8,128)S(1)}, f32[4,64,512]{2,1,0:T(8,128)S(1)}, f32[4,64,512]{2,1,0:T(8,128)S(1)}) fusion(f32[4,64,512]{2,1,0:T(8,128)S(1)} %get-tuple-element.17, f32[4,64,512]{2,1,0:T(8,128)S(1)} %get-tuple-element.15, f32[4,64,256]{2,1,0:T(8,128)} %copy-done.5, f32[4,64,256]{2,1,0:T(8,128)} %slice.668, f32[4,64,256]{2,1,0:T(8,128)S(1)} %slice.698, ...), kind=kLoop, calls=%fused_computation.64 | loop fusion | flops 1703936 | bytes 4456448 | tf_op jit(solution)/shard_map/add | solution.py:47
  61.4 4.2 %all-gather.9 = f32[2,266,128]{2,1,0:T(8,128)S(1)} all-gather(f32[1,266,128]{2,1,0:T(8,128)S(1)} %bitcast.686), channel_id=3, replica_groups=mesh['th'=2,'tl'=2,'z3'=2,'z2'=2,'z1'=2,'z0'=2,'xh'=2,'xl'=2,'core'=2] {..., dimensions={0}, use_global_device_ids=true | all-gather | bytes 408576 | tf_op jit(solution)/shard_map/all_gather | solution.py:85
  65.6 5.5 %all-gather.10 = f32[2,266,128]{2,1,0:T(8,128)S(1)} all-gather(f32[1,266,128]{2,1,0:T(8,128)S(1)} %bitcast.687), channel_id=4, replica_groups=mesh['th'=2,'tl'=2,'z3'=2,'z2'=2,'z1'=2,'z0'=2,'xh'=2,'xl'=2,'core'=2] {..., dimensions={0}, use_global_device_ids=true | all-gather | bytes 408576 | tf_op jit(solution)/shard_map/all_gather | solution.py:85
  71.2 6.1 %all-gather.11 = f32[2,266,128]{2,1,0:T(8,128)S(1)} all-gather(f32[1,266,128]{2,1,0:T(8,128)S(1)} %bitcast.688), channel_id=5, replica_groups=mesh['th'=2,'tl'=2,'z3'=2,'z2'=2,'z1'=2,'z0'=2,'xh'=2,'xl'=2,'core'=2] {..., dimensions={0}, use_global_device_ids=true | all-gather | bytes 408576 | tf_op jit(solution)/shard_map/all_gather | solution.py:85
  77.4 4.6 %all-gather.12 = f32[2,266,128]{2,1,0:T(8,128)S(1)} all-gather(f32[1,266,128]{2,1,0:T(8,128)S(1)} %bitcast.689), channel_id=6, replica_groups=mesh['th'=2,'tl'=2,'z3'=2,'z2'=2,'z1'=2,'z0'=2,'xh'=2,'xl'=2,'core'=2] {..., dimensions={0}, use_global_device_ids=true | all-gather | bytes 408576 | tf_op jit(solution)/shard_map/all_gather | solution.py:85
  82.7 6.8 %all-gather.13 = f32[2,266,128]{2,1,0:T(8,128)S(1)} all-gather(f32[1,266,128]{2,1,0:T(8,128)S(1)} %bitcast.690), channel_id=7, replica_groups=mesh['th'=2,'tl'=2,'z3'=2,'z2'=2,'z1'=2,'z0'=2,'xh'=2,'xl'=2,'core'=2] {..., dimensions={0}, use_global_device_ids=true | all-gather | bytes 408576 | tf_op jit(solution)/shard_map/all_gather | solution.py:85
  90.2 18.0 %all-gather.14 = f32[2,266,128]{2,1,0:T(8,128)S(1)} all-gather(f32[1,266,128]{2,1,0:T(8,128)S(1)} %bitcast.691), channel_id=8, replica_groups=mesh['th'=2,'tl'=2,'z3'=2,'z2'=2,'z1'=2,'z0'=2,'xh'=2,'xl'=2,'core'=2] {..., dimensions={0}, use_global_device_ids=true | all-gather | bytes 408576 | tf_op jit(solution)/shard_map/all_gather | solution.py:85
  109.5 0.8 broadcast_select_fusion.13
  110.8 0.8 broadcast_select_fusion.8
  112.5 22.3 %all-gather.15 = f32[2,266,128]{2,1,0:T(8,128)S(1)} all-gather(f32[1,266,128]{2,1,0:T(8,128)S(1)} %bitcast.692), channel_id=9, replica_groups=mesh['th'=2,'tl'=2,'z3'=2,'z2'=2,'z1'=2,'z0'=2,'xh'=2,'xl'=2,'core'=2] {..., dimensions={0}, use_global_device_ids=true | all-gather | bytes 408576 | tf_op jit(solution)/shard_map/all_gather | solution.py:85
  135.8 1.0 divide_add_fusion
  (126 shorter events, 15.7 us)
Async XLA Ops:
  0.6 31.8 %copy-start = (bf16[4,512,128]{2,1,0:T(8,128)(2,1)S(1)}, bf16[4,512,128]{2,1,0:T(8,128)(2,1)}, u32[]{:S(2)}) copy-start(bf16[4,512,128]{2,1,0:T(8,128)(2,1)} %param.17) | copy-start | bytes 1572868
  0.6 21.7 %copy-start.4 = (bf16[4,512,256]{2,1,0:T(8,128)(2,1)S(1)}, bf16[4,512,256]{2,1,0:T(8,128)(2,1)}, u32[]{:S(2)}) copy-start(bf16[4,512,256]{2,1,0:T(8,128)(2,1)} %param.9) | copy-start | bytes 3145732
  1.9 20.6 %collective-permute-start.1 = (bf16[4,136,256]{2,1,0:T(8,128)(2,1)S(1)}, bf16[4,136,256]{2,1,0:T(8,128)(2,1)S(1)}, u32[]{:S(2)}, u32[]{:S(2)}) collective-permute-start(bf16[4,136,256]{2,1,0:T(8,128)(2,1)S(1)} %get-tuple-element.77), channel_id=1, source_target_pairs={{1,0},{2,1},{3,2},{4,3},{5,4},{6,5},{7,6},{8,7},{9,8},{10,9},{11,1... | collective-permute-start | bytes 835592 | tf_op jit(solution)/shard_map/ppermute | solution.py:22
  10.6 11.7 %collective-permute-start = (bf16[4,136,256]{2,1,0:T(8,128)(2,1)S(1)}, bf16[4,136,256]{2,1,0:T(8,128)(2,1)S(1)}, u32[]{:S(2)}, u32[]{:S(2)}) collective-permute-start(bf16[4,136,256]{2,1,0:T(8,128)(2,1)S(1)} %get-tuple-element.78), channel_id=1, source_target_pairs={{0,1},{1,2},{2,3},{3,4},{4,5},{5,6},{6,7},{7,8},{8,9},{9,10},{10,1... | collective-permute-start | bytes 835592 | tf_op jit(solution)/shard_map/ppermute | solution.py:19
  22.3 1.3 copy-start.8
  32.4 0.8 copy-start.9
  33.7 11.9 %copy-start.10 = (f32[4,512]{1,0:T(4,128)S(1)}, f32[4,512]{1,0:T(4,128)}, u32[]{:S(2)}) copy-start(f32[4,512]{1,0:T(4,128)} %param.15) | copy-start | bytes 24580
  56.2 1.3 copy-start.5
  57.5 0.9 copy-start.2
  82.0 0.7 copy-start.6
  82.7 53.1 %copy-start.3 = (f32[4,64,512]{2,1,0:T(8,128)S(1)}, f32[4,64,512]{2,1,0:T(8,128)}, u32[]{:S(2)}) copy-start(f32[4,64,512]{2,1,0:T(8,128)} %copy-done.2) | copy-start | bytes 1572868
  89.4 0.7 copy-start.7
  112.5 24.3 %copy-start.1 = (bf16[4,512,128]{2,1,0:T(8,128)(2,1)S(1)}, bf16[4,512,128]{2,1,0:T(8,128)(2,1)}, u32[]{:S(2)}) copy-start(bf16[4,512,128]{2,1,0:T(8,128)(2,1)} %param.17) | copy-start | bytes 1572868

commit v10 on v9

--- a/solution.py
+++ b/solution.py
@@ -9,6 +9,7 @@
 HALO = 136
 TIME = ("z3", "z2", "z1", "z0", "xh", "xl", "core")
 TAKE = ("th", "tl")
+ROUNDS = ((("tl",), "core"), (("th",), "xl"), ((), "xh"), ((), "z0"), ((), "z1"), ((), "z2"), ((), "z3"))
 
 
 def extended_2(block, sides, width):
@@ -75,18 +76,21 @@
     return total
 
 
-def scan_and_sum(totals, grad, axes):
+def scan_and_sum(totals, grad, rounds):
     identity = (jnp.ones_like(totals[0]),) + tuple(jnp.zeros_like(item) for item in totals[1:])
     prefix = identity
     rows = grad.shape[0]
     width = totals[0].shape[0]
-    for axis in axes:
+    for extra, axis in rounds:
         digit = lax.axis_index(axis)
-        slots = lax.all_gather(jnp.concatenate((grad,) + tuple(totals)), axis)
-        radix = slots.shape[0]
+        slots = lax.all_gather(jnp.concatenate((grad,) + tuple(totals)), extra + (axis,))
         grad = slots[0, :rows]
-        for j in range(1, radix):
+        for j in range(1, slots.shape[0]):
             grad = grad + slots[j, :rows]
+        radix = lax.axis_size(axis)
+        if extra:
+            slots = slots.reshape((-1, radix) + slots.shape[1:])
+            slots = lax.dynamic_index_in_dim(slots, lax.axis_index(extra), 0, False)
         parts = [
             tuple(slots[j, rows + k * width : rows + (k + 1) * width] for k in range(len(totals)))
             for j in range(radix)
@@ -174,10 +178,9 @@
     grad_local = jnp.einsum(
         "tfw,tfs->ws", hidden, head_cotangent, preferred_element_type=jnp.float32
     )
-    grad_local = gather_sum(gather_sum(grad_local, "tl"), "th")
     local = doubling_prefix(elems, 2)
     totals = tuple(item[:, :, -1].reshape(-1, grad_local.shape[1]) for item in local)
-    prefix, head_grad = scan_and_sum(totals, grad_local, TIME[::-1])
+    prefix, head_grad = scan_and_sum(totals, grad_local, ROUNDS)
     prefix = tuple(item.reshape(local[0].shape[:2])[:, :, None] for item in prefix)
     final = combine(prefix, local)
     return (final[1], head_grad)

time: 137 us -> 144 us (1.051)
  blocking collectives: 78.8 us -> 82.7 us
  other arithmetic: 19 us -> 20.6 us
    all_gather x9 -> x7, blocking collectives: 78.8 us -> 82.7 us  [scan_and_sum(): lax.all_gather(jnp.concatenate((grad,) + tuple(totals)), extra + (axis,))]
    unnamed x24 -> x22, local copies, waits for them, and re-layouts: 2.97 us -> 2.35 us
where the time goes in v10:
time: 144 us; the launch traced here: 143 us
  blocking collectives  82.7 us (57%)
  other arithmetic  20.6 us (14%)
  local copies, waits for them, and re-layouts  12.2 us (8%)
  starting transfers between devices  10.7 us (7%)
  matrix products  9.42 us (7%)
  between operations  7.04 us (5%)
    all_gather x7, blocking collectives, scan_and_sum(): lax.all_gather(jnp.concatenate((grad,) + tuple(totals)), extra + (axis,))  82.7 us
    add x9, other arithmetic, combine(): new_c = a_two * a_two * c_one / denom + c_two  9.85 us
    ppermute x1, starting transfers between devices, extended_2(): lax.ppermute(lax.slice_in_dim(block, 0, width, axis=dim), axis, backward)  8.75 us
    dot_general x9, matrix products, conv_layer(): jnp.einsum('tfw,wv->tfv', piece, weights[tap], preferred_element_type=jnp...  8.46 us
  transfers between devices with their start and end apart: 2, of which 0 were waited for; matrix products, arithmetic and copies ran while one was open for 3% of the time, Pallas kernels for 0%

profile of v10, /device:TPU:1, one launch (start us, length us, event | category | flops | bytes accessed | tf_op | source)
XLA Modules:
  0.0 142.6 jit_solution(13432721578066545291)
XLA Ops:
  0.7 1.2 fusion.169
  1.9 8.7 %collective-permute-start.1 = (bf16[4,136,256]{2,1,0:T(8,128)(2,1)S(1)}, bf16[4,136,256]{2,1,0:T(8,128)(2,1)S(1)}, u32[]{:S(2)}, u32[]{:S(2)}) collective-permute-start(bf16[4,136,256]{2,1,0:T(8,128)(2,1)S(1)} %get-tuple-element.77), channel_id=1, source_target_pairs={{1,0},{2,1},{3,2},{4,3},{5,4},{6,5},{7,6},{8,7},{9,8},{10,9},{11,1... | collective-permute-start | bytes 835592 | tf_op jit(solution)/shard_map/ppermute | solution.py:23
  10.6 1.9 %collective-permute-start = (bf16[4,136,256]{2,1,0:T(8,128)(2,1)S(1)}, bf16[4,136,256]{2,1,0:T(8,128)(2,1)S(1)}, u32[]{:S(2)}, u32[]{:S(2)}) collective-permute-start(bf16[4,136,256]{2,1,0:T(8,128)(2,1)S(1)} %get-tuple-element.78), channel_id=1, source_target_pairs={{0,1},{1,2},{2,3},{3,4},{4,5},{5,6},{6,7},{7,8},{8,9},{9,10},{10,1... | collective-permute-start | bytes 835592 | tf_op jit(solution)/shard_map/ppermute | solution.py:20
  12.6 0.8 exponential_bitcast_fusion
  13.4 0.8 fusion.170
  14.2 1.4 fusion.171
  22.4 1.1 copy-done.6
  24.7 2.0 %broadcast_select_fusion.1 = bf16[4,784,256]{2,1,0:T(8,128)(2,1)S(1)} fusion(pred[784]{0:T(1024)(128)(4,1)S(1)} %fusion.71, f32[256]{0:T(256)S(1)} %bitcast.703, s32[]{:T(128)S(6)} %select_n.481, bf16[4,784,256]{2,1,0:T(8,128)(2,1)S(1)} %constant_dynamic-update-slice_fusion, f32[4,784,256]{2,1,0:T(8,128)S(1)} %fusion.3, f32[4,784,256]{2,1,0:T(8,128)S(1)} %fusion.56, ...), kind=kOutput, calls=%fused_computation.21 | convolution fusion | flops 419872768 | bytes 11372548 | tf_op jit(solution)/shard_map/tfw,wv->tfv/dot_general | solution.py:131
  27.9 1.9 %broadcast_select_fusion = bf16[4,784,256]{2,1,0:T(8,128)(2,1)S(1)} fusion(pred[784]{0:T(1024)(128)(4,1)S(1)} %fusion.71, f32[256]{0:T(256)S(1)} %bitcast.702, f32[4,784,256]{2,1,0:T(8,128)S(1)} %fusion.6, f32[4,784,256]{2,1,0:T(8,128)S(1)} %fusion.5, bf16[4,784,256]{2,1,0:T(8,128)(2,1)S(1)} %broadcast_select_fusion.1, ...), kind=kOutput, calls=%fused_computation.20 | convolution fusion | flops 419872768 | bytes 11372544 | tf_op jit(solution)/shard_map/tfw,wv->tfv/dot_general | solution.py:131
  31.0 1.0 negate_exponential_fusion
  34.3 0.8 divide_add_fusion.14
  35.2 1.1 divide_add_fusion.13
  36.3 1.3 divide_add_fusion.12
  37.6 1.3 divide_add_fusion.11
  38.9 1.3 divide_add_fusion.10
  40.2 1.3 divide_add_fusion.9
  41.5 1.5 %divide_add_fusion.8 = (f32[4,64,512]{2,1,0:T(8,128)S(1)}, f32[4,64,512]{2,1,0:T(8,128)S(1)}, f32[4,64,512]{2,1,0:T(8,128)S(1)}, f32[4,64,512]{2,1,0:T(8,128)S(1)}, f32[4,64,512]{2,1,0:T(8,128)S(1)}) fusion(f32[4,64,512]{2,1,0:T(8,128)S(1)} %get-tuple-element.29, f32[4,64,448]{2,1,0:T(8,128)S(1)} %bitcast.629, f32[4,64,480]{2,1,0:T(8,128)S(1)} %bitcast.657, ...), kind=kLoop, calls=%fused_computation.93 | loop fusion | flops 3407872 | bytes 10223616 | tf_op jit(solution)/shard_map/add | solution.py:47
  43.1 1.2 fusion.20
  45.2 0.8 slice.692
  46.5 0.8 slice.664
  47.9 1.5 %fusion.28 = (f32[4,64,512]{2,1,0:T(8,128)S(1)}, f32[4,64,512]{2,1,0:T(8,128)S(1)}, f32[4,64,512]{2,1,0:T(8,128)S(1)}) fusion(f32[4,64,512]{2,1,0:T(8,128)S(1)} %get-tuple-element.17, f32[4,64,512]{2,1,0:T(8,128)S(1)} %get-tuple-element.15, f32[4,64,256]{2,1,0:T(8,128)} %copy-done.5, f32[4,64,256]{2,1,0:T(8,128)} %slice.664, f32[4,64,256]{2,1,0:T(8,128)S(1)} %slice.690, ...), kind=kLoop, calls=%fused_computation.64 | loop fusion | flops 1703936 | bytes 4456448 | tf_op jit(solution)/shard_map/add | solution.py:48
  50.1 7.4 %all-gather.7 = f32[4,266,128]{2,1,0:T(8,128)S(1)} all-gather(f32[1,266,128]{2,1,0:T(8,128)S(1)} %bitcast.694), channel_id=2, replica_groups=mesh['th'=2,'tl'=2,'z3'=2,'z2'=2,'z1'=2,'z0'=2,'xh'=2,'xl'=2,'core'=2] {..., dimensions={0}, use_global_device_ids=true | all-gather | bytes 680960 | tf_op jit(solution)/shard_map/all_gather | solution.py:86
  59.1 0.9 bitcast_add_fusion.16
  60.0 14.1 %all-gather.8 = f32[4,266,128]{2,1,0:T(8,128)S(1)} all-gather(f32[1,266,128]{2,1,0:T(8,128)S(1)} %bitcast.695), channel_id=3, replica_groups=mesh['th'=2,'tl'=2,'z3'=2,'z2'=2,'z1'=2,'z0'=2,'xh'=2,'xl'=2,'core'=2] {..., dimensions={0}, use_global_device_ids=true | all-gather | bytes 680960 | tf_op jit(solution)/shard_map/all_gather | solution.py:86
  75.0 6.1 %all-gather.9 = f32[2,266,128]{2,1,0:T(8,128)S(1)} all-gather(f32[1,266,128]{2,1,0:T(8,128)S(1)} %bitcast.696), channel_id=4, replica_groups=mesh['th'=2,'tl'=2,'z3'=2,'z2'=2,'z1'=2,'z0'=2,'xh'=2,'xl'=2,'core'=2] {..., dimensions={0}, use_global_device_ids=true | all-gather | bytes 408576 | tf_op jit(solution)/shard_map/all_gather | solution.py:86
  81.1 4.6 %all-gather.10 = f32[2,266,128]{2,1,0:T(8,128)S(1)} all-gather(f32[1,266,128]{2,1,0:T(8,128)S(1)} %bitcast.697), channel_id=5, replica_groups=mesh['th'=2,'tl'=2,'z3'=2,'z2'=2,'z1'=2,'z0'=2,'xh'=2,'xl'=2,'core'=2] {..., dimensions={0}, use_global_device_ids=true | all-gather | bytes 408576 | tf_op jit(solution)/shard_map/all_gather | solution.py:86
  85.8 8.3 %all-gather.11 = f32[2,266,128]{2,1,0:T(8,128)S(1)} all-gather(f32[1,266,128]{2,1,0:T(8,128)S(1)} %bitcast.698), channel_id=6, replica_groups=mesh['th'=2,'tl'=2,'z3'=2,'z2'=2,'z1'=2,'z0'=2,'xh'=2,'xl'=2,'core'=2] {..., dimensions={0}, use_global_device_ids=true | all-gather | bytes 408576 | tf_op jit(solution)/shard_map/all_gather | solution.py:86
  94.1 20.2 %all-gather.12 = f32[2,266,128]{2,1,0:T(8,128)S(1)} all-gather(f32[1,266,128]{2,1,0:T(8,128)S(1)} %bitcast.699), channel_id=7, replica_groups=mesh['th'=2,'tl'=2,'z3'=2,'z2'=2,'z1'=2,'z0'=2,'xh'=2,'xl'=2,'core'=2] {..., dimensions={0}, use_global_device_ids=true | all-gather | bytes 408576 | tf_op jit(solution)/shard_map/all_gather | solution.py:86
  114.3 0.8 broadcast_select_fusion.28
  115.6 0.8 broadcast_select_fusion.23
  118.6 22.0 %all-gather.13 = f32[2,266,128]{2,1,0:T(8,128)S(1)} all-gather(f32[1,266,128]{2,1,0:T(8,128)S(1)} %bitcast.700), channel_id=8, replica_groups=mesh['th'=2,'tl'=2,'z3'=2,'z2'=2,'z1'=2,'z0'=2,'xh'=2,'xl'=2,'core'=2] {..., dimensions={0}, use_global_device_ids=true | all-gather | bytes 408576 | tf_op jit(solution)/shard_map/all_gather | solution.py:86
  141.6 1.0 divide_add_fusion
  (122 shorter events, 15.6 us)
Async XLA Ops:
  0.6 31.9 %copy-start = (bf16[4,512,128]{2,1,0:T(8,128)(2,1)S(1)}, bf16[4,512,128]{2,1,0:T(8,128)(2,1)}, u32[]{:S(2)}) copy-start(bf16[4,512,128]{2,1,0:T(8,128)(2,1)} %param.17) | copy-start | bytes 1572868
  0.6 21.7 %copy-start.4 = (bf16[4,512,256]{2,1,0:T(8,128)(2,1)S(1)}, bf16[4,512,256]{2,1,0:T(8,128)(2,1)}, u32[]{:S(2)}) copy-start(bf16[4,512,256]{2,1,0:T(8,128)(2,1)} %param.9) | copy-start | bytes 3145732
  1.9 20.5 %collective-permute-start.1 = (bf16[4,136,256]{2,1,0:T(8,128)(2,1)S(1)}, bf16[4,136,256]{2,1,0:T(8,128)(2,1)S(1)}, u32[]{:S(2)}, u32[]{:S(2)}) collective-permute-start(bf16[4,136,256]{2,1,0:T(8,128)(2,1)S(1)} %get-tuple-element.77), channel_id=1, source_target_pairs={{1,0},{2,1},{3,2},{4,3},{5,4},{6,5},{7,6},{8,7},{9,8},{10,9},{11,1... | collective-permute-start | bytes 835592 | tf_op jit(solution)/shard_map/ppermute | solution.py:23
  10.6 11.7 %collective-permute-start = (bf16[4,136,256]{2,1,0:T(8,128)(2,1)S(1)}, bf16[4,136,256]{2,1,0:T(8,128)(2,1)S(1)}, u32[]{:S(2)}, u32[]{:S(2)}) collective-permute-start(bf16[4,136,256]{2,1,0:T(8,128)(2,1)S(1)} %get-tuple-element.78), channel_id=1, source_target_pairs={{0,1},{1,2},{2,3},{3,4},{4,5},{5,6},{6,7},{7,8},{8,9},{9,10},{10,1... | collective-permute-start | bytes 835592 | tf_op jit(solution)/shard_map/ppermute | solution.py:20
  22.3 1.3 copy-start.6
  32.6 0.8 copy-start.8
  33.4 0.9 copy-start.9
  45.2 1.3 copy-start.5
  46.5 0.9 copy-start.2
  74.2 0.7 copy-start.7
  85.8 55.8 %copy-start.3 = (f32[4,64,512]{2,1,0:T(8,128)S(1)}, f32[4,64,512]{2,1,0:T(8,128)}, u32[]{:S(2)}) copy-start(f32[4,64,512]{2,1,0:T(8,128)} %copy-done.2) | copy-start | bytes 1572868
  118.6 24.0 %copy-start.1 = (bf16[4,512,128]{2,1,0:T(8,128)(2,1)S(1)}, bf16[4,512,128]{2,1,0:T(8,128)(2,1)}, u32[]{:S(2)}) copy-start(bf16[4,512,128]{2,1,0:T(8,128)(2,1)} %param.17) | copy-start | bytes 1572868

commit v11 on v9

--- a/solution.py
+++ b/solution.py
@@ -65,6 +65,10 @@
         result = combine(tuple(moved), result)
         offset = offset * 2
     return result
+
+
+def pair_sum(value, axis):
+    return value + lax.ppermute(value, axis, [(0, 1), (1, 0)])
 
 
 def gather_sum(value, axis):
@@ -174,7 +178,7 @@
     grad_local = jnp.einsum(
         "tfw,tfs->ws", hidden, head_cotangent, preferred_element_type=jnp.float32
     )
-    grad_local = gather_sum(gather_sum(grad_local, "tl"), "th")
+    grad_local = pair_sum(pair_sum(grad_local, "tl"), "th")
     local = doubling_prefix(elems, 2)
     totals = tuple(item[:, :, -1].reshape(-1, grad_local.shape[1]) for item in local)
     prefix, head_grad = scan_and_sum(totals, grad_local, TIME[::-1])

time: 137 us -> 133 us (0.971)
  the two profiles are of different devices: /device:TPU:1 before, /device:TPU:3 now
where the time goes in v11:
time: 133 us; the launch traced here: 132 us
  blocking collectives  71 us (53%)
  other arithmetic  17.8 us (13%)
  starting transfers between devices  13.5 us (10%)
  local copies, waits for them, and re-layouts  10.5 us (8%)
  matrix products  9.25 us (7%)
  between operations  7.04 us (5%)
  waiting for transfers between devices  3.37 us (3%)
    all_gather x7, blocking collectives, scan_and_sum(): slots = lax.all_gather(jnp.concatenate((grad,) + tuple(totals)), axis)  71 us
    add x9, other arithmetic, combine(): new_c = a_two * a_two * c_one / denom + c_two  9.63 us
    dot_general x9, matrix products, conv_layer(): jnp.einsum('tfw,wv->tfv', piece, weights[tap], preferred_element_type=jnp...  8.29 us
    ppermute x2, starting transfers between devices, pair_sum(): return value + lax.ppermute(value, axis, [(0, 1), (1, 0)])  7.92 us
    ppermute x2, waiting for transfers between devices, pair_sum(): return value + lax.ppermute(value, axis, [(0, 1), (1, 0)])  3.36 us
    ppermute x1, starting transfers between devices, extended_2(): lax.ppermute(lax.slice_in_dim(block, block.shape[dim] - width, None, axis...  3.02 us
    unnamed x18, local copies, waits for them, and re-layouts  2.91 us
  transfers between devices with their start and end apart: 4, of which 1 were waited for; matrix products, arithmetic and copies ran while one was open for 13% of the time, Pallas kernels for 0%

profile of v11, /device:TPU:3, one launch (start us, length us, event | category | flops | bytes accessed | tf_op | source)
XLA Modules:
  0.0 132.5 jit_solution(7573488230593974239)
XLA Ops:
  0.7 1.2 fusion.169
  1.9 2.6 %collective-permute-start.1 = (bf16[4,136,256]{2,1,0:T(8,128)(2,1)S(1)}, bf16[4,136,256]{2,1,0:T(8,128)(2,1)S(1)}, u32[]{:S(2)}, u32[]{:S(2)}) collective-permute-start(bf16[4,136,256]{2,1,0:T(8,128)(2,1)S(1)} %get-tuple-element.77), channel_id=1, source_target_pairs={{1,0},{2,1},{3,2},{4,3},{5,4},{6,5},{7,6},{8,7},{9,8},{10,9},{11,1... | collective-permute-start | bytes 835592 | tf_op jit(solution)/shard_map/ppermute | solution.py:22
  4.4 3.0 %collective-permute-start = (bf16[4,136,256]{2,1,0:T(8,128)(2,1)S(1)}, bf16[4,136,256]{2,1,0:T(8,128)(2,1)S(1)}, u32[]{:S(2)}, u32[]{:S(2)}) collective-permute-start(bf16[4,136,256]{2,1,0:T(8,128)(2,1)S(1)} %get-tuple-element.78), channel_id=1, source_target_pairs={{0,1},{1,2},{2,3},{3,4},{4,5},{5,6},{6,7},{7,8},{8,9},{9,10},{10,1... | collective-permute-start | bytes 835592 | tf_op jit(solution)/shard_map/ppermute | solution.py:19
  7.5 0.8 exponential_bitcast_fusion
  8.3 0.8 fusion.170
  9.1 1.4 %fusion.171 = (s32[1]{0:T(128)}, s32[1]{0:T(128)}, s32[1]{0:T(128)}) fusion(s32[3]{0:T(128)} %param.12), kind=kLoop, calls=%fused_computation.399 | loop fusion | bytes 24 | tf_op jit(solution)/shard_map/slice | solution.py:162
  17.4 1.1 copy-done.5
  19.7 2.0 %broadcast_select_fusion.1 = bf16[4,784,256]{2,1,0:T(8,128)(2,1)S(1)} fusion(pred[784]{0:T(1024)(128)(4,1)S(1)} %fusion.71, f32[256]{0:T(256)S(1)} %bitcast.695, s32[]{:T(128)S(6)} %select_n.474, bf16[4,784,256]{2,1,0:T(8,128)(2,1)S(1)} %constant_dynamic-update-slice_fusion, f32[4,784,256]{2,1,0:T(8,128)S(1)} %fusion.3, f32[4,784,256]{2,1,0:T(8,128)S(1)} %fusion.56, ...), kind=kOutput, calls=%fused_computation.21 | convolution fusion | flops 419872768 | bytes 11372548 | tf_op jit(solution)/shard_map/tfw,wv->tfv/dot_general | solution.py:131
  22.9 1.7 %broadcast_select_fusion = bf16[4,784,256]{2,1,0:T(8,128)(2,1)S(1)} fusion(pred[784]{0:T(1024)(128)(4,1)S(1)} %fusion.71, f32[256]{0:T(256)S(1)} %bitcast.694, f32[4,784,256]{2,1,0:T(8,128)S(1)} %fusion.6, f32[4,784,256]{2,1,0:T(8,128)S(1)} %fusion.5, bf16[4,784,256]{2,1,0:T(8,128)(2,1)S(1)} %broadcast_select_fusion.1, ...), kind=kOutput, calls=%fused_computation.20 | convolution fusion | flops 419872768 | bytes 11372544 | tf_op jit(solution)/shard_map/tfw,wv->tfv/dot_general | solution.py:131
  25.8 1.0 negate_exponential_fusion
  28.6 3.4 %collective-permute-start.2 = (f32[256,128]{1,0:T(8,128)S(1)}, f32[256,128]{1,0:T(8,128)S(1)}, u32[]{:S(2)}, u32[]{:S(2)}) collective-permute-start(f32[256,128]{1,0:T(8,128)S(1)} %convolution_bitcast_fusion.1), channel_id=1, source_target_pairs={{0,128},{128,0},{1,129},{129,1},{2,130},{130,2},{3,131},{131,3},{4... | collective-permute-start | bytes 393224 | tf_op jit(solution)/shard_map/ppermute | solution.py:71
  32.5 0.8 divide_add_fusion.14
  33.3 1.1 divide_add_fusion.13
  34.5 1.3 divide_add_fusion.12
  35.8 1.3 divide_add_fusion.11
  37.1 1.3 divide_add_fusion.10
  38.4 1.3 divide_add_fusion.9
  39.7 1.3 divide_add_fusion.8
  41.0 1.2 fusion.20
  42.3 0.7 fusion.21
  44.6 4.5 %collective-permute-start.3 = (f32[256,128]{1,0:T(8,128)S(1)}, f32[256,128]{1,0:T(8,128)S(1)}, u32[]{:S(2)}, u32[]{:S(2)}) collective-permute-start(f32[256,128]{1,0:T(8,128)S(1)} %add.1017), channel_id=1, source_target_pairs={{0,256},{256,0},{1,257},{257,1},{2,258},{258,2},{3,259},{259,3},{4... | collective-permute-start | bytes 393224 | tf_op jit(solution)/shard_map/ppermute | solution.py:71
  50.0 3.4 %collective-permute-done.3 = f32[256,128]{1,0:T(8,128)S(1)} collective-permute-done((f32[256,128]{1,0:T(8,128)S(1)}, f32[256,128]{1,0:T(8,128)S(1)}, u32[]{:S(2)}, u32[]{:S(2)}) %collective-permute-start.3) | collective-permute-done | bytes 131104 | tf_op jit(solution)/shard_map/ppermute | solution.py:71
  53.4 2.2 %all-gather.7 = f32[2,266,128]{2,1,0:T(8,128)S(1)} all-gather(f32[1,266,128]{2,1,0:T(8,128)S(1)} %bitcast.686), channel_id=2, replica_groups=mesh['th'=2,'tl'=2,'z3'=2,'z2'=2,'z1'=2,'z0'=2,'xh'=2,'xl'=2,'core'=2] {..., dimensions={0}, use_global_device_ids=true | all-gather | bytes 408576 | tf_op jit(solution)/shard_map/all_gather | solution.py:89
  55.7 7.6 %all-gather.8 = f32[2,266,128]{2,1,0:T(8,128)S(1)} all-gather(f32[1,266,128]{2,1,0:T(8,128)S(1)} %bitcast.687), channel_id=3, replica_groups=mesh['th'=2,'tl'=2,'z3'=2,'z2'=2,'z1'=2,'z0'=2,'xh'=2,'xl'=2,'core'=2] {..., dimensions={0}, use_global_device_ids=true | all-gather | bytes 408576 | tf_op jit(solution)/shard_map/all_gather | solution.py:89
  63.4 6.4 %all-gather.9 = f32[2,266,128]{2,1,0:T(8,128)S(1)} all-gather(f32[1,266,128]{2,1,0:T(8,128)S(1)} %bitcast.688), channel_id=4, replica_groups=mesh['th'=2,'tl'=2,'z3'=2,'z2'=2,'z1'=2,'z0'=2,'xh'=2,'xl'=2,'core'=2] {..., dimensions={0}, use_global_device_ids=true | all-gather | bytes 408576 | tf_op jit(solution)/shard_map/all_gather | solution.py:89
  69.9 4.6 %all-gather.10 = f32[2,266,128]{2,1,0:T(8,128)S(1)} all-gather(f32[1,266,128]{2,1,0:T(8,128)S(1)} %bitcast.689), channel_id=5, replica_groups=mesh['th'=2,'tl'=2,'z3'=2,'z2'=2,'z1'=2,'z0'=2,'xh'=2,'xl'=2,'core'=2] {..., dimensions={0}, use_global_device_ids=true | all-gather | bytes 408576 | tf_op jit(solution)/shard_map/all_gather | solution.py:89
  75.2 6.9 %all-gather.11 = f32[2,266,128]{2,1,0:T(8,128)S(1)} all-gather(f32[1,266,128]{2,1,0:T(8,128)S(1)} %bitcast.690), channel_id=6, replica_groups=mesh['th'=2,'tl'=2,'z3'=2,'z2'=2,'z1'=2,'z0'=2,'xh'=2,'xl'=2,'core'=2] {..., dimensions={0}, use_global_device_ids=true | all-gather | bytes 408576 | tf_op jit(solution)/shard_map/all_gather | solution.py:89
  82.9 20.7 %all-gather.12 = f32[2,266,128]{2,1,0:T(8,128)S(1)} all-gather(f32[1,266,128]{2,1,0:T(8,128)S(1)} %bitcast.691), channel_id=7, replica_groups=mesh['th'=2,'tl'=2,'z3'=2,'z2'=2,'z1'=2,'z0'=2,'xh'=2,'xl'=2,'core'=2] {..., dimensions={0}, use_global_device_ids=true | all-gather | bytes 408576 | tf_op jit(solution)/shard_map/all_gather | solution.py:89
  104.9 0.8 broadcast_select_fusion.13
  106.2 0.8 broadcast_select_fusion.8
  107.9 22.6 %all-gather.13 = f32[2,266,128]{2,1,0:T(8,128)S(1)} all-gather(f32[1,266,128]{2,1,0:T(8,128)S(1)} %bitcast.692), channel_id=8, replica_groups=mesh['th'=2,'tl'=2,'z3'=2,'z2'=2,'z1'=2,'z0'=2,'xh'=2,'xl'=2,'core'=2] {..., dimensions={0}, use_global_device_ids=true | all-gather | bytes 408576 | tf_op jit(solution)/shard_map/all_gather | solution.py:89
  131.5 1.0 divide_add_fusion
  (122 shorter events, 14.5 us)
Async XLA Ops:
  0.6 26.7 %copy-start = (bf16[4,512,128]{2,1,0:T(8,128)(2,1)S(1)}, bf16[4,512,128]{2,1,0:T(8,128)(2,1)}, u32[]{:S(2)}) copy-start(bf16[4,512,128]{2,1,0:T(8,128)(2,1)} %param.17) | copy-start | bytes 1572868
  0.6 16.6 %copy-start.2 = (bf16[4,512,256]{2,1,0:T(8,128)(2,1)S(1)}, bf16[4,512,256]{2,1,0:T(8,128)(2,1)}, u32[]{:S(2)}) copy-start(bf16[4,512,256]{2,1,0:T(8,128)(2,1)} %param.9) | copy-start | bytes 3145732
  1.9 15.5 %collective-permute-start.1 = (bf16[4,136,256]{2,1,0:T(8,128)(2,1)S(1)}, bf16[4,136,256]{2,1,0:T(8,128)(2,1)S(1)}, u32[]{:S(2)}, u32[]{:S(2)}) collective-permute-start(bf16[4,136,256]{2,1,0:T(8,128)(2,1)S(1)} %get-tuple-element.77), channel_id=1, source_target_pairs={{1,0},{2,1},{3,2},{4,3},{5,4},{6,5},{7,6},{8,7},{9,8},{10,9},{11,1... | collective-permute-start | bytes 835592 | tf_op jit(solution)/shard_map/ppermute | solution.py:22
  4.4 12.8 %collective-permute-start = (bf16[4,136,256]{2,1,0:T(8,128)(2,1)S(1)}, bf16[4,136,256]{2,1,0:T(8,128)(2,1)S(1)}, u32[]{:S(2)}, u32[]{:S(2)}) collective-permute-start(bf16[4,136,256]{2,1,0:T(8,128)(2,1)S(1)} %get-tuple-element.78), channel_id=1, source_target_pairs={{0,1},{1,2},{2,3},{3,4},{4,5},{5,6},{6,7},{7,8},{8,9},{9,10},{10,1... | collective-permute-start | bytes 835592 | tf_op jit(solution)/shard_map/ppermute | solution.py:19
  17.2 1.3 copy-start.5
  27.3 0.8 copy-start.6
  28.2 4.3 %copy-start.7 = (f32[4,512]{1,0:T(4,128)S(1)}, f32[4,512]{1,0:T(4,128)}, u32[]{:S(2)}) copy-start(f32[4,512]{1,0:T(4,128)} %param.15) | copy-start | bytes 24580
  28.6 15.9 %collective-permute-start.2 = (f32[256,128]{1,0:T(8,128)S(1)}, f32[256,128]{1,0:T(8,128)S(1)}, u32[]{:S(2)}, u32[]{:S(2)}) collective-permute-start(f32[256,128]{1,0:T(8,128)S(1)} %convolution_bitcast_fusion.1), channel_id=1, source_target_pairs={{0,128},{128,0},{1,129},{129,1},{2,130},{130,2},{3,131},{131,3},{4... | collective-permute-start | bytes 393224 | tf_op jit(solution)/shard_map/ppermute | solution.py:71
  44.6 8.8 %collective-permute-start.3 = (f32[256,128]{1,0:T(8,128)S(1)}, f32[256,128]{1,0:T(8,128)S(1)}, u32[]{:S(2)}, u32[]{:S(2)}) collective-permute-start(f32[256,128]{1,0:T(8,128)S(1)} %add.1017), channel_id=1, source_target_pairs={{0,256},{256,0},{1,257},{257,1},{2,258},{258,2},{3,259},{259,3},{4... | collective-permute-start | bytes 393224 | tf_op jit(solution)/shard_map/ppermute | solution.py:71
  74.4 0.7 copy-start.3
  82.2 0.7 copy-start.4
  107.9 24.6 %copy-start.1 = (bf16[4,512,128]{2,1,0:T(8,128)(2,1)S(1)}, bf16[4,512,128]{2,1,0:T(8,128)(2,1)}, u32[]{:S(2)}) copy-start(bf16[4,512,128]{2,1,0:T(8,128)(2,1)} %param.17) | copy-start | bytes 1572868

commit v12 on v11

--- a/solution.py
+++ b/solution.py
@@ -86,7 +86,14 @@
     width = totals[0].shape[0]
     for axis in axes:
         digit = lax.axis_index(axis)
-        slots = lax.all_gather(jnp.concatenate((grad,) + tuple(totals)), axis)
+        packed = jnp.concatenate((grad,) + tuple(totals))
+        if axis in ("z2", "z3"):
+            other = lax.ppermute(packed, axis, [(0, 1), (1, 0)])
+            low = jnp.where(digit == 0, packed, other)
+            high = jnp.where(digit == 0, other, packed)
+            slots = jnp.stack([low, high])
+        else:
+            slots = lax.all_gather(packed, axis)
         radix = slots.shape[0]
         grad = slots[0, :rows]
         for j in range(1, radix):

time: 133 us -> 135 us (1.015)
  blocking collectives: 71 us -> 27.6 us
  waiting for transfers between devices: 3.37 us -> 27.6 us
  starting transfers between devices: 13.5 us -> 33.6 us
    all_gather x7 -> x5, blocking collectives: 71 us -> 27.6 us  [scan_and_sum(): slots = lax.all_gather(packed, axis)]
    ppermute x0 -> x2, waiting for transfers between devices: none -> 24.2 us  [scan_and_sum(): other = lax.ppermute(packed, axis, [(0, 1), (1, 0)])]
    ppermute x0 -> x2, starting transfers between devices: none -> 20.1 us  [scan_and_sum(): other = lax.ppermute(packed, axis, [(0, 1), (1, 0)])]
    concatenate x7, local copies, waits for them, and re-layouts: 0.32 us -> 2.13 us  [scan_and_sum(): packed = jnp.concatenate((grad,) + tuple(totals))]
    add x7, other arithmetic: 0.76 us -> 2.17 us  [scan_and_sum(): grad = grad + slots[j, :rows]]
    unnamed x18 -> x16, local copies, waits for them, and re-layouts: 2.91 us -> 1.58 us
  transfers between devices with their start and end apart: 4 -> 6, of which waited for: 1 -> 3; matrix products, arithmetic and copies ran while one was open for 13% -> 13% of each run, Pallas kernels for 0% -> 0%
where the time goes in v12:
time: 135 us; the launch traced here: 134 us
  starting transfers between devices  33.6 us (25%)
  waiting for transfers between devices  27.6 us (20%)
  blocking collectives  27.6 us (20%)
  other arithmetic  18.5 us (14%)
  local copies, waits for them, and re-layouts  10.9 us (8%)
  matrix products  9.26 us (7%)
  between operations  6.9 us (5%)
    all_gather x5, blocking collectives, scan_and_sum(): slots = lax.all_gather(packed, axis)  27.6 us
    ppermute x2, waiting for transfers between devices, scan_and_sum(): other = lax.ppermute(packed, axis, [(0, 1), (1, 0)])  24.2 us
    ppermute x2, starting transfers between devices, scan_and_sum(): other = lax.ppermute(packed, axis, [(0, 1), (1, 0)])  20.1 us
    add x9, other arithmetic, combine(): new_c = a_two * a_two * c_one / denom + c_two  9.63 us
    dot_general x9, matrix products, conv_layer(): jnp.einsum('tfw,wv->tfv', piece, weights[tap], preferred_element_type=jnp...  8.3 us
    ppermute x2, starting transfers between devices, pair_sum(): return value + lax.ppermute(value, axis, [(0, 1), (1, 0)])  7.91 us
    ppermute x2, waiting for transfers between devices, pair_sum(): return value + lax.ppermute(value, axis, [(0, 1), (1, 0)])  3.4 us
    ppermute x1, starting transfers between devices, extended_2(): lax.ppermute(lax.slice_in_dim(block, block.shape[dim] - width, None, axis...  3.02 us
  transfers between devices with their start and end apart: 6, of which 3 were waited for; matrix products, arithmetic and copies ran while one was open for 13% of the time, Pallas kernels for 0%

profile of v12, /device:TPU:3, one launch (start us, length us, event | category | flops | bytes accessed | tf_op | source)
XLA Modules:
  0.0 134.4 jit_solution(11946964052330758263)
XLA Ops:
  0.7 1.2 fusion.169
  1.9 2.6 %collective-permute-start.1 = (bf16[4,136,256]{2,1,0:T(8,128)(2,1)S(1)}, bf16[4,136,256]{2,1,0:T(8,128)(2,1)S(1)}, u32[]{:S(2)}, u32[]{:S(2)}) collective-permute-start(bf16[4,136,256]{2,1,0:T(8,128)(2,1)S(1)} %get-tuple-element.77), channel_id=1, source_target_pairs={{1,0},{2,1},{3,2},{4,3},{5,4},{6,5},{7,6},{8,7},{9,8},{10,9},{11,1... | collective-permute-start | bytes 835592 | tf_op jit(solution)/shard_map/ppermute | solution.py:22
  4.4 3.0 %collective-permute-start = (bf16[4,136,256]{2,1,0:T(8,128)(2,1)S(1)}, bf16[4,136,256]{2,1,0:T(8,128)(2,1)S(1)}, u32[]{:S(2)}, u32[]{:S(2)}) collective-permute-start(bf16[4,136,256]{2,1,0:T(8,128)(2,1)S(1)} %get-tuple-element.78), channel_id=1, source_target_pairs={{0,1},{1,2},{2,3},{3,4},{4,5},{5,6},{6,7},{7,8},{8,9},{9,10},{10,1... | collective-permute-start | bytes 835592 | tf_op jit(solution)/shard_map/ppermute | solution.py:19
  9.1 1.4 %fusion.171 = (s32[1]{0:T(128)}, s32[1]{0:T(128)}, s32[1]{0:T(128)}) fusion(s32[3]{0:T(128)} %param.12), kind=kLoop, calls=%fused_computation.403 | loop fusion | bytes 24 | tf_op jit(solution)/shard_map/slice | solution.py:169
  17.2 1.1 copy-done.4
  19.5 2.0 %broadcast_select_fusion.1 = bf16[4,784,256]{2,1,0:T(8,128)(2,1)S(1)} fusion(pred[784]{0:T(1024)(128)(4,1)S(1)} %fusion.71, f32[256]{0:T(256)S(1)} %bitcast.699, s32[]{:T(128)S(6)} %select_n.496, bf16[4,784,256]{2,1,0:T(8,128)(2,1)S(1)} %constant_dynamic-update-slice_fusion, f32[4,784,256]{2,1,0:T(8,128)S(1)} %fusion.3, f32[4,784,256]{2,1,0:T(8,128)S(1)} %fusion.56, ...), kind=kOutput, calls=%fused_computation.21 | convolution fusion | flops 419872768 | bytes 11372548 | tf_op jit(solution)/shard_map/tfw,wv->tfv/dot_general | solution.py:138
  22.7 1.7 %broadcast_select_fusion = bf16[4,784,256]{2,1,0:T(8,128)(2,1)S(1)} fusion(pred[784]{0:T(1024)(128)(4,1)S(1)} %fusion.71, f32[256]{0:T(256)S(1)} %bitcast.698, f32[4,784,256]{2,1,0:T(8,128)S(1)} %fusion.6, f32[4,784,256]{2,1,0:T(8,128)S(1)} %fusion.5, bf16[4,784,256]{2,1,0:T(8,128)(2,1)S(1)} %broadcast_select_fusion.1, ...), kind=kOutput, calls=%fused_computation.20 | convolution fusion | flops 419872768 | bytes 11372544 | tf_op jit(solution)/shard_map/tfw,wv->tfv/dot_general | solution.py:138
  25.6 1.0 negate_exponential_fusion
  28.4 3.4 %collective-permute-start.2 = (f32[256,128]{1,0:T(8,128)S(1)}, f32[256,128]{1,0:T(8,128)S(1)}, u32[]{:S(2)}, u32[]{:S(2)}) collective-permute-start(f32[256,128]{1,0:T(8,128)S(1)} %convolution_bitcast_fusion.1), channel_id=1, source_target_pairs={{0,128},{128,0},{1,129},{129,1},{2,130},{130,2},{3,131},{131,3},{4... | collective-permute-start | bytes 393224 | tf_op jit(solution)/shard_map/ppermute | solution.py:71
  32.3 0.8 divide_add_fusion.14
  33.1 1.1 divide_add_fusion.13
  34.3 1.3 divide_add_fusion.12
  35.6 1.3 divide_add_fusion.11
  36.9 1.3 divide_add_fusion.10
  38.2 1.3 divide_add_fusion.9
  39.5 1.3 divide_add_fusion.8
  40.8 1.2 fusion.20
  44.4 4.5 %collective-permute-start.3 = (f32[256,128]{1,0:T(8,128)S(1)}, f32[256,128]{1,0:T(8,128)S(1)}, u32[]{:S(2)}, u32[]{:S(2)}) collective-permute-start(f32[256,128]{1,0:T(8,128)S(1)} %add.1017), channel_id=1, source_target_pairs={{0,256},{256,0},{1,257},{257,1},{2,258},{258,2},{3,259},{259,3},{4... | collective-permute-start | bytes 393224 | tf_op jit(solution)/shard_map/ppermute | solution.py:71
  49.8 3.4 %collective-permute-done.3 = f32[256,128]{1,0:T(8,128)S(1)} collective-permute-done((f32[256,128]{1,0:T(8,128)S(1)}, f32[256,128]{1,0:T(8,128)S(1)}, u32[]{:S(2)}, u32[]{:S(2)}) %collective-permute-start.3) | collective-permute-done | bytes 131104 | tf_op jit(solution)/shard_map/ppermute | solution.py:71
  53.3 2.1 %all-gather.5 = f32[2,266,128]{2,1,0:T(8,128)S(1)} all-gather(f32[1,266,128]{2,1,0:T(8,128)S(1)} %bitcast.692), channel_id=2, replica_groups=mesh['th'=2,'tl'=2,'z3'=2,'z2'=2,'z1'=2,'z0'=2,'xh'=2,'xl'=2,'core'=2] {..., dimensions={0}, use_global_device_ids=true | all-gather | bytes 408576 | tf_op jit(solution)/shard_map/all_gather | solution.py:96
  55.5 7.5 %all-gather.6 = f32[2,266,128]{2,1,0:T(8,128)S(1)} all-gather(f32[1,266,128]{2,1,0:T(8,128)S(1)} %bitcast.693), channel_id=3, replica_groups=mesh['th'=2,'tl'=2,'z3'=2,'z2'=2,'z1'=2,'z0'=2,'xh'=2,'xl'=2,'core'=2] {..., dimensions={0}, use_global_device_ids=true | all-gather | bytes 408576 | tf_op jit(solution)/shard_map/all_gather | solution.py:96
  63.2 6.4 %all-gather.7 = f32[2,266,128]{2,1,0:T(8,128)S(1)} all-gather(f32[1,266,128]{2,1,0:T(8,128)S(1)} %bitcast.694), channel_id=4, replica_groups=mesh['th'=2,'tl'=2,'z3'=2,'z2'=2,'z1'=2,'z0'=2,'xh'=2,'xl'=2,'core'=2] {..., dimensions={0}, use_global_device_ids=true | all-gather | bytes 408576 | tf_op jit(solution)/shard_map/all_gather | solution.py:96
  69.7 4.6 %all-gather.8 = f32[2,266,128]{2,1,0:T(8,128)S(1)} all-gather(f32[1,266,128]{2,1,0:T(8,128)S(1)} %bitcast.695), channel_id=5, replica_groups=mesh['th'=2,'tl'=2,'z3'=2,'z2'=2,'z1'=2,'z0'=2,'xh'=2,'xl'=2,'core'=2] {..., dimensions={0}, use_global_device_ids=true | all-gather | bytes 408576 | tf_op jit(solution)/shard_map/all_gather | solution.py:96
  75.0 1.0 concatenate.209
  76.0 7.0 %all-gather.9 = f32[2,266,128]{2,1,0:T(8,128)S(1)} all-gather(f32[1,266,128]{2,1,0:T(8,128)S(1)} %bitcast.696), channel_id=6, replica_groups=mesh['th'=2,'tl'=2,'z3'=2,'z2'=2,'z1'=2,'z0'=2,'xh'=2,'xl'=2,'core'=2] {..., dimensions={0}, use_global_device_ids=true | all-gather | bytes 408576 | tf_op jit(solution)/shard_map/all_gather | solution.py:96
  84.9 0.8 broadcast_select_fusion.13
  86.1 0.9 concatenate.210
  87.1 8.9 %collective-permute-start.4 = (f32[266,128]{1,0:T(8,128)S(1)}, f32[266,128]{1,0:T(8,128)S(1)}, u32[]{:S(2)}, u32[]{:S(2)}) collective-permute-start(f32[266,128]{1,0:T(8,128)S(1)} %concatenate.210), channel_id=1, source_target_pairs={{0,32},{32,0},{1,33},{33,1},{2,34},{34,2},{3,35},{35,3},{4,36},{36... | collective-permute-start | bytes 408584 | tf_op jit(solution)/shard_map/ppermute | solution.py:91
  96.5 12.6 %collective-permute-done.4 = f32[266,128]{1,0:T(8,128)S(1)} collective-permute-done((f32[266,128]{1,0:T(8,128)S(1)}, f32[266,128]{1,0:T(8,128)S(1)}, u32[]{:S(2)}, u32[]{:S(2)}) %collective-permute-start.4) | collective-permute-done | bytes 136224 | tf_op jit(solution)/shard_map/ppermute | solution.py:91
  109.2 11.2 %collective-permute-start.5 = (f32[266,128]{1,0:T(8,128)S(1)}, f32[266,128]{1,0:T(8,128)S(1)}, u32[]{:S(2)}, u32[]{:S(2)}) collective-permute-start(f32[266,128]{1,0:T(8,128)S(1)} %concatenate.211), channel_id=1, source_target_pairs={{0,64},{64,0},{1,65},{65,1},{2,66},{66,2},{3,67},{67,3},{4,68},{68... | collective-permute-start | bytes 408584 | tf_op jit(solution)/shard_map/ppermute | solution.py:91
  120.8 11.6 %collective-permute-done.5 = f32[266,128]{1,0:T(8,128)S(1)} collective-permute-done((f32[266,128]{1,0:T(8,128)S(1)}, f32[266,128]{1,0:T(8,128)S(1)}, u32[]{:S(2)}, u32[]{:S(2)}) %collective-permute-start.5) | collective-permute-done | bytes 136224 | tf_op jit(solution)/shard_map/ppermute | solution.py:91
  133.4 1.0 divide_add_fusion
  (124 shorter events, 16.9 us)
Async XLA Ops:
  0.6 26.5 %copy-start = (bf16[4,512,128]{2,1,0:T(8,128)(2,1)S(1)}, bf16[4,512,128]{2,1,0:T(8,128)(2,1)}, u32[]{:S(2)}) copy-start(bf16[4,512,128]{2,1,0:T(8,128)(2,1)} %param.17) | copy-start | bytes 1572868
  0.6 16.4 %copy-start.2 = (bf16[4,512,256]{2,1,0:T(8,128)(2,1)S(1)}, bf16[4,512,256]{2,1,0:T(8,128)(2,1)}, u32[]{:S(2)}) copy-start(bf16[4,512,256]{2,1,0:T(8,128)(2,1)} %param.9) | copy-start | bytes 3145732
  1.9 15.3 %collective-permute-start.1 = (bf16[4,136,256]{2,1,0:T(8,128)(2,1)S(1)}, bf16[4,136,256]{2,1,0:T(8,128)(2,1)S(1)}, u32[]{:S(2)}, u32[]{:S(2)}) collective-permute-start(bf16[4,136,256]{2,1,0:T(8,128)(2,1)S(1)} %get-tuple-element.77), channel_id=1, source_target_pairs={{1,0},{2,1},{3,2},{4,3},{5,4},{6,5},{7,6},{8,7},{9,8},{10,9},{11,1... | collective-permute-start | bytes 835592 | tf_op jit(solution)/shard_map/ppermute | solution.py:22
  4.4 12.6 %collective-permute-start = (bf16[4,136,256]{2,1,0:T(8,128)(2,1)S(1)}, bf16[4,136,256]{2,1,0:T(8,128)(2,1)S(1)}, u32[]{:S(2)}, u32[]{:S(2)}) collective-permute-start(bf16[4,136,256]{2,1,0:T(8,128)(2,1)S(1)} %get-tuple-element.78), channel_id=1, source_target_pairs={{0,1},{1,2},{2,3},{3,4},{4,5},{5,6},{6,7},{7,8},{8,9},{9,10},{10,1... | collective-permute-start | bytes 835592 | tf_op jit(solution)/shard_map/ppermute | solution.py:19
  17.0 1.3 copy-start.4
  27.1 0.8 copy-start.5
  28.0 4.3 %copy-start.6 = (f32[4,512]{1,0:T(4,128)S(1)}, f32[4,512]{1,0:T(4,128)}, u32[]{:S(2)}) copy-start(f32[4,512]{1,0:T(4,128)} %param.15) | copy-start | bytes 24580
  28.4 16.0 %collective-permute-start.2 = (f32[256,128]{1,0:T(8,128)S(1)}, f32[256,128]{1,0:T(8,128)S(1)}, u32[]{:S(2)}, u32[]{:S(2)}) collective-permute-start(f32[256,128]{1,0:T(8,128)S(1)} %convolution_bitcast_fusion.1), channel_id=1, source_target_pairs={{0,128},{128,0},{1,129},{129,1},{2,130},{130,2},{3,131},{131,3},{4... | collective-permute-start | bytes 393224 | tf_op jit(solution)/shard_map/ppermute | solution.py:71
  44.4 8.8 %collective-permute-start.3 = (f32[256,128]{1,0:T(8,128)S(1)}, f32[256,128]{1,0:T(8,128)S(1)}, u32[]{:S(2)}, u32[]{:S(2)}) collective-permute-start(f32[256,128]{1,0:T(8,128)S(1)} %add.1017), channel_id=1, source_target_pairs={{0,256},{256,0},{1,257},{257,1},{2,258},{258,2},{3,259},{259,3},{4... | collective-permute-start | bytes 393224 | tf_op jit(solution)/shard_map/ppermute | solution.py:71
  74.3 1.7 %copy-start.3 = (f32[2,266,128]{2,1,0:T(8,128)}, f32[2,266,128]{2,1,0:T(8,128)S(1)}, u32[]{:S(2)}) copy-start(f32[2,266,128]{2,1,0:T(8,128)S(1)} %all-gather.8) | copy-start | bytes 817156
  87.1 22.0 %collective-permute-start.4 = (f32[266,128]{1,0:T(8,128)S(1)}, f32[266,128]{1,0:T(8,128)S(1)}, u32[]{:S(2)}, u32[]{:S(2)}) collective-permute-start(f32[266,128]{1,0:T(8,128)S(1)} %concatenate.210), channel_id=1, source_target_pairs={{0,32},{32,0},{1,33},{33,1},{2,34},{34,2},{3,35},{35,3},{4,36},{36... | collective-permute-start | bytes 408584 | tf_op jit(solution)/shard_map/ppermute | solution.py:91
  109.2 23.2 %collective-permute-start.5 = (f32[266,128]{1,0:T(8,128)S(1)}, f32[266,128]{1,0:T(8,128)S(1)}, u32[]{:S(2)}, u32[]{:S(2)}) collective-permute-start(f32[266,128]{1,0:T(8,128)S(1)} %concatenate.211), channel_id=1, source_target_pairs={{0,64},{64,0},{1,65},{65,1},{2,66},{66,2},{3,67},{67,3},{4,68},{68... | collective-permute-start | bytes 408584 | tf_op jit(solution)/shard_map/ppermute | solution.py:91
  132.4 2.0 %copy-start.1 = (bf16[4,512,128]{2,1,0:T(8,128)(2,1)S(1)}, bf16[4,512,128]{2,1,0:T(8,128)(2,1)}, u32[]{:S(2)}) copy-start(bf16[4,512,128]{2,1,0:T(8,128)(2,1)} %param.17) | copy-start | bytes 1572868

commit v13 on v11

--- a/solution.py
+++ b/solution.py
@@ -6,7 +6,7 @@
 STATE = 64
 LAYERS = 3
 DMAX = 64
-HALO = 136
+HALO = LAYERS * DMAX
 TIME = ("z3", "z2", "z1", "z0", "xh", "xl", "core")
 TAKE = ("th", "tl")
 
@@ -154,14 +154,12 @@
     halo = HALO
     hidden = extended_2(hidden, ((TIME, 1),), halo)
     count = lax.axis_size(TIME)
-    spots = position * block_len - halo + jnp.arange(block_len + 2 * halo, dtype=jnp.int32)
-    inside = ((spots >= 0) & (spots < count * block_len))[None, :, None]
-    pad = ((0, 0), (DMAX, DMAX), (0, 0))
     for layer in range(LAYERS):
-        extended = jnp.pad(hidden, pad)
-        hidden = conv_layer(extended, conv_weight[layer], conv_bias[layer], dilations[layer])
+        hidden = conv_layer(hidden, conv_weight[layer], conv_bias[layer], dilations[layer])
+        start = position * block_len - halo + (layer + 1) * DMAX
+        spots = start + jnp.arange(hidden.shape[1], dtype=jnp.int32)
+        inside = ((spots >= 0) & (spots < count * block_len))[None, :, None]
         hidden = jnp.where(inside, hidden, jnp.zeros_like(hidden))
-    hidden = hidden[:, halo : halo + block_len]
     head = jnp.einsum("tfw,ws->tsf", hidden, head_weight, preferred_element_type=jnp.float32)
     obs = head[:, :STATE]
     logp = head[:, STATE:]

time: 133 us -> 152 us (1.14)
  the two profiles are of different devices: /device:TPU:3 before, /device:TPU:1 now
where the time goes in v13:
time: 152 us; the launch traced here: 150 us
  blocking collectives  69.1 us (45%)
  local copies, waits for them, and re-layouts  21.8 us (14%)
  other arithmetic  20.9 us (14%)
  starting transfers between devices  13.9 us (9%)
  waiting for transfers between devices  9.05 us (6%)
  matrix products  8.75 us (6%)
  between operations  6.84 us (4%)
    all_gather x7, blocking collectives, scan_and_sum(): slots = lax.all_gather(jnp.concatenate((grad,) + tuple(totals)), axis)  69.1 us
    concatenate x7, local copies, waits for them, and re-layouts, scan_and_sum(): slots = lax.all_gather(jnp.concatenate((grad,) + tuple(totals)), axis)  13.1 us
    add x9, other arithmetic, combine(): new_c = a_two * a_two * c_one / denom + c_two  9.84 us
    ppermute x2, waiting for transfers between devices, pair_sum(): return value + lax.ppermute(value, axis, [(0, 1), (1, 0)])  9.04 us
    dot_general x9, matrix products, conv_layer(): jnp.einsum('tfw,wv->tfv', piece, weights[tap], preferred_element_type=jnp...  7.79 us
    ppermute x1, starting transfers between devices, extended_2(): lax.ppermute(lax.slice_in_dim(block, 0, width, axis=dim), axis, backward)  5.56 us
    ppermute x1, starting transfers between devices, extended_2(): lax.ppermute(lax.slice_in_dim(block, block.shape[dim] - width, None, axis...  4.5 us
    ppermute x2, starting transfers between devices, pair_sum(): return value + lax.ppermute(value, axis, [(0, 1), (1, 0)])  3.84 us
  transfers between devices with their start and end apart: 4, of which 2 were waited for; matrix products, arithmetic and copies ran while one was open for 4% of the time, Pallas kernels for 0%

profile of v13, /device:TPU:1, one launch (start us, length us, event | category | flops | bytes accessed | tf_op | source)
XLA Modules:
  0.0 150.4 jit_solution(7153591590039770496)
XLA Ops:
  0.7 1.3 fusion.183
  1.9 4.5 %collective-permute-start = (bf16[4,192,256]{2,1,0:T(8,128)(2,1)S(1)}, bf16[4,192,256]{2,1,0:T(8,128)(2,1)S(1)}, u32[]{:S(2)}, u32[]{:S(2)}) collective-permute-start(bf16[4,192,256]{2,1,0:T(8,128)(2,1)S(1)} %get-tuple-element.78), channel_id=1, source_target_pairs={{0,1},{1,2},{2,3},{3,4},{4,5},{5,6},{6,7},{7,8},{8,9},{9,10},{10,1... | collective-permute-start | bytes 1179656 | tf_op jit(solution)/shard_map/ppermute | solution.py:19
  6.5 5.6 %collective-permute-start.1 = (bf16[4,192,256]{2,1,0:T(8,128)(2,1)S(1)}, bf16[4,192,256]{2,1,0:T(8,128)(2,1)S(1)}, u32[]{:S(2)}, u32[]{:S(2)}) collective-permute-start(bf16[4,192,256]{2,1,0:T(8,128)(2,1)S(1)} %get-tuple-element.77), channel_id=1, source_target_pairs={{1,0},{2,1},{3,2},{4,3},{5,4},{6,5},{7,6},{8,7},{9,8},{10,9},{11,1... | collective-permute-start | bytes 1179656 | tf_op jit(solution)/shard_map/ppermute | solution.py:22
  13.6 1.4 fusion.185
  21.7 1.1 copy-done.5
  23.9 2.0 %broadcast_select_fusion = bf16[4,768,256]{2,1,0:T(8,128)(2,1)S(1)} fusion(pred[768]{0:T(1024)(128)(4,1)S(1)} %fusion.87, f32[256]{0:T(256)S(1)} %bitcast.690, bf16[4,896,256]{2,1,0:T(8,128)(2,1)S(1)} %constant_dynamic-update-slice_fusion, s32[]{:T(128)S(6)} %select_n.476, f32[4,768,256]{2,1,0:T(8,128)S(1)} %fusion.4, f32[4,768,256]{2,1,0:T(8,128)S(1)} %fusion.6, ...), kind=kOutput, calls=%fused_computation.7 | convolution fusion | flops 411303936 | bytes 11143172 | tf_op jit(solution)/shard_map/tfw,wv->tfv/dot_general | solution.py:131
  27.0 1.5 broadcast_select_fusion.1
  29.4 1.2 fusion.17
  32.4 1.1 divide_add_fusion.13
  33.5 1.3 divide_add_fusion.12
  34.8 1.3 divide_add_fusion.11
  36.1 1.3 divide_add_fusion.10
  37.4 1.5 %divide_add_fusion.9 = (f32[4,64,512]{2,1,0:T(8,128)S(1)}, f32[4,64,512]{2,1,0:T(8,128)S(1)}, f32[4,64,512]{2,1,0:T(8,128)S(1)}, f32[4,64,512]{2,1,0:T(8,128)S(1)}, f32[4,64,512]{2,1,0:T(8,128)S(1)}) fusion(f32[4,64,512]{2,1,0:T(8,128)S(1)} %get-tuple-element.34, f32[4,64,480]{2,1,0:T(8,128)S(1)} %bitcast.624, f32[4,64,496]{2,1,0:T(8,128)S(1)} %bitcast.661, ...), kind=kLoop, calls=%fused_computation.95 | loop fusion | flops 3407872 | bytes 10354688 | tf_op jit(solution)/shard_map/add | solution.py:46
  38.9 1.3 divide_add_fusion.8
  40.3 1.2 fusion.35
  42.9 1.9 %collective-permute-start.2 = (f32[256,128]{1,0:T(8,128)S(1)}, f32[256,128]{1,0:T(8,128)S(1)}, u32[]{:S(2)}, u32[]{:S(2)}) collective-permute-start(f32[256,128]{1,0:T(8,128)S(1)} %convolution_bitcast_fusion.1), channel_id=1, source_target_pairs={{0,128},{128,0},{1,129},{129,1},{2,130},{130,2},{3,131},{131,3},{4... | collective-permute-start | bytes 393224 | tf_op jit(solution)/shard_map/ppermute | solution.py:71
  46.3 3.7 %collective-permute-done.2 = f32[256,128]{1,0:T(8,128)S(1)} collective-permute-done((f32[256,128]{1,0:T(8,128)S(1)}, f32[256,128]{1,0:T(8,128)S(1)}, u32[]{:S(2)}, u32[]{:S(2)}) %collective-permute-start.2) | collective-permute-done | bytes 131104 | tf_op jit(solution)/shard_map/ppermute | solution.py:71
  50.0 1.9 %collective-permute-start.3 = (f32[256,128]{1,0:T(8,128)S(1)}, f32[256,128]{1,0:T(8,128)S(1)}, u32[]{:S(2)}, u32[]{:S(2)}) collective-permute-start(f32[256,128]{1,0:T(8,128)S(1)} %add.1046), channel_id=1, source_target_pairs={{0,256},{256,0},{1,257},{257,1},{2,258},{258,2},{3,259},{259,3},{4... | collective-permute-start | bytes 393224 | tf_op jit(solution)/shard_map/ppermute | solution.py:71
  52.7 5.4 %collective-permute-done.3 = f32[256,128]{1,0:T(8,128)S(1)} collective-permute-done((f32[256,128]{1,0:T(8,128)S(1)}, f32[256,128]{1,0:T(8,128)S(1)}, u32[]{:S(2)}, u32[]{:S(2)}) %collective-permute-start.3) | collective-permute-done | bytes 131104 | tf_op jit(solution)/shard_map/ppermute | solution.py:71
  58.2 2.9 %all-gather.7 = f32[2,266,128]{2,1,0:T(8,128)S(1)} all-gather(f32[1,266,128]{2,1,0:T(8,128)S(1)} %bitcast.681), channel_id=2, replica_groups=mesh['th'=2,'tl'=2,'z3'=2,'z2'=2,'z1'=2,'z0'=2,'xh'=2,'xl'=2,'core'=2] {..., dimensions={0}, use_global_device_ids=true | all-gather | bytes 408576 | tf_op jit(solution)/shard_map/all_gather | solution.py:89
  61.1 5.5 %all-gather.8 = f32[2,266,128]{2,1,0:T(8,128)S(1)} all-gather(f32[1,266,128]{2,1,0:T(8,128)S(1)} %bitcast.682), channel_id=3, replica_groups=mesh['th'=2,'tl'=2,'z3'=2,'z2'=2,'z1'=2,'z0'=2,'xh'=2,'xl'=2,'core'=2] {..., dimensions={0}, use_global_device_ids=true | all-gather | bytes 408576 | tf_op jit(solution)/shard_map/all_gather | solution.py:89
  66.7 1.9 %concatenate.207 = f32[266,128]{1,0:T(8,128)} concatenate(f32[256,128]{1,0:T(8,128)S(1)} %fusion.60, f32[2,128]{1,0:T(2,128)S(1)} %get-tuple-element.100, f32[2,128]{1,0:T(2,128)S(1)} %get-tuple-element.99, f32[2,128]{1,0:T(2,128)S(1)} %get-tuple-element.98, f32[2,128]{1,0:T(2,128)S(1)} %get-tuple-element.97, f32[2,128]{1,0:T(2,128)S(1)} %get-tuple-element.10), dimensions={0} | concatenate | bytes 272384 | tf_op jit(solution)/shard_map/concatenate | solution.py:89
  68.6 6.3 %all-gather.9 = f32[2,266,128]{2,1,0:T(8,128)S(1)} all-gather(f32[1,266,128]{2,1,0:T(8,128)} %bitcast.683), channel_id=4, replica_groups=mesh['th'=2,'tl'=2,'z3'=2,'z2'=2,'z1'=2,'z0'=2,'xh'=2,'xl'=2,'core'=2] {..., dimensions={0}, use_global_device_ids=true | all-gather | bytes 408576 | tf_op jit(solution)/shard_map/all_gather | solution.py:89
  75.5 2.8 %concatenate.208 = f32[266,128]{1,0:T(8,128)} concatenate(f32[256,128]{1,0:T(8,128)} %fusion.59, f32[2,128]{1,0:T(2,128)S(1)} %get-tuple-element.96, f32[2,128]{1,0:T(2,128)S(1)} %get-tuple-element.95, f32[2,128]{1,0:T(2,128)S(1)} %get-tuple-element.94, f32[2,128]{1,0:T(2,128)S(1)} %get-tuple-element.93, f32[2,128]{1,0:T(2,128)S(1)} %get-tuple-element.8), dimensions={0} | concatenate | bytes 272384 | tf_op jit(solution)/shard_map/concatenate | solution.py:89
  78.3 4.8 %all-gather.10 = f32[2,266,128]{2,1,0:T(8,128)S(1)} all-gather(f32[1,266,128]{2,1,0:T(8,128)} %bitcast.684), channel_id=5, replica_groups=mesh['th'=2,'tl'=2,'z3'=2,'z2'=2,'z1'=2,'z0'=2,'xh'=2,'xl'=2,'core'=2] {..., dimensions={0}, use_global_device_ids=true | all-gather | bytes 408576 | tf_op jit(solution)/shard_map/all_gather | solution.py:89
  83.9 2.8 %concatenate.209 = f32[266,128]{1,0:T(8,128)} concatenate(f32[256,128]{1,0:T(8,128)} %fusion.58, f32[2,128]{1,0:T(2,128)S(1)} %get-tuple-element.92, f32[2,128]{1,0:T(2,128)S(1)} %get-tuple-element.91, f32[2,128]{1,0:T(2,128)S(1)} %get-tuple-element.90, f32[2,128]{1,0:T(2,128)S(1)} %get-tuple-element.89, f32[2,128]{1,0:T(2,128)S(1)} %get-tuple-element.6), dimensions={0} | concatenate | bytes 272384 | tf_op jit(solution)/shard_map/concatenate | solution.py:89
  86.6 7.1 %all-gather.11 = f32[2,266,128]{2,1,0:T(8,128)S(1)} all-gather(f32[1,266,128]{2,1,0:T(8,128)} %bitcast.685), channel_id=6, replica_groups=mesh['th'=2,'tl'=2,'z3'=2,'z2'=2,'z1'=2,'z0'=2,'xh'=2,'xl'=2,'core'=2] {..., dimensions={0}, use_global_device_ids=true | all-gather | bytes 408576 | tf_op jit(solution)/shard_map/all_gather | solution.py:89
  94.5 2.8 %concatenate.210 = f32[266,128]{1,0:T(8,128)} concatenate(f32[256,128]{1,0:T(8,128)} %fusion.57, f32[2,128]{1,0:T(2,128)S(1)} %get-tuple-element.88, f32[2,128]{1,0:T(2,128)S(1)} %get-tuple-element.87, f32[2,128]{1,0:T(2,128)S(1)} %get-tuple-element.86, f32[2,128]{1,0:T(2,128)S(1)} %get-tuple-element.85, f32[2,128]{1,0:T(2,128)S(1)} %get-tuple-element.4), dimensions={0} | concatenate | bytes 272384 | tf_op jit(solution)/shard_map/concatenate | solution.py:89
  97.3 20.0 %all-gather.12 = f32[2,266,128]{2,1,0:T(8,128)S(1)} all-gather(f32[1,266,128]{2,1,0:T(8,128)} %bitcast.686), channel_id=7, replica_groups=mesh['th'=2,'tl'=2,'z3'=2,'z2'=2,'z1'=2,'z0'=2,'xh'=2,'xl'=2,'core'=2] {..., dimensions={0}, use_global_device_ids=true | all-gather | bytes 408576 | tf_op jit(solution)/shard_map/all_gather | solution.py:89
  118.0 2.8 %concatenate.211 = f32[266,128]{1,0:T(8,128)} concatenate(f32[256,128]{1,0:T(8,128)} %fusion.56, f32[2,128]{1,0:T(2,128)S(1)} %get-tuple-element.84, f32[2,128]{1,0:T(2,128)S(1)} %get-tuple-element.83, f32[2,128]{1,0:T(2,128)S(1)} %get-tuple-element.82, f32[2,128]{1,0:T(2,128)S(1)} %get-tuple-element.81, f32[2,128]{1,0:T(2,128)S(1)} %get-tuple-element.2), dimensions={0} | concatenate | bytes 272384 | tf_op jit(solution)/shard_map/concatenate | solution.py:89
  120.8 22.6 %all-gather.13 = f32[2,266,128]{2,1,0:T(8,128)S(1)} all-gather(f32[1,266,128]{2,1,0:T(8,128)} %bitcast.687), channel_id=8, replica_groups=mesh['th'=2,'tl'=2,'z3'=2,'z2'=2,'z1'=2,'z0'=2,'xh'=2,'xl'=2,'core'=2] {..., dimensions={0}, use_global_device_ids=true | all-gather | bytes 408576 | tf_op jit(solution)/shard_map/all_gather | solution.py:89
  149.3 1.0 divide_add_fusion
  (123 shorter events, 20.0 us)
Async XLA Ops:
  0.6 41.8 %copy-start = (bf16[4,512,128]{2,1,0:T(8,128)(2,1)S(1)}, bf16[4,512,128]{2,1,0:T(8,128)(2,1)}, u32[]{:S(2)}) copy-start(bf16[4,512,128]{2,1,0:T(8,128)(2,1)} %param.17) | copy-start | bytes 1572868
  0.6 20.9 %copy-start.1 = (bf16[4,512,256]{2,1,0:T(8,128)(2,1)S(1)}, bf16[4,512,256]{2,1,0:T(8,128)(2,1)}, u32[]{:S(2)}) copy-start(bf16[4,512,256]{2,1,0:T(8,128)(2,1)} %param.9) | copy-start | bytes 3145732
  1.9 19.5 %collective-permute-start = (bf16[4,192,256]{2,1,0:T(8,128)(2,1)S(1)}, bf16[4,192,256]{2,1,0:T(8,128)(2,1)S(1)}, u32[]{:S(2)}, u32[]{:S(2)}) collective-permute-start(bf16[4,192,256]{2,1,0:T(8,128)(2,1)S(1)} %get-tuple-element.78), channel_id=1, source_target_pairs={{0,1},{1,2},{2,3},{3,4},{4,5},{5,6},{6,7},{7,8},{8,9},{9,10},{10,1... | collective-permute-start | bytes 1179656 | tf_op jit(solution)/shard_map/ppermute | solution.py:19
  6.5 15.2 %collective-permute-start.1 = (bf16[4,192,256]{2,1,0:T(8,128)(2,1)S(1)}, bf16[4,192,256]{2,1,0:T(8,128)(2,1)S(1)}, u32[]{:S(2)}, u32[]{:S(2)}) collective-permute-start(bf16[4,192,256]{2,1,0:T(8,128)(2,1)S(1)} %get-tuple-element.77), channel_id=1, source_target_pairs={{1,0},{2,1},{3,2},{4,3},{5,4},{6,5},{7,6},{8,7},{9,8},{10,9},{11,1... | collective-permute-start | bytes 1179656 | tf_op jit(solution)/shard_map/ppermute | solution.py:22
  21.5 1.3 copy-start.5
  29.4 1.2 copy-start.6
  30.6 0.9 copy-start.7
  42.9 7.1 %collective-permute-start.2 = (f32[256,128]{1,0:T(8,128)S(1)}, f32[256,128]{1,0:T(8,128)S(1)}, u32[]{:S(2)}, u32[]{:S(2)}) collective-permute-start(f32[256,128]{1,0:T(8,128)S(1)} %convolution_bitcast_fusion.1), channel_id=1, source_target_pairs={{0,128},{128,0},{1,129},{129,1},{2,130},{130,2},{3,131},{131,3},{4... | collective-permute-start | bytes 393224 | tf_op jit(solution)/shard_map/ppermute | solution.py:71
  50.0 8.1 %collective-permute-start.3 = (f32[256,128]{1,0:T(8,128)S(1)}, f32[256,128]{1,0:T(8,128)S(1)}, u32[]{:S(2)}, u32[]{:S(2)}) collective-permute-start(f32[256,128]{1,0:T(8,128)S(1)} %add.1046), channel_id=1, source_target_pairs={{0,256},{256,0},{1,257},{257,1},{2,258},{258,2},{3,259},{259,3},{4... | collective-permute-start | bytes 393224 | tf_op jit(solution)/shard_map/ppermute | solution.py:71
  83.1 0.8 copy-start.2
  93.7 0.7 copy-start.3
  117.3 0.8 copy-start.4

commit v14 on v11

--- a/solution.py
+++ b/solution.py
@@ -6,7 +6,7 @@
 STATE = 64
 LAYERS = 3
 DMAX = 64
-HALO = 136
+HALO = 130
 TIME = ("z3", "z2", "z1", "z0", "xh", "xl", "core")
 TAKE = ("th", "tl")
 

time: 133 us -> 137 us (1.030)
  the two profiles are of different devices: /device:TPU:3 before, /device:TPU:1 now
where the time goes in v14:
time: 137 us; the launch traced here: 136 us
  blocking collectives  69.2 us (51%)
  other arithmetic  19.3 us (14%)
  starting transfers between devices  14.5 us (11%)
  local copies, waits for them, and re-layouts  10.7 us (8%)
  matrix products  10.1 us (7%)
  between operations  6.61 us (5%)
  waiting for transfers between devices  5.54 us (4%)
    all_gather x7, blocking collectives, scan_and_sum(): slots = lax.all_gather(jnp.concatenate((grad,) + tuple(totals)), axis)  69.2 us
    add x9, other arithmetic, combine(): new_c = a_two * a_two * c_one / denom + c_two  9.63 us
    dot_general x9, matrix products, conv_layer(): jnp.einsum('tfw,wv->tfv', piece, weights[tap], preferred_element_type=jnp...  9.11 us
    ppermute x1, starting transfers between devices, extended_2(): lax.ppermute(lax.slice_in_dim(block, 0, width, axis=dim), axis, backward)  5.56 us
    ppermute x2, waiting for transfers between devices, pair_sum(): return value + lax.ppermute(value, axis, [(0, 1), (1, 0)])  5.53 us
    ppermute x1, starting transfers between devices, extended_2(): lax.ppermute(lax.slice_in_dim(block, block.shape[dim] - width, None, axis...  4.62 us
    ppermute x2, starting transfers between devices, pair_sum(): return value + lax.ppermute(value, axis, [(0, 1), (1, 0)])  4.28 us
  transfers between devices with their start and end apart: 4, of which 1 were waited for; matrix products, arithmetic and copies ran while one was open for 13% of the time, Pallas kernels for 0%

profile of v14, /device:TPU:1, one launch (start us, length us, event | category | flops | bytes accessed | tf_op | source)
XLA Modules:
  0.0 135.8 jit_solution(3088114826543092808)
XLA Ops:
  0.7 2.0 %fusion.168 = (bf16[4,130,256]{2,1,0:T(8,128)(2,1)}, bf16[4,130,256]{2,1,0:T(8,128)(2,1)}) fusion(bf16[4,512,256]{2,1,0:T(8,128)(2,1)} %param.9), kind=kLoop, calls=%fused_computation.394 | loop fusion | bytes 1064960 | tf_op jit(solution)/shard_map/slice | solution.py:20
  2.7 4.6 %collective-permute-start = (bf16[4,130,256]{2,1,0:T(8,128)(2,1)}, bf16[4,130,256]{2,1,0:T(8,128)(2,1)S(1)}, u32[]{:S(2)}, u32[]{:S(2)}) collective-permute-start(bf16[4,130,256]{2,1,0:T(8,128)(2,1)} %get-tuple-element.77), channel_id=1, source_target_pairs={{0,1},{1,2},{2,3},{3,4},{4,5},{5,6},{6,7},{7,8},{8,9},{9,10},{10,1... | collective-permute-start | bytes 798728 | tf_op jit(solution)/shard_map/ppermute | solution.py:19
  7.3 5.6 %collective-permute-start.1 = (bf16[4,130,256]{2,1,0:T(8,128)(2,1)}, bf16[4,130,256]{2,1,0:T(8,128)(2,1)S(1)}, u32[]{:S(2)}, u32[]{:S(2)}) collective-permute-start(bf16[4,130,256]{2,1,0:T(8,128)(2,1)} %get-tuple-element.78), channel_id=1, source_target_pairs={{1,0},{2,1},{3,2},{4,3},{5,4},{6,5},{7,6},{8,7},{9,8},{10,9},{11,1... | collective-permute-start | bytes 798728 | tf_op jit(solution)/shard_map/ppermute | solution.py:22
  12.9 1.4 %fusion.170 = (s32[1]{0:T(128)}, s32[1]{0:T(128)}, s32[1]{0:T(128)}) fusion(s32[3]{0:T(128)} %param.12), kind=kLoop, calls=%fused_computation.396 | loop fusion | bytes 24 | tf_op jit(solution)/shard_map/slice | solution.py:162
  14.3 0.8 exponential_bitcast_fusion
  21.4 0.8 fusion.169
  23.8 2.2 %broadcast_select_fusion.1 = bf16[4,772,256]{2,1,0:T(8,128)(2,1)S(1)} fusion(pred[772]{0:T(1024)(128)(4,1)S(1)} %fusion.70, f32[256]{0:T(256)S(1)} %bitcast.695, s32[]{:T(128)S(6)} %select_n.474, bf16[4,772,256]{2,1,0:T(8,128)(2,1)S(1)} %pad_maximum_fusion, f32[4,772,256]{2,1,0:T(8,128)S(1)} %fusion.3, f32[4,772,256]{2,1,0:T(8,128)S(1)} %fusion.55, ...), kind=kOutput, calls=%fused_computation.21 | convolution fusion | flops 413446144 | bytes 11249668 | tf_op jit(solution)/shard_map/tfw,wv->tfv/dot_general | solution.py:131
  27.5 1.8 %broadcast_select_fusion = bf16[4,772,256]{2,1,0:T(8,128)(2,1)S(1)} fusion(pred[772]{0:T(1024)(128)(4,1)S(1)} %fusion.70, f32[256]{0:T(256)S(1)} %bitcast.694, f32[4,772,256]{2,1,0:T(8,128)S(1)} %fusion.5, f32[4,772,256]{2,1,0:T(8,128)S(1)} %fusion.4, bf16[4,772,256]{2,1,0:T(8,128)(2,1)S(1)} %broadcast_select_fusion.1, ...), kind=kOutput, calls=%fused_computation.20 | convolution fusion | flops 413446144 | bytes 11249664 | tf_op jit(solution)/shard_map/tfw,wv->tfv/dot_general | solution.py:131
  30.5 1.2 negate_exponential_fusion
  31.7 0.9 broadcast_select_fusion.2
  33.6 2.1 %collective-permute-start.2 = (f32[256,128]{1,0:T(8,128)S(1)}, f32[256,128]{1,0:T(8,128)S(1)}, u32[]{:S(2)}, u32[]{:S(2)}) collective-permute-start(f32[256,128]{1,0:T(8,128)S(1)} %convolution_bitcast_fusion.1), channel_id=1, source_target_pairs={{0,128},{128,0},{1,129},{129,1},{2,130},{130,2},{3,131},{131,3},{4... | collective-permute-start | bytes 393224 | tf_op jit(solution)/shard_map/ppermute | solution.py:71
  36.2 0.8 divide_add_fusion.14
  37.0 1.1 divide_add_fusion.13
  38.2 1.3 divide_add_fusion.12
  39.5 1.3 divide_add_fusion.11
  40.8 1.3 divide_add_fusion.10
  42.1 1.3 divide_add_fusion.9
  43.4 1.3 divide_add_fusion.8
  44.7 1.2 fusion.19
  48.3 2.2 %collective-permute-start.3 = (f32[256,128]{1,0:T(8,128)S(1)}, f32[256,128]{1,0:T(8,128)S(1)}, u32[]{:S(2)}, u32[]{:S(2)}) collective-permute-start(f32[256,128]{1,0:T(8,128)S(1)} %add.1017), channel_id=1, source_target_pairs={{0,256},{256,0},{1,257},{257,1},{2,258},{258,2},{3,259},{259,3},{4... | collective-permute-start | bytes 393224 | tf_op jit(solution)/shard_map/ppermute | solution.py:71
  51.4 5.5 %collective-permute-done.3 = f32[256,128]{1,0:T(8,128)S(1)} collective-permute-done((f32[256,128]{1,0:T(8,128)S(1)}, f32[256,128]{1,0:T(8,128)S(1)}, u32[]{:S(2)}, u32[]{:S(2)}) %collective-permute-start.3) | collective-permute-done | bytes 131104 | tf_op jit(solution)/shard_map/ppermute | solution.py:71
  57.0 2.0 %all-gather.7 = f32[2,266,128]{2,1,0:T(8,128)S(1)} all-gather(f32[1,266,128]{2,1,0:T(8,128)S(1)} %bitcast.686), channel_id=2, replica_groups=mesh['th'=2,'tl'=2,'z3'=2,'z2'=2,'z1'=2,'z0'=2,'xh'=2,'xl'=2,'core'=2] {..., dimensions={0}, use_global_device_ids=true | all-gather | bytes 408576 | tf_op jit(solution)/shard_map/all_gather | solution.py:89
  59.1 5.5 %all-gather.8 = f32[2,266,128]{2,1,0:T(8,128)S(1)} all-gather(f32[1,266,128]{2,1,0:T(8,128)S(1)} %bitcast.687), channel_id=3, replica_groups=mesh['th'=2,'tl'=2,'z3'=2,'z2'=2,'z1'=2,'z0'=2,'xh'=2,'xl'=2,'core'=2] {..., dimensions={0}, use_global_device_ids=true | all-gather | bytes 408576 | tf_op jit(solution)/shard_map/all_gather | solution.py:89
  64.7 6.1 %all-gather.9 = f32[2,266,128]{2,1,0:T(8,128)S(1)} all-gather(f32[1,266,128]{2,1,0:T(8,128)S(1)} %bitcast.688), channel_id=4, replica_groups=mesh['th'=2,'tl'=2,'z3'=2,'z2'=2,'z1'=2,'z0'=2,'xh'=2,'xl'=2,'core'=2] {..., dimensions={0}, use_global_device_ids=true | all-gather | bytes 408576 | tf_op jit(solution)/shard_map/all_gather | solution.py:89
  70.9 4.8 %all-gather.10 = f32[2,266,128]{2,1,0:T(8,128)S(1)} all-gather(f32[1,266,128]{2,1,0:T(8,128)S(1)} %bitcast.689), channel_id=5, replica_groups=mesh['th'=2,'tl'=2,'z3'=2,'z2'=2,'z1'=2,'z0'=2,'xh'=2,'xl'=2,'core'=2] {..., dimensions={0}, use_global_device_ids=true | all-gather | bytes 408576 | tf_op jit(solution)/shard_map/all_gather | solution.py:89
  76.4 7.6 %all-gather.11 = f32[2,266,128]{2,1,0:T(8,128)S(1)} all-gather(f32[1,266,128]{2,1,0:T(8,128)S(1)} %bitcast.690), channel_id=6, replica_groups=mesh['th'=2,'tl'=2,'z3'=2,'z2'=2,'z1'=2,'z0'=2,'xh'=2,'xl'=2,'core'=2] {..., dimensions={0}, use_global_device_ids=true | all-gather | bytes 408576 | tf_op jit(solution)/shard_map/all_gather | solution.py:89
  84.7 20.2 %all-gather.12 = f32[2,266,128]{2,1,0:T(8,128)S(1)} all-gather(f32[1,266,128]{2,1,0:T(8,128)S(1)} %bitcast.691), channel_id=7, replica_groups=mesh['th'=2,'tl'=2,'z3'=2,'z2'=2,'z1'=2,'z0'=2,'xh'=2,'xl'=2,'core'=2] {..., dimensions={0}, use_global_device_ids=true | all-gather | bytes 408576 | tf_op jit(solution)/shard_map/all_gather | solution.py:89
  106.9 0.8 broadcast_select_fusion.13
  108.1 0.8 broadcast_select_fusion.8
  109.8 1.0 concatenate.211
  110.8 23.0 %all-gather.13 = f32[2,266,128]{2,1,0:T(8,128)S(1)} all-gather(f32[1,266,128]{2,1,0:T(8,128)S(1)} %bitcast.692), channel_id=8, replica_groups=mesh['th'=2,'tl'=2,'z3'=2,'z2'=2,'z1'=2,'z0'=2,'xh'=2,'xl'=2,'core'=2] {..., dimensions={0}, use_global_device_ids=true | all-gather | bytes 408576 | tf_op jit(solution)/shard_map/all_gather | solution.py:89
  134.8 1.0 divide_add_fusion
  (120 shorter events, 15.8 us)
Async XLA Ops:
  0.6 32.0 %copy-start = (bf16[4,512,128]{2,1,0:T(8,128)(2,1)S(1)}, bf16[4,512,128]{2,1,0:T(8,128)(2,1)}, u32[]{:S(2)}) copy-start(bf16[4,512,128]{2,1,0:T(8,128)(2,1)} %param.17) | copy-start | bytes 1572868
  0.6 21.5 %copy-start.2 = (bf16[4,512,256]{2,1,0:T(8,128)(2,1)S(1)}, bf16[4,512,256]{2,1,0:T(8,128)(2,1)}, u32[]{:S(2)}) copy-start(bf16[4,512,256]{2,1,0:T(8,128)(2,1)} %param.9) | copy-start | bytes 3145732
  2.7 19.9 %copy-start.5 = (bf16[3,3,256,256]{3,2,1,0:T(8,128)(2,1)S(1)}, bf16[3,3,256,256]{3,2,1,0:T(8,128)(2,1)}, u32[]{:S(2)}) copy-start(bf16[3,3,256,256]{3,2,1,0:T(8,128)(2,1)} %param.10) | copy-start | bytes 3538948
  2.7 19.5 %collective-permute-start = (bf16[4,130,256]{2,1,0:T(8,128)(2,1)}, bf16[4,130,256]{2,1,0:T(8,128)(2,1)S(1)}, u32[]{:S(2)}, u32[]{:S(2)}) collective-permute-start(bf16[4,130,256]{2,1,0:T(8,128)(2,1)} %get-tuple-element.77), channel_id=1, source_target_pairs={{0,1},{1,2},{2,3},{3,4},{4,5},{5,6},{6,7},{7,8},{8,9},{9,10},{10,1... | collective-permute-start | bytes 798728 | tf_op jit(solution)/shard_map/ppermute | solution.py:19
  7.3 14.9 %collective-permute-start.1 = (bf16[4,130,256]{2,1,0:T(8,128)(2,1)}, bf16[4,130,256]{2,1,0:T(8,128)(2,1)S(1)}, u32[]{:S(2)}, u32[]{:S(2)}) collective-permute-start(bf16[4,130,256]{2,1,0:T(8,128)(2,1)} %get-tuple-element.78), channel_id=1, source_target_pairs={{1,0},{2,1},{3,2},{4,3},{5,4},{6,5},{7,6},{8,7},{9,8},{10,9},{11,1... | collective-permute-start | bytes 798728 | tf_op jit(solution)/shard_map/ppermute | solution.py:22
  31.7 1.4 %copy-start.6 = (bf16[256,128]{1,0:T(8,128)(2,1)S(1)}, bf16[256,128]{1,0:T(8,128)(2,1)}, u32[]{:S(2)}) copy-start(bf16[256,128]{1,0:T(8,128)(2,1)} %param.13) | copy-start | bytes 196612
  33.1 3.1 %copy-start.7 = (f32[4,512]{1,0:T(4,128)S(1)}, f32[4,512]{1,0:T(4,128)}, u32[]{:S(2)}) copy-start(f32[4,512]{1,0:T(4,128)} %param.15) | copy-start | bytes 24580
  33.6 14.7 %collective-permute-start.2 = (f32[256,128]{1,0:T(8,128)S(1)}, f32[256,128]{1,0:T(8,128)S(1)}, u32[]{:S(2)}, u32[]{:S(2)}) collective-permute-start(f32[256,128]{1,0:T(8,128)S(1)} %convolution_bitcast_fusion.1), channel_id=1, source_target_pairs={{0,128},{128,0},{1,129},{129,1},{2,130},{130,2},{3,131},{131,3},{4... | collective-permute-start | bytes 393224 | tf_op jit(solution)/shard_map/ppermute | solution.py:71
  48.3 8.6 %collective-permute-start.3 = (f32[256,128]{1,0:T(8,128)S(1)}, f32[256,128]{1,0:T(8,128)S(1)}, u32[]{:S(2)}, u32[]{:S(2)}) collective-permute-start(f32[256,128]{1,0:T(8,128)S(1)} %add.1017), channel_id=1, source_target_pairs={{0,256},{256,0},{1,257},{257,1},{2,258},{258,2},{3,259},{259,3},{4... | collective-permute-start | bytes 393224 | tf_op jit(solution)/shard_map/ppermute | solution.py:71
  75.6 0.7 copy-start.3
  84.0 0.7 copy-start.4
  109.8 26.0 %copy-start.1 = (bf16[4,512,128]{2,1,0:T(8,128)(2,1)S(1)}, bf16[4,512,128]{2,1,0:T(8,128)(2,1)}, u32[]{:S(2)}) copy-start(bf16[4,512,128]{2,1,0:T(8,128)(2,1)} %param.17) | copy-start | bytes 1572868

commit v15 on v14

--- a/solution.py
+++ b/solution.py
@@ -6,7 +6,7 @@
 STATE = 64
 LAYERS = 3
 DMAX = 64
-HALO = 130
+HALO = 144
 TIME = ("z3", "z2", "z1", "z0", "xh", "xl", "core")
 TAKE = ("th", "tl")
 

time: 137 us -> 154 us (1.12)
  local copies, waits for them, and re-layouts: 10.7 us -> 21.9 us
  waiting for transfers between devices: 5.54 us -> 9.74 us
  other arithmetic: 19.3 us -> 21.4 us
    concatenate x7, local copies, waits for them, and re-layouts: 1.28 us -> 13.1 us  [scan_and_sum(): slots = lax.all_gather(jnp.concatenate((grad,) + tuple(totals)), axis)]
    ppermute x2, waiting for transfers between devices: 5.53 us -> 9.73 us  [pair_sum(): return value + lax.ppermute(value, axis, [(0, 1), (1, 0)])]
    add x7, other arithmetic: 1.42 us -> 3.57 us  [scan_and_sum(): grad = grad + slots[j, :rows]]
  transfers between devices with their start and end apart: 4 -> 4, of which waited for: 1 -> 2; matrix products, arithmetic and copies ran while one was open for 13% -> 4% of each run, Pallas kernels for 0% -> 0%
where the time goes in v15:
time: 154 us; the launch traced here: 152 us
  blocking collectives  69.1 us (45%)
  local copies, waits for them, and re-layouts  21.9 us (14%)
  other arithmetic  21.4 us (14%)
  starting transfers between devices  13.9 us (9%)
  waiting for transfers between devices  9.74 us (6%)
  matrix products  9.53 us (6%)
  between operations  6.75 us (4%)
    all_gather x7, blocking collectives, scan_and_sum(): slots = lax.all_gather(jnp.concatenate((grad,) + tuple(totals)), axis)  69.1 us
    concatenate x7, local copies, waits for them, and re-layouts, scan_and_sum(): slots = lax.all_gather(jnp.concatenate((grad,) + tuple(totals)), axis)  13.1 us
    add x9, other arithmetic, combine(): new_c = a_two * a_two * c_one / denom + c_two  9.84 us
    ppermute x2, waiting for transfers between devices, pair_sum(): return value + lax.ppermute(value, axis, [(0, 1), (1, 0)])  9.73 us
    dot_general x9, matrix products, conv_layer(): jnp.einsum('tfw,wv->tfv', piece, weights[tap], preferred_element_type=jnp...  8.57 us
    ppermute x1, starting transfers between devices, extended_2(): lax.ppermute(lax.slice_in_dim(block, 0, width, axis=dim), axis, backward)  5.56 us
    ppermute x1, starting transfers between devices, extended_2(): lax.ppermute(lax.slice_in_dim(block, block.shape[dim] - width, None, axis...  4.5 us
    ppermute x2, starting transfers between devices, pair_sum(): return value + lax.ppermute(value, axis, [(0, 1), (1, 0)])  3.84 us
  transfers between devices with their start and end apart: 4, of which 2 were waited for; matrix products, arithmetic and copies ran while one was open for 4% of the time, Pallas kernels for 0%

profile of v15, /device:TPU:1, one launch (start us, length us, event | category | flops | bytes accessed | tf_op | source)
XLA Modules:
  0.0 152.4 jit_solution(10690082405651163197)
XLA Ops:
  0.7 1.2 fusion.169
  1.9 4.5 %collective-permute-start = (bf16[4,144,256]{2,1,0:T(8,128)(2,1)S(1)}, bf16[4,144,256]{2,1,0:T(8,128)(2,1)S(1)}, u32[]{:S(2)}, u32[]{:S(2)}) collective-permute-start(bf16[4,144,256]{2,1,0:T(8,128)(2,1)S(1)} %get-tuple-element.78), channel_id=1, source_target_pairs={{0,1},{1,2},{2,3},{3,4},{4,5},{5,6},{6,7},{7,8},{8,9},{9,10},{10,1... | collective-permute-start | bytes 884744 | tf_op jit(solution)/shard_map/ppermute | solution.py:19
  6.4 5.6 %collective-permute-start.1 = (bf16[4,144,256]{2,1,0:T(8,128)(2,1)S(1)}, bf16[4,144,256]{2,1,0:T(8,128)(2,1)S(1)}, u32[]{:S(2)}, u32[]{:S(2)}) collective-permute-start(bf16[4,144,256]{2,1,0:T(8,128)(2,1)S(1)} %get-tuple-element.77), channel_id=1, source_target_pairs={{1,0},{2,1},{3,2},{4,3},{5,4},{6,5},{7,6},{8,7},{9,8},{10,9},{11,1... | collective-permute-start | bytes 884744 | tf_op jit(solution)/shard_map/ppermute | solution.py:22
  12.0 1.4 fusion.171
  21.5 1.1 copy-done.5
  23.8 2.0 %broadcast_select_fusion.1 = bf16[4,800,256]{2,1,0:T(8,128)(2,1)S(1)} fusion(pred[800]{0:T(1024)(128)(4,1)S(1)} %fusion.71, f32[256]{0:T(256)S(1)} %bitcast.695, s32[]{:T(128)S(6)} %select_n.474, bf16[4,800,256]{2,1,0:T(8,128)(2,1)S(1)} %constant_dynamic-update-slice_fusion, f32[4,800,256]{2,1,0:T(8,128)S(1)} %fusion.3, f32[4,800,256]{2,1,0:T(8,128)S(1)} %fusion.56, ...), kind=kOutput, calls=%fused_computation.21 | convolution fusion | flops 428441600 | bytes 11601924 | tf_op jit(solution)/shard_map/tfw,wv->tfv/dot_general | solution.py:131
  27.1 1.9 %broadcast_select_fusion = bf16[4,800,256]{2,1,0:T(8,128)(2,1)S(1)} fusion(pred[800]{0:T(1024)(128)(4,1)S(1)} %fusion.71, f32[256]{0:T(256)S(1)} %bitcast.694, f32[4,800,256]{2,1,0:T(8,128)S(1)} %fusion.6, f32[4,800,256]{2,1,0:T(8,128)S(1)} %fusion.5, bf16[4,800,256]{2,1,0:T(8,128)(2,1)S(1)} %broadcast_select_fusion.1, ...), kind=kOutput, calls=%fused_computation.20 | convolution fusion | flops 428441600 | bytes 11601920 | tf_op jit(solution)/shard_map/tfw,wv->tfv/dot_general | solution.py:131
  30.2 1.0 negate_exponential_fusion
  33.9 1.1 divide_add_fusion.13
  35.0 1.3 divide_add_fusion.12
  36.3 1.3 divide_add_fusion.11
  37.6 1.3 divide_add_fusion.10
  38.9 1.3 divide_add_fusion.9
  40.2 1.5 divide_add_fusion.8
  41.8 1.2 fusion.20
  44.9 1.9 %collective-permute-start.2 = (f32[256,128]{1,0:T(8,128)S(1)}, f32[256,128]{1,0:T(8,128)S(1)}, u32[]{:S(2)}, u32[]{:S(2)}) collective-permute-start(f32[256,128]{1,0:T(8,128)S(1)} %convolution_bitcast_fusion.1), channel_id=1, source_target_pairs={{0,128},{128,0},{1,129},{129,1},{2,130},{130,2},{3,131},{131,3},{4... | collective-permute-start | bytes 393224 | tf_op jit(solution)/shard_map/ppermute | solution.py:71
  47.5 4.5 %collective-permute-done.2 = f32[256,128]{1,0:T(8,128)S(1)} collective-permute-done((f32[256,128]{1,0:T(8,128)S(1)}, f32[256,128]{1,0:T(8,128)S(1)}, u32[]{:S(2)}, u32[]{:S(2)}) %collective-permute-start.2) | collective-permute-done | bytes 131104 | tf_op jit(solution)/shard_map/ppermute | solution.py:71
  52.0 1.9 %collective-permute-start.3 = (f32[256,128]{1,0:T(8,128)S(1)}, f32[256,128]{1,0:T(8,128)S(1)}, u32[]{:S(2)}, u32[]{:S(2)}) collective-permute-start(f32[256,128]{1,0:T(8,128)S(1)} %add.1017), channel_id=1, source_target_pairs={{0,256},{256,0},{1,257},{257,1},{2,258},{258,2},{3,259},{259,3},{4... | collective-permute-start | bytes 393224 | tf_op jit(solution)/shard_map/ppermute | solution.py:71
  54.8 5.3 %collective-permute-done.3 = f32[256,128]{1,0:T(8,128)S(1)} collective-permute-done((f32[256,128]{1,0:T(8,128)S(1)}, f32[256,128]{1,0:T(8,128)S(1)}, u32[]{:S(2)}, u32[]{:S(2)}) %collective-permute-start.3) | collective-permute-done | bytes 131104 | tf_op jit(solution)/shard_map/ppermute | solution.py:71
  60.2 2.9 %all-gather.7 = f32[2,266,128]{2,1,0:T(8,128)S(1)} all-gather(f32[1,266,128]{2,1,0:T(8,128)S(1)} %bitcast.686), channel_id=2, replica_groups=mesh['th'=2,'tl'=2,'z3'=2,'z2'=2,'z1'=2,'z0'=2,'xh'=2,'xl'=2,'core'=2] {..., dimensions={0}, use_global_device_ids=true | all-gather | bytes 408576 | tf_op jit(solution)/shard_map/all_gather | solution.py:89
  63.1 5.5 %all-gather.8 = f32[2,266,128]{2,1,0:T(8,128)S(1)} all-gather(f32[1,266,128]{2,1,0:T(8,128)S(1)} %bitcast.687), channel_id=3, replica_groups=mesh['th'=2,'tl'=2,'z3'=2,'z2'=2,'z1'=2,'z0'=2,'xh'=2,'xl'=2,'core'=2] {..., dimensions={0}, use_global_device_ids=true | all-gather | bytes 408576 | tf_op jit(solution)/shard_map/all_gather | solution.py:89
  68.7 1.9 %concatenate.207 = f32[266,128]{1,0:T(8,128)} concatenate(f32[256,128]{1,0:T(8,128)S(1)} %fusion.45, f32[2,128]{1,0:T(2,128)S(1)} %get-tuple-element.100, f32[2,128]{1,0:T(2,128)S(1)} %get-tuple-element.99, f32[2,128]{1,0:T(2,128)S(1)} %get-tuple-element.98, f32[2,128]{1,0:T(2,128)S(1)} %get-tuple-element.97, f32[2,128]{1,0:T(2,128)S(1)} %get-tuple-element.10), dimensions={0} | concatenate | bytes 272384 | tf_op jit(solution)/shard_map/concatenate | solution.py:89
  70.6 6.3 %all-gather.9 = f32[2,266,128]{2,1,0:T(8,128)S(1)} all-gather(f32[1,266,128]{2,1,0:T(8,128)} %bitcast.688), channel_id=4, replica_groups=mesh['th'=2,'tl'=2,'z3'=2,'z2'=2,'z1'=2,'z0'=2,'xh'=2,'xl'=2,'core'=2] {..., dimensions={0}, use_global_device_ids=true | all-gather | bytes 408576 | tf_op jit(solution)/shard_map/all_gather | solution.py:89
  77.5 2.8 %concatenate.208 = f32[266,128]{1,0:T(8,128)} concatenate(f32[256,128]{1,0:T(8,128)} %fusion.44, f32[2,128]{1,0:T(2,128)S(1)} %get-tuple-element.96, f32[2,128]{1,0:T(2,128)S(1)} %get-tuple-element.95, f32[2,128]{1,0:T(2,128)S(1)} %get-tuple-element.94, f32[2,128]{1,0:T(2,128)S(1)} %get-tuple-element.93, f32[2,128]{1,0:T(2,128)S(1)} %get-tuple-element.8), dimensions={0} | concatenate | bytes 272384 | tf_op jit(solution)/shard_map/concatenate | solution.py:89
  80.3 4.8 %all-gather.10 = f32[2,266,128]{2,1,0:T(8,128)S(1)} all-gather(f32[1,266,128]{2,1,0:T(8,128)} %bitcast.689), channel_id=5, replica_groups=mesh['th'=2,'tl'=2,'z3'=2,'z2'=2,'z1'=2,'z0'=2,'xh'=2,'xl'=2,'core'=2] {..., dimensions={0}, use_global_device_ids=true | all-gather | bytes 408576 | tf_op jit(solution)/shard_map/all_gather | solution.py:89
  85.9 2.8 %concatenate.209 = f32[266,128]{1,0:T(8,128)} concatenate(f32[256,128]{1,0:T(8,128)} %fusion.43, f32[2,128]{1,0:T(2,128)S(1)} %get-tuple-element.92, f32[2,128]{1,0:T(2,128)S(1)} %get-tuple-element.91, f32[2,128]{1,0:T(2,128)S(1)} %get-tuple-element.90, f32[2,128]{1,0:T(2,128)S(1)} %get-tuple-element.89, f32[2,128]{1,0:T(2,128)S(1)} %get-tuple-element.6), dimensions={0} | concatenate | bytes 272384 | tf_op jit(solution)/shard_map/concatenate | solution.py:89
  88.6 7.1 %all-gather.11 = f32[2,266,128]{2,1,0:T(8,128)S(1)} all-gather(f32[1,266,128]{2,1,0:T(8,128)} %bitcast.690), channel_id=6, replica_groups=mesh['th'=2,'tl'=2,'z3'=2,'z2'=2,'z1'=2,'z0'=2,'xh'=2,'xl'=2,'core'=2] {..., dimensions={0}, use_global_device_ids=true | all-gather | bytes 408576 | tf_op jit(solution)/shard_map/all_gather | solution.py:89
  96.5 2.8 %concatenate.210 = f32[266,128]{1,0:T(8,128)} concatenate(f32[256,128]{1,0:T(8,128)} %fusion.42, f32[2,128]{1,0:T(2,128)S(1)} %get-tuple-element.88, f32[2,128]{1,0:T(2,128)S(1)} %get-tuple-element.87, f32[2,128]{1,0:T(2,128)S(1)} %get-tuple-element.86, f32[2,128]{1,0:T(2,128)S(1)} %get-tuple-element.85, f32[2,128]{1,0:T(2,128)S(1)} %get-tuple-element.4), dimensions={0} | concatenate | bytes 272384 | tf_op jit(solution)/shard_map/concatenate | solution.py:89
  99.3 20.0 %all-gather.12 = f32[2,266,128]{2,1,0:T(8,128)S(1)} all-gather(f32[1,266,128]{2,1,0:T(8,128)} %bitcast.691), channel_id=7, replica_groups=mesh['th'=2,'tl'=2,'z3'=2,'z2'=2,'z1'=2,'z0'=2,'xh'=2,'xl'=2,'core'=2] {..., dimensions={0}, use_global_device_ids=true | all-gather | bytes 408576 | tf_op jit(solution)/shard_map/all_gather | solution.py:89
  120.0 2.8 %concatenate.211 = f32[266,128]{1,0:T(8,128)} concatenate(f32[256,128]{1,0:T(8,128)} %fusion.41, f32[2,128]{1,0:T(2,128)S(1)} %get-tuple-element.84, f32[2,128]{1,0:T(2,128)S(1)} %get-tuple-element.83, f32[2,128]{1,0:T(2,128)S(1)} %get-tuple-element.82, f32[2,128]{1,0:T(2,128)S(1)} %get-tuple-element.81, f32[2,128]{1,0:T(2,128)S(1)} %get-tuple-element.2), dimensions={0} | concatenate | bytes 272384 | tf_op jit(solution)/shard_map/concatenate | solution.py:89
  122.8 22.6 %all-gather.13 = f32[2,266,128]{2,1,0:T(8,128)S(1)} all-gather(f32[1,266,128]{2,1,0:T(8,128)} %bitcast.692), channel_id=8, replica_groups=mesh['th'=2,'tl'=2,'z3'=2,'z2'=2,'z1'=2,'z0'=2,'xh'=2,'xl'=2,'core'=2] {..., dimensions={0}, use_global_device_ids=true | all-gather | bytes 408576 | tf_op jit(solution)/shard_map/all_gather | solution.py:89
  151.4 1.0 divide_add_fusion
  (122 shorter events, 21.3 us)
Async XLA Ops:
  0.6 43.8 %copy-start = (bf16[4,512,128]{2,1,0:T(8,128)(2,1)S(1)}, bf16[4,512,128]{2,1,0:T(8,128)(2,1)}, u32[]{:S(2)}) copy-start(bf16[4,512,128]{2,1,0:T(8,128)(2,1)} %param.17) | copy-start | bytes 1572868
  0.6 20.8 %copy-start.1 = (bf16[4,512,256]{2,1,0:T(8,128)(2,1)S(1)}, bf16[4,512,256]{2,1,0:T(8,128)(2,1)}, u32[]{:S(2)}) copy-start(bf16[4,512,256]{2,1,0:T(8,128)(2,1)} %param.9) | copy-start | bytes 3145732
  1.9 19.5 %collective-permute-start = (bf16[4,144,256]{2,1,0:T(8,128)(2,1)S(1)}, bf16[4,144,256]{2,1,0:T(8,128)(2,1)S(1)}, u32[]{:S(2)}, u32[]{:S(2)}) collective-permute-start(bf16[4,144,256]{2,1,0:T(8,128)(2,1)S(1)} %get-tuple-element.78), channel_id=1, source_target_pairs={{0,1},{1,2},{2,3},{3,4},{4,5},{5,6},{6,7},{7,8},{8,9},{9,10},{10,1... | collective-permute-start | bytes 884744 | tf_op jit(solution)/shard_map/ppermute | solution.py:19
  6.4 15.1 %collective-permute-start.1 = (bf16[4,144,256]{2,1,0:T(8,128)(2,1)S(1)}, bf16[4,144,256]{2,1,0:T(8,128)(2,1)S(1)}, u32[]{:S(2)}, u32[]{:S(2)}) collective-permute-start(bf16[4,144,256]{2,1,0:T(8,128)(2,1)S(1)} %get-tuple-element.77), channel_id=1, source_target_pairs={{1,0},{2,1},{3,2},{4,3},{5,4},{6,5},{7,6},{8,7},{9,8},{10,9},{11,1... | collective-permute-start | bytes 884744 | tf_op jit(solution)/shard_map/ppermute | solution.py:22
  21.4 1.3 copy-start.5
  31.3 0.8 copy-start.6
  32.1 0.9 copy-start.7
  44.9 7.1 %collective-permute-start.2 = (f32[256,128]{1,0:T(8,128)S(1)}, f32[256,128]{1,0:T(8,128)S(1)}, u32[]{:S(2)}, u32[]{:S(2)}) collective-permute-start(f32[256,128]{1,0:T(8,128)S(1)} %convolution_bitcast_fusion.1), channel_id=1, source_target_pairs={{0,128},{128,0},{1,129},{129,1},{2,130},{130,2},{3,131},{131,3},{4... | collective-permute-start | bytes 393224 | tf_op jit(solution)/shard_map/ppermute | solution.py:71
  52.0 8.1 %collective-permute-start.3 = (f32[256,128]{1,0:T(8,128)S(1)}, f32[256,128]{1,0:T(8,128)S(1)}, u32[]{:S(2)}, u32[]{:S(2)}) collective-permute-start(f32[256,128]{1,0:T(8,128)S(1)} %add.1017), channel_id=1, source_target_pairs={{0,256},{256,0},{1,257},{257,1},{2,258},{258,2},{3,259},{259,3},{4... | collective-permute-start | bytes 393224 | tf_op jit(solution)/shard_map/ppermute | solution.py:71
  85.1 0.8 copy-start.2
  95.8 0.8 copy-start.3
  119.3 0.8 copy-start.4
